TPU v7x, 768 devices: a whole 4x8x12 slice. The times are simulated.
768 devices in a mesh: dom: 16 (over x, z_hi, core), sub: 48 (over z_lo, y).
Axes of the slice: x: 4, y: 8, z: 12 (z_hi: 2, z_lo: 6; z = z_hi * 6 + z_lo), core: 2. Of those that a mesh axis runs over, the one named last changes fastest.
Arguments:
- node_feat: bfloat16 [384, 1152, 128], P('dom', 'sub'), may hold values from -6 to 6
- edge_feat: bfloat16 [786432, 128], P(('dom', 'sub')), may hold values from -6 to 6
- edge_dst: int32 [786432], P(('dom', 'sub')), may hold values from 0 to 575
- edge_dir: int32 [786432], P(('dom', 'sub')), may hold values from 0 to 3, as said below
- edge_count: int32 [768], P(('dom', 'sub')), may hold values from 512 to 1024, as said below
- w_edge_in: bfloat16 [384, 128], P('dom'), may hold values from -0.3125 to 0.3125
- w_edge_out: bfloat16 [128, 128], P('dom'), may hold values from -0.5 to 0.5
- w_node_in: bfloat16 [256, 128], P('dom'), may hold values from -0.375 to 0.375
- w_node_out: bfloat16 [128, 128], P('dom'), may hold values from -0.5 to 0.5
- gains: bfloat16 [2, 128], P(None, 'dom'), may hold values from 0.099609375 to 1.8984375
- node_cot: bfloat16 [384, 1152, 128], P('dom', 'sub'), may hold values from -6 to 6
- edge_cot: bfloat16 [786432, 128], P(('dom', 'sub')), may hold values from -6 to 6
Outputs:
- node_grad: bfloat16 [384, 1152, 128], P('dom', 'sub')
- edge_grad: bfloat16 [786432, 128], P(('dom', 'sub'))
- w_edge_in_grad: float32 [384, 128], P('dom')
- w_edge_out_grad: float32 [128, 128], P('dom')
- w_node_in_grad: float32 [256, 128], P('dom')
- w_node_out_grad: float32 [128, 128], P('dom')
- gain_grad: float32 [2, 128], P(None, 'dom')
Inputs may be any that keep to these rules, and one draw needn't show every extreme that they name: `edge_dir`: the sender lies inside the global grid. A device's live edges are its first edge_count slots; some device is full.
All inputs are finite; a program needn't handle non-finite values.
Results may differ from a plain program's by a relative error of at most 0.033.
The roundings to bfloat16 on the way count: a program that leaves them out, or rounds other values in their place, can miss the bound.
Values may be sent and summed in bfloat16 or wider, within the bound.
No kernel may reach another device: no remote copies, remote signals or barrier semaphores. Data moves between devices by JAX's collectives and lax.ppermute only.
A program may use at most 32 MiB of HBM per device.

v0:
```python
import jax
import jax.numpy as jnp
from jax import lax
from jax.sharding import PartitionSpec as P


def with_halo(block, sides, width):
    for axis, dim in sides:
        count = lax.axis_size(axis)
        forward = [(i, i + 1) for i in range(count - 1)]
        backward = [(target, source) for source, target in forward]
        low = lax.ppermute(
            lax.slice_in_dim(block, block.shape[dim] - width, None, axis=dim), axis, forward
        )
        high = lax.ppermute(lax.slice_in_dim(block, 0, width, axis=dim), axis, backward)
        block = jnp.concatenate([low, block, high], axis=dim)
    return block


def layer_norm(raw_out):
    average = jnp.mean(raw_out, axis=-1, keepdims=True)
    centered = raw_out - average
    inv_std = lax.rsqrt(jnp.mean(centered * centered, axis=-1, keepdims=True) + 1e-05)
    return (centered * inv_std, inv_std)


def norm_back(upstream, normed, inv_std):
    return (
        upstream
        - jnp.mean(upstream, axis=-1, keepdims=True)
        - normed * jnp.mean(upstream * normed, axis=-1, keepdims=True)
    ) * inv_std


def mlp_forward(inputs, w_first, w_second, gain_vec):
    pre_act = jnp.dot(inputs, w_first, preferred_element_type=jnp.float32)
    hidden = jnp.maximum(pre_act, 0.0).astype(jnp.bfloat16)
    raw_out = jnp.dot(hidden, w_second, preferred_element_type=jnp.float32)
    normed, inv_std = layer_norm(raw_out)
    return (pre_act, hidden, normed, inv_std, normed * gain_vec)


def mlp_backward(upstream, inputs, pre_act, hidden, normed, inv_std, gain_vec, w_first, w_second):
    gain_part = jnp.sum(upstream * normed, axis=0)
    grad_raw = norm_back(upstream * gain_vec, normed, inv_std).astype(jnp.bfloat16)
    second_part = jnp.dot(hidden.T, grad_raw, preferred_element_type=jnp.float32)
    grad_hidden = jnp.dot(grad_raw, w_second.T, preferred_element_type=jnp.float32)
    grad_pre = jnp.where(pre_act > 0, grad_hidden, 0.0).astype(jnp.bfloat16)
    first_part = jnp.dot(inputs.T, grad_pre, preferred_element_type=jnp.float32)
    grad_inputs = jnp.dot(grad_pre, w_first.T, preferred_element_type=jnp.float32)
    return (grad_inputs, first_part, second_part, gain_part)


def shards(
    node_feat,
    edge_feat,
    edge_dst,
    edge_dir,
    edge_count,
    w_edge_in,
    w_edge_out,
    w_node_in,
    w_node_out,
    gains,
    node_cot,
    edge_cot,
):
    full_edge_in, full_edge_out, full_node_in, full_node_out, full_gains = (
        lax.all_gather(w_edge_in, "dom", axis=0, tiled=True),
        lax.all_gather(w_edge_out, "dom", axis=0, tiled=True),
        lax.all_gather(w_node_in, "dom", axis=0, tiled=True),
        lax.all_gather(w_node_out, "dom", axis=0, tiled=True),
        lax.all_gather(gains, "dom", axis=1, tiled=True),
    )
    gain_edge = full_gains[0].astype(jnp.float32)
    gain_node = full_gains[1].astype(jnp.float32)
    block_side = node_feat.shape[0]
    latent = node_feat.shape[2]
    padded_side = block_side + 2
    padded = with_halo(node_feat, (("dom", 0), ("sub", 1)), 1).reshape(
        padded_side * padded_side, latent
    )
    node_row = edge_dst // block_side
    node_col = edge_dst % block_side
    step_row = jnp.where(edge_dir == 0, 1, jnp.where(edge_dir == 1, -1, 0)).astype(jnp.int32)
    step_col = jnp.where(edge_dir == 2, 1, jnp.where(edge_dir == 3, -1, 0)).astype(jnp.int32)
    target_pad = (node_row + 1) * padded_side + node_col + 1
    source_pad = (node_row + 1 + step_row) * padded_side + node_col + 1 + step_col
    active = (jnp.arange(edge_dst.shape[0], dtype=jnp.int32) < edge_count[0]).astype(jnp.float32)[
        :, None
    ]
    inputs = jnp.concatenate([edge_feat, padded[source_pad], padded[target_pad]], axis=1)
    pre_e, hidden_e, normed_e, inv_e, message = mlp_forward(
        inputs, full_edge_in, full_edge_out, gain_edge
    )
    aggregate = jax.ops.segment_sum(
        message * active, edge_dst, num_segments=block_side * block_side
    )
    node_rows = node_feat.reshape(block_side * block_side, latent)
    node_input = jnp.concatenate([node_rows, aggregate.astype(jnp.bfloat16)], axis=1)
    pre_n, hidden_n, normed_n, inv_n, _ = mlp_forward(
        node_input, full_node_in, full_node_out, gain_node
    )
    node_upstream = node_cot.reshape(block_side * block_side, latent).astype(jnp.float32)
    node_in_grad, node_first, node_second, node_gain = mlp_backward(
        node_upstream,
        node_input,
        pre_n,
        hidden_n,
        normed_n,
        inv_n,
        gain_node,
        full_node_in,
        full_node_out,
    )
    cot_float = edge_cot.astype(jnp.float32)
    upstream = active * (cot_float + node_in_grad[:, latent:][edge_dst])
    edge_in_grad, edge_first, edge_second, edge_gain = mlp_backward(
        upstream, inputs, pre_e, hidden_e, normed_e, inv_e, gain_edge, full_edge_in, full_edge_out
    )
    edge_grad = (cot_float + edge_in_grad[:, :latent]).astype(jnp.bfloat16)
    spread = jnp.zeros((padded_side * padded_side, latent), jnp.float32)
    spread = (
        spread.at[source_pad]
        .add(edge_in_grad[:, latent : 2 * latent])
        .at[target_pad]
        .add(edge_in_grad[:, 2 * latent :])
    )
    spread = spread.reshape(padded_side, padded_side, latent)
    outgoing = jnp.stack(
        [
            jnp.stack([spread[1:-1, 0], spread[0, 1:-1]]),
            jnp.stack([spread[-1, 1:-1], spread[1:-1, -1]]),
        ]
    )
    incoming = with_halo(outgoing.astype(jnp.bfloat16), (("dom", 0), ("sub", 1)), 1).astype(
        outgoing.dtype
    )
    inner = spread[1:-1, 1:-1]
    inner = inner.at[0].add(incoming[0, 1]).at[-1].add(incoming[3, 2])
    inner = inner.at[:, 0].add(incoming[2, 0]).at[:, -1].add(incoming[1, 3])
    node_total = node_upstream + node_in_grad[:, :latent]
    node_grad = (node_total.reshape(block_side, block_side, latent) + inner).astype(jnp.bfloat16)
    nodes_all = block_side * block_side * lax.axis_size("dom") * lax.axis_size("sub")
    grad_scale = lax.rsqrt(jnp.float32(nodes_all))
    gain_terms = jnp.stack([edge_gain, node_gain]) * grad_scale
    local_terms = (
        edge_first * grad_scale,
        edge_second * grad_scale,
        node_first * grad_scale,
        node_second * grad_scale,
        gain_terms,
    )
    summed = lax.psum(
        (local_terms[0], local_terms[1], local_terms[2], local_terms[3], local_terms[4]), "sub"
    )
    results = (
        lax.psum_scatter(
            summed[0].astype(jnp.bfloat16), "dom", scatter_dimension=0, tiled=True
        ).astype(jnp.float32),
        lax.psum_scatter(
            summed[1].astype(jnp.bfloat16), "dom", scatter_dimension=0, tiled=True
        ).astype(jnp.float32),
        lax.psum_scatter(
            summed[2].astype(jnp.bfloat16), "dom", scatter_dimension=0, tiled=True
        ).astype(jnp.float32),
        lax.psum_scatter(
            summed[3].astype(jnp.bfloat16), "dom", scatter_dimension=0, tiled=True
        ).astype(jnp.float32),
        lax.psum_scatter(
            summed[4].astype(jnp.bfloat16), "dom", scatter_dimension=1, tiled=True
        ).astype(jnp.float32),
    )
    return (node_grad, edge_grad, results[0], results[1], results[2], results[3], results[4])


def solution(mesh):
    in_specs = (
        P("dom", "sub", None),
        P(("dom", "sub"), None),
        P(("dom", "sub")),
        P(("dom", "sub")),
        P(("dom", "sub")),
        P("dom", None),
        P("dom", None),
        P("dom", None),
        P("dom", None),
        P(None, "dom"),
        P("dom", "sub", None),
        P(("dom", "sub"), None),
    )
    out_specs = (
        P("dom", "sub", None),
        P(("dom", "sub"), None),
        P("dom", None),
        P("dom", None),
        P("dom", None),
        P("dom", None),
        P(None, "dom"),
    )
    return jax.shard_map(shards, mesh=mesh, in_specs=in_specs, out_specs=out_specs, check_vma=False)
```

profile of v0, /device:TPU:6, one launch (start us, length us, event | category | flops | bytes accessed | tf_op | source)
XLA Modules:
  0.0 953.3 jit_solution(17308657520514252429)
XLA Ops:
  7.2 0.8 fusion.34
  8.0 14.8 %collective-permute-start.1 = (bf16[1,24,128]{2,1,0:T(8,128)(2,1)S(1)}, bf16[1,24,128]{2,1,0:T(8,128)(2,1)S(1)}, u32[]{:S(2)}, u32[]{:S(2)}) collective-permute-start(bf16[1,24,128]{2,1,0:T(8,128)(2,1)S(1)} %get-tuple-element.101), channel_id=1, source_target_pairs={{48,0},{96,48},{144,96},{192,144},{240,192},{288,240},{336,288},{3... | collective-permute-start | bytes 18440 | tf_op jit(solution)/shard_map/ppermute | solution.py:15
  22.9 1.9 collective-permute-start
  24.8 31.6 %all-gather = bf16[16,8,2]{1,2,0:T(2,128)(2,1)S(1)} all-gather(bf16[1,8,2]{1,2,0:T(2,128)(2,1)} %bitcast.79), channel_id=1, replica_groups=mesh['dom'=16,'sub'=48] {'dom'}, dimensions={0}, use_global_device_ids=true | all-gather | bytes 544 | tf_op jit(solution)/shard_map/all_gather | solution.py:73
  56.4 0.1 reshape.272
  56.5 1.1 fusion.8
  57.6 0.9 bitcast_multiply_fusion.1
  59.2 31.1 %all_gather.18 = bf16[256,128]{1,0:T(8,128)(2,1)S(1)} all-gather(bf16[16,128]{1,0:T(8,128)(2,1)} %param.27), channel_id=1, replica_groups=mesh['dom'=16,'sub'=48] {'dom'}, dimensions={0}, use_global_device_ids=true | all-gather | bytes 69632 | tf_op jit(solution)/shard_map/all_gather | solution.py:71
  90.2 34.5 %all_gather.15 = bf16[384,128]{1,0:T(8,128)(2,1)S(1)} all-gather(bf16[24,128]{1,0:T(8,128)(2,1)} %param.25), channel_id=1, replica_groups=mesh['dom'=16,'sub'=48] {'dom'}, dimensions={0}, use_global_device_ids=true | all-gather | bytes 104448 | tf_op jit(solution)/shard_map/all_gather | solution.py:69
  124.8 1.0 constant_dynamic-update-slice_fusion.5
  125.8 1.3 broadcast_clamp_fusion
  127.1 31.8 %all_gather.16 = bf16[128,128]{1,0:T(8,128)(2,1)S(1)} all-gather(bf16[8,128]{1,0:T(8,128)(2,1)} %param.26), channel_id=1, replica_groups=mesh['dom'=16,'sub'=48] {'dom'}, dimensions={0}, use_global_device_ids=true | all-gather | bytes 34816 | tf_op jit(solution)/shard_map/all_gather | solution.py:70
  159.0 3.5 collective-permute-start.2
  162.5 1.3 collective-permute-start.3
  163.8 34.0 %all_gather.19 = bf16[128,128]{1,0:T(8,128)(2,1)S(1)} all-gather(bf16[8,128]{1,0:T(8,128)(2,1)S(1)} %copy-done.11), channel_id=1, replica_groups=mesh['dom'=16,'sub'=48] {'dom'}, dimensions={0}, use_global_device_ids=true | all-gather | bytes 34816 | tf_op jit(solution)/shard_map/all_gather | solution.py:72
  197.8 0.1 div.36
  197.9 0.1 copy.38
  198.1 0.1 pad_maximum_fusion.1
  198.3 3.2 gather_fusion.1
  201.5 3.2 gather_fusion
  204.8 0.4 fusion.38
  205.2 0.3 fusion.36
  205.6 0.1 multiply_multiply_fusion
  205.7 1.0 copy.37
  206.7 6.5 scatter_custom_fusion
  213.2 0.2 fusion.11
  213.5 0.3 fusion.37
  213.8 0.3 multiply_reduce_fusion.5
  214.1 0.8 fusion.9
  214.8 0.4 multiply_convert_fusion.1
  215.2 0.9 convolution_multiply_fusion.2
  216.1 0.2 fusion.1
  216.3 1.0 convolution_multiply_fusion.1
  217.2 0.2 fusion.39
  217.5 0.8 slice_add_fusion
  218.2 2.8 gather_fusion.2
  221.1 0.2 copy.39
  221.3 0.9 multiply_reduce_fusion
  222.2 0.2 multiply_convert_fusion
  222.4 0.3 convolution_multiply_fusion.3
  222.7 0.3 fusion
  222.9 0.4 convolution_multiply_fusion
  223.4 0.4 fusion.40
  223.8 6.4 scatter_custom_fusion.1
  230.2 6.5 scatter_custom_fusion.2
  236.9 4.8 collective-permute-start.5
  241.7 306.6 %all-reduce.10 = (bf16[384,128]{1,0:T(8,128)(2,1)}, bf16[128,128]{1,0:T(8,128)(2,1)}, bf16[256,128]{1,0:T(8,128)(2,1)}, bf16[128,128]{1,0:T(8,128)(2,1)}, bf16[2,128]{1,0:T(2,128)(2,1)}) all-reduce(f32[384,128]{1,0:T(8,128)S(1)} %convolution_multiply_fusion, ...), channel_id=1, replica_groups=mesh['dom'=16,'sub'=48] {'sub'}, use_global_device_ids=true, to_apply=%region_11.12 | all-reduce | flops 114944 | bytes 689664 | tf_op jit(solution)/shard_map/psum | solution.py:154
  548.4 1.9 collective-permute-start.4
  550.3 1.3 dynamic-slice.28
  552.3 0.2 copy.52
  552.6 8.0 collective-permute-done.4
  560.6 1.3 collective-permute-start.6
  561.9 1.4 collective-permute-start.7
  563.5 0.8 copy.45
  564.4 3.4 collective-permute-done.7
  568.1 0.7 copy.44
  568.8 176.4 %all-reduce.9.cloned.1.call-done = (bf16[128,128]{1,0:T(8,128)(2,1)}, bf16[128,128]{1,0:T(8,128)(2,1)}, bf16[2,128]{1,0:T(2,128)(2,1)}) async-done(((bf16[128,128]{1,0:T(8,128)(2,1)}, bf16[128,128]{1,0:T(8,128)(2,1)}, bf16[2,128]{1,0:T(2,128)(2,1)}), (bf16[128,128]{1,0:T(8,128)(2,1)}, bf16[128,128]{1,0:T(8,128)(2,1)}, bf16[2,128]{1,0:T(2,128)(2,1)})) %all-reduce.9.cloned.1.call-update) | async-done | bytes 66064
  745.3 1.2 dynamic-slice_convert_fusion.1
  746.5 1.3 fusion.24
  747.8 1.3 dynamic-slice_convert_fusion
  749.1 102.9 %reduce-scatter.6.cloned.1.call-done = bf16[16,128]{1,0:T(8,128)(2,1)} async-done(((bf16[256,128]{1,0:T(8,128)(2,1)}), bf16[16,128]{1,0:T(8,128)(2,1)}) %reduce-scatter.6.cloned.1.call-update) | async-done | bytes 4112 | tf_op jit(solution)/shard_map/reduce_scatter | solution.py:164
  851.9 1.3 convert_element_type.104
  853.2 92.3 %reduce-scatter.8.cloned.1.call-done = bf16[24,128]{1,0:T(8,128)(2,1)} async-done(((bf16[384,128]{1,0:T(8,128)(2,1)}), bf16[24,128]{1,0:T(8,128)(2,1)}) %reduce-scatter.8.cloned.1.call-update) | async-done | bytes 6160
  945.5 1.3 convert_element_type.100
  (79 shorter events, 1.2 us)
Async XLA Ops:
  7.2 151.7 %copy-start.2 = (bf16[24,24,128]{2,1,0:T(8,128)(2,1)S(1)}, bf16[24,24,128]{2,1,0:T(8,128)(2,1)}, u32[]{:S(2)}) copy-start(bf16[24,24,128]{2,1,0:T(8,128)(2,1)} %param.20) | copy-start | bytes 442372
  7.2 156.6 %copy-start.11 = (bf16[8,128]{1,0:T(8,128)(2,1)S(1)}, bf16[8,128]{1,0:T(8,128)(2,1)}, u32[]{:S(2)}) copy-start(bf16[8,128]{1,0:T(8,128)(2,1)} %param.28) | copy-start | bytes 6148
  7.2 190.7 %copy-start.5 = (bf16[1024,128]{1,0:T(8,128)(2,1)S(1)}, bf16[1024,128]{1,0:T(8,128)(2,1)}, u32[]{:S(2)}) copy-start(bf16[1024,128]{1,0:T(8,128)(2,1)} %param.31) | copy-start | bytes 786436
  7.2 738.1 %all-reduce.9.cloned.1.call-start = ((), (), s32[]{:S(2)}) async-start(), calls=%async_computation.4 | async-start | bytes 132096
  8.0 150.9 %collective-permute-start.1 = (bf16[1,24,128]{2,1,0:T(8,128)(2,1)S(1)}, bf16[1,24,128]{2,1,0:T(8,128)(2,1)S(1)}, u32[]{:S(2)}, u32[]{:S(2)}) collective-permute-start(bf16[1,24,128]{2,1,0:T(8,128)(2,1)S(1)} %get-tuple-element.101), channel_id=1, source_target_pairs={{48,0},{96,48},{144,96},{192,144},{240,192},{288,240},{336,288},{3... | collective-permute-start | bytes 18440 | tf_op jit(solution)/shard_map/ppermute | solution.py:15
  22.9 136.0 %collective-permute-start = (bf16[1,24,128]{2,1,0:T(8,128)(2,1)S(1)}, bf16[1,24,128]{2,1,0:T(8,128)(2,1)S(1)}, u32[]{:S(2)}, u32[]{:S(2)}) collective-permute-start(bf16[1,24,128]{2,1,0:T(8,128)(2,1)S(1)} %get-tuple-element.102), channel_id=1, source_target_pairs={{0,48},{48,96},{96,144},{144,192},{192,240},{240,288},{288,336},{3... | collective-permute-start | bytes 18440 | tf_op jit(solution)/shard_map/ppermute | solution.py:12
  56.5 149.1 %copy-start.8 = (f32[128]{0:T(128)}, f32[128]{0:T(128)S(1)}, u32[]{:S(2)}) copy-start(f32[128]{0:T(128)S(1)} %get-tuple-element.112) | copy-start | bytes 1540
  158.9 46.3 %copy-start.3 = (bf16[128,128]{1,0:T(8,128)(2,1)}, bf16[128,128]{1,0:T(8,128)(2,1)S(1)}, u32[]{:S(2)}) copy-start(bf16[128,128]{1,0:T(8,128)(2,1)S(1)} %all_gather.16) | copy-start | bytes 98308
  159.0 39.1 %collective-permute-start.2 = (bf16[26,1,128]{2,1,0:T(2,128)(2,1)S(1)}, bf16[26,1,128]{2,1,0:T(2,128)(2,1)S(1)}, u32[]{:S(2)}, u32[]{:S(2)}) collective-permute-start(bf16[26,1,128]{2,1,0:T(2,128)(2,1)S(1)} %get-tuple-element.99), channel_id=1, source_target_pairs={{0,1},{1,2},{2,3},{3,4},{4,5},{5,6},{6,7},{7,8},{8,9},{9,10},{10,1... | collective-permute-start | bytes 19976 | tf_op jit(solution)/shard_map/ppermute | solution.py:12
  162.5 35.6 %collective-permute-start.3 = (bf16[26,1,128]{2,1,0:T(2,128)(2,1)S(1)}, bf16[26,1,128]{2,1,0:T(2,128)(2,1)S(1)}, u32[]{:S(2)}, u32[]{:S(2)}) collective-permute-start(bf16[26,1,128]{2,1,0:T(2,128)(2,1)S(1)} %get-tuple-element.100), channel_id=1, source_target_pairs={{1,0},{2,1},{3,2},{4,3},{5,4},{6,5},{7,6},{8,7},{9,8},{10,9},{11,1... | collective-permute-start | bytes 19976 | tf_op jit(solution)/shard_map/ppermute | solution.py:15
  205.7 8.4 copy-start
  221.1 1.1 copy-start.9
  221.3 1.4 copy-start.4
  223.7 13.1 %copy-start.10 = (f32[128]{0:T(128)S(1)}, f32[128]{0:T(128)}, u32[]{:S(2)}) copy-start(f32[128]{0:T(128)} %get-tuple-element.79) | copy-start | bytes 1540
  223.7 17.9 %copy-start.6 = (f32[128,128]{1,0:T(8,128)S(1)}, f32[128,128]{1,0:T(8,128)}, u32[]{:S(2)}) copy-start(f32[128,128]{1,0:T(8,128)} %convolution_multiply_fusion.2) | copy-start | bytes 196612
  223.8 17.9 %copy-start.7 = (f32[256,128]{1,0:T(8,128)S(1)}, f32[256,128]{1,0:T(8,128)}, u32[]{:S(2)}) copy-start(f32[256,128]{1,0:T(8,128)} %convolution_multiply_fusion.1) | copy-start | bytes 393220
  236.9 315.7 %collective-permute-start.5 = (bf16[1,2,24,128]{3,2,1,0:T(8,128)(2,1)S(1)}, bf16[1,2,24,128]{3,2,1,0:T(8,128)(2,1)S(1)}, u32[]{:S(2)}, u32[]{:S(2)}) collective-permute-start(bf16[1,2,24,128]{3,2,1,0:T(8,128)(2,1)S(1)} %maximum_bitcast_fusion.1), channel_id=1, source_target_pairs={{48,0},{96,48},{144,96},{192,144},{240,192},{288,240},{336,288},{3... | collective-permute-start | bytes 36872 | tf_op jit(solution)/shard_map/ppermute | solution.py:15
  548.3 303.6 %reduce-scatter.6.cloned.1.call-start = ((), (), s32[]{:S(2)}) async-start(), calls=%async_computation.2 | async-start | bytes 69632 | tf_op jit(solution)/shard_map/reduce_scatter | solution.py:164
  548.4 12.2 %collective-permute-start.4 = (bf16[1,2,24,128]{3,2,1,0:T(8,128)(2,1)S(1)}, bf16[1,2,24,128]{3,2,1,0:T(8,128)(2,1)S(1)}, u32[]{:S(2)}, u32[]{:S(2)}) collective-permute-start(bf16[1,2,24,128]{3,2,1,0:T(8,128)(2,1)S(1)} %maximum_bitcast_fusion), channel_id=1, source_target_pairs={{0,48},{48,96},{96,144},{144,192},{192,240},{240,288},{288,336},{3... | collective-permute-start | bytes 36872 | tf_op jit(solution)/shard_map/ppermute | solution.py:12
  552.5 393.0 %reduce-scatter.8.cloned.1.call-start = ((), (), s32[]{:S(2)}) async-start(), calls=%async_computation.3 | async-start | bytes 104448
  560.6 3.8 collective-permute-start.6
  561.9 6.1 copy-start.1
  561.9 5.9 collective-permute-start.7
Sparse Core Ops, SparseCore 0:
  548.4 196.7 all-reduce.8
  751.1 100.8 reduce-scatter.5
  857.9 87.5 reduce-scatter.7
where the time goes:
time: 954 us; the launch traced here: 953 us
  blocking collectives  470 us (49%)
  waiting for transfers between devices  383 us (40%)
  other arithmetic  32.9 us (3%)
  starting transfers between devices  31.1 us (3%)
  local copies, waits for them, and re-layouts  16.2 us (2%)
  between operations  15.8 us (2%)
    psum x1, blocking collectives, shards(): lax.psum((local_terms[0], local_terms[1], local_terms[2], local_terms[3],...  307 us
    unnamed x5, waiting for transfers between devices  269 us
    reduce_scatter x1, waiting for transfers between devices, shards(): lax.psum_scatter(summed[2].astype(jnp.bfloat16), 'dom', scatter_dimension...  103 us
    all_gather x1, blocking collectives, shards(): lax.all_gather(w_edge_in, 'dom', axis=0, tiled=True)  34.5 us
    all_gather x1, blocking collectives, shards(): lax.all_gather(w_node_out, 'dom', axis=0, tiled=True)  34 us
    all_gather x1, blocking collectives, shards(): lax.all_gather(w_edge_out, 'dom', axis=0, tiled=True)  31.8 us
    all_gather x1, blocking collectives, shards(): lax.all_gather(gains, 'dom', axis=1, tiled=True)  31.6 us
    all_gather x1, blocking collectives, shards(): lax.all_gather(w_node_in, 'dom', axis=0, tiled=True)  31.1 us
  transfers between devices with their start and end apart: 11, of which 5 were waited for; matrix products, arithmetic and copies ran while one was open for 1% of the time, Pallas kernels for 0%

commit v1 on v0

--- a/solution.py
+++ b/solution.py
@@ -49,6 +49,46 @@
     first_part = jnp.dot(inputs.T, grad_pre, preferred_element_type=jnp.float32)
     grad_inputs = jnp.dot(grad_pre, w_first.T, preferred_element_type=jnp.float32)
     return (grad_inputs, first_part, second_part, gain_part)
+
+
+def gather_params(weights, gains):
+    latent = weights[0].shape[1]
+    gain_row = gains.reshape(1, -1)
+    gain_row = jnp.pad(gain_row, ((0, 0), (0, latent - gain_row.shape[1])))
+    packed = jnp.concatenate(list(weights) + [gain_row], axis=0)
+    full = lax.all_gather(packed, "dom", axis=0, tiled=False)
+    count = full.shape[0]
+    outs = []
+    start = 0
+    for w in weights:
+        rows = w.shape[0]
+        outs.append(full[:, start : start + rows].reshape(count * rows, latent))
+        start += rows
+    width = gains.shape[1]
+    gain_full = full[:, start, : 2 * width].reshape(count, 2, width)
+    gain_full = jnp.transpose(gain_full, (1, 0, 2)).reshape(2, count * width)
+    outs.append(gain_full)
+    return tuple(outs)
+
+
+def reduce_params(parts, gain_terms, scale):
+    count = lax.axis_size("dom")
+    latent = parts[0].shape[1]
+    blocks = [p.reshape(count, p.shape[0] // count, latent) for p in parts]
+    width = gain_terms.shape[1] // count
+    gain_block = jnp.transpose(gain_terms.reshape(2, count, width), (1, 0, 2)).reshape(count, 1, 2 * width)
+    gain_block = jnp.pad(gain_block, ((0, 0), (0, 0), (0, latent - 2 * width)))
+    packed = jnp.concatenate(blocks + [gain_block], axis=1)
+    shard = lax.psum_scatter(packed, "dom", scatter_dimension=0, tiled=True)[0]
+    shard = lax.psum(shard, "sub") * scale
+    outs = []
+    start = 0
+    for b in blocks:
+        rows = b.shape[1]
+        outs.append(shard[start : start + rows])
+        start += rows
+    outs.append(shard[start, : 2 * width].reshape(2, width))
+    return tuple(outs)
 
 
 def shards(
@@ -65,12 +105,8 @@
     node_cot,
     edge_cot,
 ):
-    full_edge_in, full_edge_out, full_node_in, full_node_out, full_gains = (
-        lax.all_gather(w_edge_in, "dom", axis=0, tiled=True),
-        lax.all_gather(w_edge_out, "dom", axis=0, tiled=True),
-        lax.all_gather(w_node_in, "dom", axis=0, tiled=True),
-        lax.all_gather(w_node_out, "dom", axis=0, tiled=True),
-        lax.all_gather(gains, "dom", axis=1, tiled=True),
+    full_edge_in, full_edge_out, full_node_in, full_node_out, full_gains = gather_params(
+        (w_edge_in, w_edge_out, w_node_in, w_node_out), gains
     )
     gain_edge = full_gains[0].astype(jnp.float32)
     gain_node = full_gains[1].astype(jnp.float32)
@@ -143,35 +179,10 @@
     node_grad = (node_total.reshape(block_side, block_side, latent) + inner).astype(jnp.bfloat16)
     nodes_all = block_side * block_side * lax.axis_size("dom") * lax.axis_size("sub")
     grad_scale = lax.rsqrt(jnp.float32(nodes_all))
-    gain_terms = jnp.stack([edge_gain, node_gain]) * grad_scale
-    local_terms = (
-        edge_first * grad_scale,
-        edge_second * grad_scale,
-        node_first * grad_scale,
-        node_second * grad_scale,
-        gain_terms,
-    )
-    summed = lax.psum(
-        (local_terms[0], local_terms[1], local_terms[2], local_terms[3], local_terms[4]), "sub"
-    )
-    results = (
-        lax.psum_scatter(
-            summed[0].astype(jnp.bfloat16), "dom", scatter_dimension=0, tiled=True
-        ).astype(jnp.float32),
-        lax.psum_scatter(
-            summed[1].astype(jnp.bfloat16), "dom", scatter_dimension=0, tiled=True
-        ).astype(jnp.float32),
-        lax.psum_scatter(
-            summed[2].astype(jnp.bfloat16), "dom", scatter_dimension=0, tiled=True
-        ).astype(jnp.float32),
-        lax.psum_scatter(
-            summed[3].astype(jnp.bfloat16), "dom", scatter_dimension=0, tiled=True
-        ).astype(jnp.float32),
-        lax.psum_scatter(
-            summed[4].astype(jnp.bfloat16), "dom", scatter_dimension=1, tiled=True
-        ).astype(jnp.float32),
-    )
-    return (node_grad, edge_grad, results[0], results[1], results[2], results[3], results[4])
+    results = reduce_params(
+        (edge_first, edge_second, node_first, node_second), jnp.stack([edge_gain, node_gain]), grad_scale
+    )
+    return (node_grad, edge_grad) + results
 
 
 def solution(mesh):

time: 954 us -> 544 us (0.57)
  waiting for transfers between devices: 383 us -> 90.7 us
  blocking collectives: 470 us -> 334 us
  local copies, waits for them, and re-layouts: 16.2 us -> 27 us
    unnamed x5 -> x1, waiting for transfers between devices: 269 us -> 0.02 us
    all_gather x5 -> x1, blocking collectives: 163 us -> 38.2 us  [gather_params(): full = lax.all_gather(packed, 'dom', axis=0, tiled=False)]
    reduce_scatter x1, waiting for transfers between devices: 103 us -> 83.1 us  [reduce_params(): shard = lax.psum_scatter(packed, 'dom', scatter_dimension=0, tiled=True)[0]]
    psum x1, blocking collectives: 307 us -> 296 us  [reduce_params(): shard = lax.psum(shard, 'sub') * scale]
  transfers between devices with their start and end apart: 11 -> 9, of which waited for: 5 -> 3; matrix products, arithmetic and copies ran while one was open for 1% -> 2% of each run, Pallas kernels for 0% -> 0%
where the time goes in v1:
time: 544 us; the launch traced here: 543 us
  blocking collectives  334 us (61%)
  waiting for transfers between devices  90.7 us (17%)
  starting transfers between devices  39.2 us (7%)
  other arithmetic  29.1 us (5%)
  local copies, waits for them, and re-layouts  27 us (5%)
  between operations  15.4 us (3%)
  matrix products  7.77 us (1%)
    psum x1, blocking collectives, reduce_params(): shard = lax.psum(shard, 'sub') * scale  296 us
    reduce_scatter x1, waiting for transfers between devices, reduce_params(): shard = lax.psum_scatter(packed, 'dom', scatter_dimension=0, tiled=True)[0]  83.1 us
    all_gather x1, blocking collectives, gather_params(): full = lax.all_gather(packed, 'dom', axis=0, tiled=False)  38.2 us
    ppermute x4, starting transfers between devices, with_halo(): lax.ppermute(lax.slice_in_dim(block, 0, width, axis=dim), axis, backward)  28.4 us
    scatter-add x2, other arithmetic, shards(): spread = spread.at[source_pad].add(edge_in_grad[:, latent:2 * latent]).at...  14.2 us
  transfers between devices with their start and end apart: 9, of which 3 were waited for; matrix products, arithmetic and copies ran while one was open for 2% of the time, Pallas kernels for 0%

profile of v1, /device:TPU:6, one launch (start us, length us, event | category | flops | bytes accessed | tf_op | source)
XLA Modules:
  0.0 543.3 jit_solution(18210627537771924385)
XLA Ops:
  7.2 0.8 fusion.36
  8.0 1.9 collective-permute-start
  9.9 14.8 %collective-permute-start.1 = (bf16[1,24,128]{2,1,0:T(8,128)(2,1)S(1)}, bf16[1,24,128]{2,1,0:T(8,128)(2,1)S(1)}, u32[]{:S(2)}, u32[]{:S(2)}) collective-permute-start(bf16[1,24,128]{2,1,0:T(8,128)(2,1)S(1)} %get-tuple-element.100), channel_id=1, source_target_pairs={{48,0},{96,48},{144,96},{192,144},{240,192},{288,240},{336,288},{3... | collective-permute-start | bytes 18440 | tf_op jit(solution)/shard_map/ppermute | solution.py:15
  24.8 0.7 constant_dynamic-update-slice_fusion.10
  25.5 0.7 reshape.262
  26.2 0.7 constant_dynamic-update-slice_fusion.9
  26.9 0.7 constant_dynamic-update-slice_fusion.8
  27.6 0.7 constant_dynamic-update-slice_fusion.7
  28.3 38.2 %all-gather.1 = bf16[16,57,128]{2,1,0:T(8,128)(2,1)S(1)} all-gather(bf16[1,57,128]{2,1,0:T(8,128)(2,1)S(1)} %bitcast.93), channel_id=2, replica_groups=mesh['dom'=16,'sub'=48] {'dom'}, dimensions={0}, use_global_device_ids=true | all-gather | bytes 248064 | tf_op jit(solution)/shard_map/all_gather | solution.py:59
  66.8 1.6 bitcast_multiply_fusion.1
  68.4 1.1 fusion.10
  69.5 1.3 broadcast_clamp_fusion
  70.8 1.0 constant_dynamic-update-slice_fusion.5
  72.6 3.5 collective-permute-start.2
  76.1 1.3 collective-permute-start.3
  77.7 0.1 copy.58
  77.9 3.8 collective-permute-done.3
  81.7 0.1 pad_maximum_fusion.1
  81.9 3.2 gather_fusion
  85.1 3.2 gather_fusion.1
  88.5 0.4 fusion.41
  88.8 0.3 fusion.39
  89.2 0.1 multiply_multiply_fusion
  89.3 1.0 copy.56
  90.3 6.5 %scatter_custom_fusion = f32[576,128]{1,0:T(8,128)S(1)} fusion(s32[1024]{0:T(1024)} %param.22, f32[1024,128]{1,0:T(8,128)} %copy.56, f32[]{:T(128)} %constant.150.clone.1), kind=kCustom, calls=%fused_computation.48 | custom fusion | flops 131072 | bytes 295424 | tf_op jit(solution)/shard_map/scatter-add | solution.py:132
  96.9 1.1 fusion.14
  98.0 0.3 fusion.40
  98.4 0.3 multiply_reduce_fusion.5
  98.7 0.8 fusion.11
  99.4 0.4 multiply_convert_fusion.1
  99.8 0.7 copy-done.3
  100.5 0.2 fusion.1
  100.7 0.2 fusion.42
  101.0 0.9 fusion.13
  101.9 0.8 slice_add_fusion
  102.7 2.8 gather_fusion.2
  105.5 0.2 copy.59
  105.7 1.4 multiply_reduce_fusion
  107.1 0.2 multiply_convert_fusion
  107.3 1.0 fusion
  108.4 1.1 fusion.44
  109.5 0.4 fusion.43
  109.8 6.9 %scatter_custom_fusion.1 = f32[676,128]{1,0:T(8,128)} fusion(s32[1024]{0:T(1024)} %get-tuple-element.113, f32[1024,384]{1,0:T(8,128)S(1)} %fusion.43, f32[]{:T(128)} %constant.150.clone.1), kind=kCustom, calls=%fused_computation.20 | custom fusion | flops 131072 | bytes 870912 | tf_op jit(solution)/shard_map/scatter-add | solution.py:161
  116.7 7.3 %scatter_custom_fusion.2 = f32[676,128]{1,0:T(8,128)} fusion(f32[676,128]{1,0:T(8,128)} %scatter_custom_fusion.1, s32[1024]{0:T(1024)} %get-tuple-element.89, f32[1024,384]{1,0:T(8,128)S(1)} %fusion.43), kind=kCustom, calls=%fused_computation.18 | custom fusion | flops 131072 | bytes 870400 | tf_op jit(solution)/shard_map/scatter-add | solution.py:163
  124.0 1.0 reshape.268
  125.2 1.7 constant_dynamic-update-slice_fusion.12
  126.9 0.9 fusion.3
  127.8 0.7 constant_dynamic-update-slice_fusion.11
  128.5 0.9 fusion.2
  129.5 1.9 collective-permute-start.4
  131.5 10.9 %collective-permute-start.5 = (bf16[1,2,24,128]{3,2,1,0:T(8,128)(2,1)S(1)}, bf16[1,2,24,128]{3,2,1,0:T(8,128)(2,1)S(1)}, u32[]{:S(2)}, u32[]{:S(2)}) collective-permute-start(bf16[1,2,24,128]{3,2,1,0:T(8,128)(2,1)S(1)} %maximum_bitcast_fusion.2), channel_id=1, source_target_pairs={{48,0},{96,48},{144,96},{192,144},{240,192},{288,240},{336,288},{3... | collective-permute-start | bytes 36872 | tf_op jit(solution)/shard_map/ppermute | solution.py:15
  142.6 1.5 dynamic-update-slice.16
  144.1 0.2 copy.73
  144.3 3.5 collective-permute-start.6
  147.8 1.4 collective-permute-start.7
  149.4 0.8 copy.67
  150.3 3.7 collective-permute-done.7
  154.4 0.7 copy.66
  155.0 83.1 %reduce-scatter.2.cloned.1.call-done = f32[1,57,128]{2,1,0:T(8,128)} async-done(((f32[16,57,128]{2,1,0:T(8,128)}), f32[1,57,128]{2,1,0:T(8,128)}) %reduce-scatter.2.cloned.1.call-update) | async-done | bytes 29200 | tf_op jit(solution)/shard_map/reduce_scatter | solution.py:82
  238.1 295.9 %psum.7 = f32[57,128]{1,0:T(8,128)S(1)} all-reduce(f32[57,128]{1,0:T(8,128)} %bitcast.92), channel_id=1, replica_groups=mesh['dom'=16,'sub'=48] {'sub'}, use_global_device_ids=true, to_apply=%region_14.15 | all-reduce | flops 7296 | bytes 58368 | tf_op jit(solution)/shard_map/psum | solution.py:83
  534.0 0.6 slice.260
  534.6 0.6 fusion.38
  535.2 0.6 slice.262
  535.9 0.6 reshape_squeeze.7
  (97 shorter events, 2.0 us)
Async XLA Ops:
  7.2 65.3 %copy-start.8 = (bf16[24,24,128]{2,1,0:T(8,128)(2,1)S(1)}, bf16[24,24,128]{2,1,0:T(8,128)(2,1)}, u32[]{:S(2)}) copy-start(bf16[24,24,128]{2,1,0:T(8,128)(2,1)} %param.20) | copy-start | bytes 442372
  7.2 70.5 %copy-start.10 = (bf16[1024,128]{1,0:T(8,128)(2,1)S(1)}, bf16[1024,128]{1,0:T(8,128)(2,1)}, u32[]{:S(2)}) copy-start(bf16[1024,128]{1,0:T(8,128)(2,1)} %param.31) | copy-start | bytes 786436
  7.2 230.9 %reduce-scatter.2.cloned.1.call-start = ((), (), s32[]{:S(2)}) async-start(), calls=%async_computation.1 | async-start | bytes 557056 | tf_op jit(solution)/shard_map/reduce_scatter | solution.py:82
  8.0 64.5 %collective-permute-start = (bf16[1,24,128]{2,1,0:T(8,128)(2,1)S(1)}, bf16[1,24,128]{2,1,0:T(8,128)(2,1)S(1)}, u32[]{:S(2)}, u32[]{:S(2)}) collective-permute-start(bf16[1,24,128]{2,1,0:T(8,128)(2,1)S(1)} %get-tuple-element.101), channel_id=1, source_target_pairs={{0,48},{48,96},{96,144},{144,192},{192,240},{240,288},{288,336},{3... | collective-permute-start | bytes 18440 | tf_op jit(solution)/shard_map/ppermute | solution.py:12
  9.9 62.6 %collective-permute-start.1 = (bf16[1,24,128]{2,1,0:T(8,128)(2,1)S(1)}, bf16[1,24,128]{2,1,0:T(8,128)(2,1)S(1)}, u32[]{:S(2)}, u32[]{:S(2)}) collective-permute-start(bf16[1,24,128]{2,1,0:T(8,128)(2,1)S(1)} %get-tuple-element.100), channel_id=1, source_target_pairs={{48,0},{96,48},{144,96},{192,144},{240,192},{288,240},{336,288},{3... | collective-permute-start | bytes 18440 | tf_op jit(solution)/shard_map/ppermute | solution.py:15
  66.5 33.3 %copy-start.5 = (bf16[16,57,128]{2,1,0:T(8,128)(2,1)}, bf16[16,57,128]{2,1,0:T(8,128)(2,1)S(1)}, u32[]{:S(2)}) copy-start(bf16[16,57,128]{2,1,0:T(8,128)(2,1)S(1)} %all-gather.1) | copy-start | bytes 700420
  72.6 5.3 collective-permute-start.2
  76.1 5.6 %collective-permute-start.3 = (bf16[26,1,128]{2,1,0:T(2,128)(2,1)S(1)}, bf16[26,1,128]{2,1,0:T(2,128)(2,1)S(1)}, u32[]{:S(2)}, u32[]{:S(2)}) collective-permute-start(bf16[26,1,128]{2,1,0:T(2,128)(2,1)S(1)} %get-tuple-element.99), channel_id=1, source_target_pairs={{1,0},{2,1},{3,2},{4,3},{5,4},{6,5},{7,6},{8,7},{9,8},{10,9},{11,1... | collective-permute-start | bytes 19976 | tf_op jit(solution)/shard_map/ppermute | solution.py:15
  77.6 11.6 %copy-start.12 = (f32[128]{0:T(128)}, f32[128]{0:T(128)S(1)}, u32[]{:S(2)}) copy-start(f32[128]{0:T(128)S(1)} %reshape.279) | copy-start | bytes 1540
  89.3 9.3 %copy-start = (bf16[24,24,128]{2,1,0:T(8,128)(2,1)S(1)}, bf16[24,24,128]{2,1,0:T(8,128)(2,1)}, u32[]{:S(2)}) copy-start(bf16[24,24,128]{2,1,0:T(8,128)(2,1)} %param.30) | copy-start | bytes 442372
  90.3 8.3 %copy-start.6 = (f32[576,128]{1,0:T(8,128)S(1)}, f32[576,128]{1,0:T(8,128)}, u32[]{:S(2)}) copy-start(f32[576,128]{1,0:T(8,128)} %bitcast_multiply_fusion.1) | copy-start | bytes 884740
  98.4 2.6 copy-start.9
  99.8 0.7 copy-start.3
  105.5 1.6 copy-start.13
  107.3 1.1 copy-start.1
  116.7 10.1 %copy-start.2 = (bf16[1024,128]{0,1:T(8,128)(2,1)S(1)}, bf16[1024,128]{0,1:T(8,128)(2,1)}, u32[]{:S(2)}) copy-start(bf16[1024,128]{0,1:T(8,128)(2,1)} %copy-done.1) | copy-start | bytes 786436
  124.0 5.3 copy-start.15
  124.0 5.4 copy-start.14
  125.1 2.7 copy-start.11
  125.1 3.4 copy-start.4
  129.5 14.7 %collective-permute-start.4 = (bf16[1,2,24,128]{3,2,1,0:T(8,128)(2,1)S(1)}, bf16[1,2,24,128]{3,2,1,0:T(8,128)(2,1)S(1)}, u32[]{:S(2)}, u32[]{:S(2)}) collective-permute-start(bf16[1,2,24,128]{3,2,1,0:T(8,128)(2,1)S(1)} %maximum_bitcast_fusion.1), channel_id=1, source_target_pairs={{0,48},{48,96},{96,144},{144,192},{192,240},{240,288},{288,336},{3... | collective-permute-start | bytes 36872 | tf_op jit(solution)/shard_map/ppermute | solution.py:12
  131.5 12.8 %collective-permute-start.5 = (bf16[1,2,24,128]{3,2,1,0:T(8,128)(2,1)S(1)}, bf16[1,2,24,128]{3,2,1,0:T(8,128)(2,1)S(1)}, u32[]{:S(2)}, u32[]{:S(2)}) collective-permute-start(bf16[1,2,24,128]{3,2,1,0:T(8,128)(2,1)S(1)} %maximum_bitcast_fusion.2), channel_id=1, source_target_pairs={{48,0},{96,48},{144,96},{192,144},{240,192},{288,240},{336,288},{3... | collective-permute-start | bytes 36872 | tf_op jit(solution)/shard_map/ppermute | solution.py:15
  144.3 6.0 %collective-permute-start.6 = (bf16[4,1,24,128]{3,2,1,0:T(8,128)(2,1)S(1)}, bf16[4,1,24,128]{3,2,1,0:T(8,128)(2,1)S(1)}, u32[]{:S(2)}, u32[]{:S(2)}) collective-permute-start(bf16[4,1,24,128]{3,2,1,0:T(8,128)(2,1)S(1)} %get-tuple-element.104), channel_id=1, source_target_pairs={{0,1},{1,2},{2,3},{3,4},{4,5},{5,6},{6,7},{7,8},{8,9},{9,10},{10,1... | collective-permute-start | bytes 73736 | tf_op jit(solution)/shard_map/ppermute | solution.py:12
  147.8 6.4 %copy-start.7 = (f32[576,128]{1,0:T(8,128)S(1)}, f32[576,128]{1,0:T(8,128)}, u32[]{:S(2)}) copy-start(f32[576,128]{1,0:T(8,128)} %get-tuple-element.92) | copy-start | bytes 884740
  147.8 6.2 %collective-permute-start.7 = (bf16[4,1,24,128]{3,2,1,0:T(8,128)(2,1)S(1)}, bf16[4,1,24,128]{3,2,1,0:T(8,128)(2,1)S(1)}, u32[]{:S(2)}, u32[]{:S(2)}) collective-permute-start(bf16[4,1,24,128]{3,2,1,0:T(8,128)(2,1)S(1)} %get-tuple-element.105), channel_id=1, source_target_pairs={{1,0},{2,1},{3,2},{4,3},{5,4},{6,5},{7,6},{8,7},{9,8},{10,9},{11,1... | collective-permute-start | bytes 73736 | tf_op jit(solution)/shard_map/ppermute | solution.py:15
Sparse Core Ops, SparseCore 0:
  144.2 93.8 reduce-scatter.1

commit v2 on v1

--- a/solution.py
+++ b/solution.py
@@ -51,12 +51,75 @@
     return (grad_inputs, first_part, second_part, gain_part)
 
 
+def exchange(value, axis, mask):
+    count = lax.axis_size(axis)
+    return lax.ppermute(value, axis, [(i, i ^ mask) for i in range(count)])
+
+
+def bit_masks(count):
+    masks = []
+    mask = 1
+    while mask < count:
+        masks.append(mask)
+        mask *= 2
+    return masks
+
+
+def gather_dom(packed):
+    index = lax.axis_index("dom")
+    block = packed
+    for mask in bit_masks(lax.axis_size("dom")):
+        other = exchange(block, "dom", mask)
+        low = (index & mask) == 0
+        block = jnp.where(low, jnp.stack([block, other]), jnp.stack([other, block]))
+    return block.reshape((-1,) + packed.shape)
+
+
+def reduce_scatter_dom(packed):
+    count = lax.axis_size("dom")
+    index = lax.axis_index("dom")
+    masks = bit_masks(count)
+    block = packed.reshape((2,) * len(masks) + packed.shape[1:])
+    for position, mask in enumerate(reversed(masks)):
+        low_half = block[0]
+        high_half = block[1]
+        low = (index & mask) == 0
+        keep = jnp.where(low, low_half, high_half)
+        send = jnp.where(low, high_half, low_half)
+        block = keep + exchange(send, "dom", mask)
+    return block
+
+
+def sum_sub(value):
+    count = lax.axis_size("sub")
+    index = lax.axis_index("sub")
+    total = value
+    mask = 1
+    while count % (2 * mask) == 0:
+        total = total + exchange(total, "sub", mask)
+        mask *= 2
+    rest = count // mask
+    if rest > 1:
+        member = index // mask
+        shifted = [total] + [
+            lax.ppermute(total, "sub", [(i, (i + k * mask) % count) for i in range(count)])
+            for k in range(1, rest)
+        ]
+        stacked = jnp.stack(shifted)
+        ordered = lax.dynamic_index_in_dim(stacked, member % rest, keepdims=False)
+        for source in range(1, rest):
+            pick = (member - source) % rest
+            ordered = ordered + lax.dynamic_index_in_dim(stacked, pick, keepdims=False)
+        total = ordered
+    return total
+
+
 def gather_params(weights, gains):
     latent = weights[0].shape[1]
     gain_row = gains.reshape(1, -1)
     gain_row = jnp.pad(gain_row, ((0, 0), (0, latent - gain_row.shape[1])))
     packed = jnp.concatenate(list(weights) + [gain_row], axis=0)
-    full = lax.all_gather(packed, "dom", axis=0, tiled=False)
+    full = gather_dom(packed)
     count = full.shape[0]
     outs = []
     start = 0
@@ -79,8 +142,8 @@
     gain_block = jnp.transpose(gain_terms.reshape(2, count, width), (1, 0, 2)).reshape(count, 1, 2 * width)
     gain_block = jnp.pad(gain_block, ((0, 0), (0, 0), (0, latent - 2 * width)))
     packed = jnp.concatenate(blocks + [gain_block], axis=1)
-    shard = lax.psum_scatter(packed, "dom", scatter_dimension=0, tiled=True)[0]
-    shard = lax.psum(shard, "sub") * scale
+    shard = reduce_scatter_dom(packed)
+    shard = sum_sub(shard) * scale
     outs = []
     start = 0
     for b in blocks:

time: 544 us -> 199 us (0.37)
  blocking collectives: 334 us -> 0 us
  starting transfers between devices: 39.2 us -> 107 us
  waiting for transfers between devices: 90.7 us -> 29.7 us
  between operations: 15.4 us -> 2.53 us
    psum x1 -> x0, blocking collectives: 296 us -> none  [reduce_params(): shard = lax.psum(shard, 'sub') * scale]
    reduce_scatter x1 -> x0, waiting for transfers between devices: 83.1 us -> none  [reduce_params(): shard = lax.psum_scatter(packed, 'dom', scatter_dimension=0, tiled=True)[0]]
    ppermute x0 -> x14, starting transfers between devices: none -> 66 us  [the longest x12 55 us: exchange(): return lax.ppermute(value, axis, [(i, i ^ mask) for i in range(count)])]
    all_gather x1 -> x0, blocking collectives: 38.2 us -> none  [gather_params(): full = lax.all_gather(packed, 'dom', axis=0, tiled=False)]
    ppermute x0 -> x14, waiting for transfers between devices: none -> 26.6 us  [the longest x12 24.9 us: exchange(): return lax.ppermute(value, axis, [(i, i ^ mask) for i in range(count)])]
  transfers between devices with their start and end apart: 9 -> 22, of which waited for: 3 -> 11; matrix products, arithmetic and copies ran while one was open for 2% -> 14% of each run, Pallas kernels for 0% -> 0%
where the time goes in v2:
time: 199 us; the launch traced here: 197 us
  starting transfers between devices  107 us (54%)
  waiting for transfers between devices  29.7 us (15%)
  other arithmetic  26.7 us (13%)
  local copies, waits for them, and re-layouts  26.2 us (13%)
  matrix products  5.05 us (3%)
  between operations  2.53 us (1%)
    ppermute x12, starting transfers between devices, exchange(): return lax.ppermute(value, axis, [(i, i ^ mask) for i in range(count)])  55 us
    ppermute x4, starting transfers between devices, with_halo(): lax.ppermute(lax.slice_in_dim(block, 0, width, axis=dim), axis, backward)  28.4 us
    ppermute x12, waiting for transfers between devices, exchange(): return lax.ppermute(value, axis, [(i, i ^ mask) for i in range(count)])  24.9 us
    scatter-add x2, other arithmetic, shards(): spread = spread.at[source_pad].add(edge_in_grad[:, latent:2 * latent]).at...  12.8 us
    ppermute x4, starting transfers between devices, with_halo(): lax.ppermute(lax.slice_in_dim(block, block.shape[dim] - width, None, axis...  12.2 us
    ppermute x2, starting transfers between devices, sum_sub(): lax.ppermute(total, 'sub', [(i, (i + k * mask) % count) for i in range(co...  11 us
    unnamed x54, local copies, waits for them, and re-layouts  8.09 us
    scatter-add x1, other arithmetic, shards(): jax.ops.segment_sum(message * active, edge_dst, num_segments=block_side *...  6.53 us
  transfers between devices with their start and end apart: 22, of which 11 were waited for; matrix products, arithmetic and copies ran while one was open for 14% of the time, Pallas kernels for 0%

profile of v2, /device:TPU:6, one launch (start us, length us, event | category | flops | bytes accessed | tf_op | source)
XLA Modules:
  0.0 196.6 jit_solution(9533495261771544659)
XLA Ops:
  0.6 0.7 constant_dynamic-update-slice_fusion.10
  1.3 0.7 reshape.589
  2.1 0.7 constant_dynamic-update-slice_fusion.9
  2.8 0.7 constant_dynamic-update-slice_fusion.8
  3.4 0.7 constant_dynamic-update-slice_fusion.7
  4.1 1.9 collective-permute-start.4
  6.1 0.7 fusion.45
  6.8 2.4 %collective-permute-start = (bf16[1,24,128]{2,1,0:T(8,128)(2,1)S(1)}, bf16[1,24,128]{2,1,0:T(8,128)(2,1)S(1)}, u32[]{:S(2)}, u32[]{:S(2)}) collective-permute-start(bf16[1,24,128]{2,1,0:T(8,128)(2,1)S(1)} %get-tuple-element.98), channel_id=1, source_target_pairs={{0,48},{48,96},{96,144},{144,192},{192,240},{240,288},{288,336},{3... | collective-permute-start | bytes 18440 | tf_op jit(solution)/shard_map/ppermute | solution.py:12
  9.2 15.0 %collective-permute-start.1 = (bf16[1,24,128]{2,1,0:T(8,128)(2,1)S(1)}, bf16[1,24,128]{2,1,0:T(8,128)(2,1)S(1)}, u32[]{:S(2)}, u32[]{:S(2)}) collective-permute-start(bf16[1,24,128]{2,1,0:T(8,128)(2,1)S(1)} %get-tuple-element.97), channel_id=1, source_target_pairs={{48,0},{96,48},{144,96},{192,144},{240,192},{288,240},{336,288},{3... | collective-permute-start | bytes 18440 | tf_op jit(solution)/shard_map/ppermute | solution.py:15
  24.2 1.3 broadcast_clamp_fusion
  25.5 1.0 constant_dynamic-update-slice_fusion.5
  27.2 0.9 constant_dynamic-update-slice_fusion.1
  28.2 3.5 %collective-permute-start.2 = (bf16[26,1,128]{2,1,0:T(2,128)(2,1)S(1)}, bf16[26,1,128]{2,1,0:T(2,128)(2,1)S(1)}, u32[]{:S(2)}, u32[]{:S(2)}) collective-permute-start(bf16[26,1,128]{2,1,0:T(2,128)(2,1)S(1)} %get-tuple-element.95), channel_id=1, source_target_pairs={{0,1},{1,2},{2,3},{3,4},{4,5},{5,6},{6,7},{7,8},{8,9},{9,10},{10,1... | collective-permute-start | bytes 19976 | tf_op jit(solution)/shard_map/ppermute | solution.py:12
  31.7 1.3 collective-permute-start.3
  33.1 1.1 copy.49
  34.2 3.1 %collective-permute-done.3 = bf16[26,1,128]{2,1,0:T(2,128)(2,1)S(1)} collective-permute-done((bf16[26,1,128]{2,1,0:T(2,128)(2,1)S(1)}, bf16[26,1,128]{2,1,0:T(2,128)(2,1)S(1)}, u32[]{:S(2)}, u32[]{:S(2)}) %collective-permute-start.3) | collective-permute-done | bytes 6688 | tf_op jit(solution)/shard_map/ppermute | solution.py:15
  37.5 3.2 %gather_fusion = bf16[1024,128]{1,0:T(8,128)(2,1)S(1)} fusion(bf16[676,128]{1,0:T(8,128)(2,1)S(1)} %reshape.588, s32[1024]{0:T(1024)S(1)} %get-tuple-element.109), kind=kCustom, calls=%fused_computation | custom fusion | bytes 528384 | tf_op jit(solution)/shard_map/gather | solution.py:191
  40.7 3.2 %gather_fusion.1 = bf16[1024,128]{1,0:T(8,128)(2,1)S(1)} fusion(bf16[676,128]{1,0:T(8,128)(2,1)S(1)} %reshape.588, s32[1024]{0:T(1024)S(1)} %get-tuple-element.81), kind=kCustom, calls=%fused_computation.1 | custom fusion | bytes 528384 | tf_op jit(solution)/shard_map/gather | solution.py:191
  44.1 9.6 %collective-permute-start.5 = (bf16[2,57,128]{2,1,0:T(8,128)(2,1)S(1)}, bf16[2,57,128]{2,1,0:T(8,128)(2,1)S(1)}, u32[]{:S(2)}, u32[]{:S(2)}) collective-permute-start(bf16[2,57,128]{2,1,0:T(8,128)(2,1)S(1)} %maximum_select_fusion.6), channel_id=1, source_target_pairs={{0,96},{48,144},{96,0},{144,48},{192,288},{240,336},{288,192},{336... | collective-permute-start | bytes 87560 | tf_op jit(solution)/shard_map/ppermute | solution.py:56
  53.7 2.5 %collective-permute-done.5 = bf16[2,57,128]{2,1,0:T(8,128)(2,1)S(1)} collective-permute-done((bf16[2,57,128]{2,1,0:T(8,128)(2,1)S(1)}, bf16[2,57,128]{2,1,0:T(8,128)(2,1)S(1)}, u32[]{:S(2)}, u32[]{:S(2)}) %collective-permute-start.5) | collective-permute-done | bytes 29216 | tf_op jit(solution)/shard_map/ppermute | solution.py:56
  56.2 2.4 %collective-permute-start.6 = (bf16[2,2,57,128]{3,2,1,0:T(8,128)(2,1)S(1)}, bf16[2,2,57,128]{3,2,1,0:T(8,128)(2,1)S(1)}, u32[]{:S(2)}, u32[]{:S(2)}) collective-permute-start(bf16[2,2,57,128]{3,2,1,0:T(8,128)(2,1)S(1)} %maximum_select_fusion.4), channel_id=1, source_target_pairs={{0,192},{48,240},{96,288},{144,336},{192,0},{240,48},{288,96},{336... | collective-permute-start | bytes 175112 | tf_op jit(solution)/shard_map/ppermute | solution.py:56
  58.7 3.7 %collective-permute-done.6 = bf16[2,2,57,128]{3,2,1,0:T(8,128)(2,1)S(1)} collective-permute-done((bf16[2,2,57,128]{3,2,1,0:T(8,128)(2,1)S(1)}, bf16[2,2,57,128]{3,2,1,0:T(8,128)(2,1)S(1)}, u32[]{:S(2)}, u32[]{:S(2)}) %collective-permute-start.6) | collective-permute-done | bytes 58400 | tf_op jit(solution)/shard_map/ppermute | solution.py:56
  62.4 3.0 %collective-permute-start.7 = (bf16[2,2,2,57,128]{4,3,2,1,0:T(8,128)(2,1)S(1)}, bf16[2,2,2,57,128]{4,3,2,1,0:T(8,128)(2,1)S(1)}, u32[]{:S(2)}, u32[]{:S(2)}) collective-permute-start(bf16[2,2,2,57,128]{4,3,2,1,0:T(8,128)(2,1)S(1)} %maximum_select_fusion.2), channel_id=1, source_target_pairs={{0,384},{48,432},{96,480},{144,528},{192,576},{240,624},{288,672},... | collective-permute-start | bytes 350216 | tf_op jit(solution)/shard_map/ppermute | solution.py:56
  65.5 6.4 %collective-permute-done.7 = bf16[2,2,2,57,128]{4,3,2,1,0:T(8,128)(2,1)S(1)} collective-permute-done((bf16[2,2,2,57,128]{4,3,2,1,0:T(8,128)(2,1)S(1)}, bf16[2,2,2,57,128]{4,3,2,1,0:T(8,128)(2,1)S(1)}, u32[]{:S(2)}, u32[]{:S(2)}) %collective-permute-start.7) | collective-permute-done | bytes 116768 | tf_op jit(solution)/shard_map/ppermute | solution.py:56
  72.5 0.7 bitcast_multiply_fusion.1
  74.4 1.0 copy.45
  75.4 6.5 %scatter_custom_fusion = f32[576,128]{1,0:T(8,128)S(1)} fusion(s32[1024]{0:T(1024)} %param.22, f32[1024,128]{1,0:T(8,128)} %copy.45, f32[]{:T(128)} %constant.190.clone.1), kind=kCustom, calls=%fused_computation.51 | custom fusion | flops 131072 | bytes 295424 | tf_op jit(solution)/shard_map/scatter-add | solution.py:195
  82.0 1.2 fusion.14
  83.8 0.7 fusion.11
  85.6 1.0 fusion.13
  86.5 0.8 slice_add_fusion
  87.3 4.0 %gather_fusion.2 = f32[1024,128]{1,0:T(8,128)} fusion(f32[576,128]{1,0:T(8,128)S(1)} %get-tuple-element.86, s32[1024]{0:T(1024)S(1)} %copy-done.12), kind=kCustom, calls=%fused_computation.2 | custom fusion | bytes 1052672 | tf_op jit(solution)/shard_map/gather | solution.py:216
  91.3 1.2 copy.50
  93.3 0.4 fusion.52
  95.4 0.8 slice_select_fusion
  96.1 2.7 %collective-permute-start.12 = (f32[2,2,2,57,128]{4,3,2,1,0:T(8,128)}, f32[2,2,2,57,128]{4,3,2,1,0:T(8,128)}, u32[]{:S(2)}, u32[]{:S(2)}) collective-permute-start(f32[2,2,2,57,128]{4,3,2,1,0:T(8,128)} %bitcast.36), channel_id=1, source_target_pairs={{0,384},{48,432},{96,480},{144,528},{192,576},{240,624},{288,672},... | collective-permute-start | bytes 700424 | tf_op jit(solution)/shard_map/ppermute | solution.py:56
  98.8 6.3 %scatter_custom_fusion.1 = f32[676,128]{1,0:T(8,128)S(1)} fusion(s32[1024]{0:T(1024)} %get-tuple-element.110, f32[1024,384]{1,0:T(8,128)S(1)} %fusion.51, f32[]{:T(128)} %constant.190.clone.1), kind=kCustom, calls=%fused_computation.20 | custom fusion | flops 131072 | bytes 870912 | tf_op jit(solution)/shard_map/scatter-add | solution.py:224
  105.0 6.5 %scatter_custom_fusion.2 = f32[676,128]{1,0:T(8,128)S(1)} fusion(f32[676,128]{1,0:T(8,128)S(1)} %scatter_custom_fusion.1, s32[1024]{0:T(1024)} %get-tuple-element.82, f32[1024,384]{1,0:T(8,128)S(1)} %fusion.51), kind=kCustom, calls=%fused_computation.18 | custom fusion | flops 131072 | bytes 870400 | tf_op jit(solution)/shard_map/scatter-add | solution.py:226
  111.7 2.1 %collective-permute-start.8 = (bf16[1,2,24,128]{3,2,1,0:T(8,128)(2,1)S(1)}, bf16[1,2,24,128]{3,2,1,0:T(8,128)(2,1)S(1)}, u32[]{:S(2)}, u32[]{:S(2)}) collective-permute-start(bf16[1,2,24,128]{3,2,1,0:T(8,128)(2,1)S(1)} %maximum_bitcast_fusion.1), channel_id=1, source_target_pairs={{0,48},{48,96},{96,144},{144,192},{192,240},{240,288},{288,336},{3... | collective-permute-start | bytes 36872 | tf_op jit(solution)/shard_map/ppermute | solution.py:12
  114.1 1.0 add.199
  115.1 1.9 collective-permute-start.13
  117.2 10.8 %collective-permute-start.9 = (bf16[1,2,24,128]{3,2,1,0:T(8,128)(2,1)S(1)}, bf16[1,2,24,128]{3,2,1,0:T(8,128)(2,1)S(1)}, u32[]{:S(2)}, u32[]{:S(2)}) collective-permute-start(bf16[1,2,24,128]{3,2,1,0:T(8,128)(2,1)S(1)} %maximum_bitcast_fusion.2), channel_id=1, source_target_pairs={{48,0},{96,48},{144,96},{192,144},{240,192},{288,240},{336,288},{3... | collective-permute-start | bytes 36872 | tf_op jit(solution)/shard_map/ppermute | solution.py:15
  128.0 0.8 copy.58
  128.9 8.3 %collective-permute-start.14 = (f32[2,57,128]{2,1,0:T(8,128)S(1)}, f32[2,57,128]{2,1,0:T(8,128)S(1)}, u32[]{:S(2)}, u32[]{:S(2)}) collective-permute-start(f32[2,57,128]{2,1,0:T(8,128)S(1)} %select_bitcast_fusion.1), channel_id=1, source_target_pairs={{0,96},{48,144},{96,0},{144,48},{192,288},{240,336},{288,192},{336... | collective-permute-start | bytes 175112 | tf_op jit(solution)/shard_map/ppermute | solution.py:56
  137.3 4.2 %collective-permute-done.14 = f32[2,57,128]{2,1,0:T(8,128)S(1)} collective-permute-done((f32[2,57,128]{2,1,0:T(8,128)S(1)}, f32[2,57,128]{2,1,0:T(8,128)S(1)}, u32[]{:S(2)}, u32[]{:S(2)}) %collective-permute-start.14) | collective-permute-done | bytes 58400 | tf_op jit(solution)/shard_map/ppermute | solution.py:56
  141.5 1.9 collective-permute-start.15
  143.5 4.2 %collective-permute-start.10 = (bf16[4,1,24,128]{3,2,1,0:T(8,128)(2,1)S(1)}, bf16[4,1,24,128]{3,2,1,0:T(8,128)(2,1)S(1)}, u32[]{:S(2)}, u32[]{:S(2)}) collective-permute-start(bf16[4,1,24,128]{3,2,1,0:T(8,128)(2,1)S(1)} %get-tuple-element.101), channel_id=1, source_target_pairs={{0,1},{1,2},{2,3},{3,4},{4,5},{5,6},{6,7},{7,8},{8,9},{9,10},{10,1... | collective-permute-start | bytes 73736 | tf_op jit(solution)/shard_map/ppermute | solution.py:12
  147.7 1.3 collective-permute-start.11
  149.0 4.8 %collective-permute-start.16 = (f32[57,128]{1,0:T(8,128)S(1)}, f32[57,128]{1,0:T(8,128)S(1)}, u32[]{:S(2)}, u32[]{:S(2)}) collective-permute-start(f32[57,128]{1,0:T(8,128)S(1)} %bitcast_add_fusion.2), channel_id=1, source_target_pairs={{0,1},{1,0},{2,3},{3,2},{4,5},{5,4},{6,7},{7,6},{8,9},{9,8},{10,11... | collective-permute-start | bytes 87560 | tf_op jit(solution)/shard_map/ppermute | solution.py:56
  153.9 1.7 collective-permute-done.16
  155.7 6.7 %collective-permute-start.17 = (f32[57,128]{1,0:T(8,128)S(1)}, f32[57,128]{1,0:T(8,128)S(1)}, u32[]{:S(2)}, u32[]{:S(2)}) collective-permute-start(f32[57,128]{1,0:T(8,128)S(1)} %add.203), channel_id=1, source_target_pairs={{0,2},{1,3},{2,0},{3,1},{4,6},{5,7},{6,4},{7,5},{8,10},{9,11},{10,... | collective-permute-start | bytes 87560 | tf_op jit(solution)/shard_map/ppermute | solution.py:56
  162.4 1.8 collective-permute-done.17
  164.2 6.9 %collective-permute-start.18 = (f32[57,128]{1,0:T(8,128)S(1)}, f32[57,128]{1,0:T(8,128)S(1)}, u32[]{:S(2)}, u32[]{:S(2)}) collective-permute-start(f32[57,128]{1,0:T(8,128)S(1)} %add.204), channel_id=1, source_target_pairs={{0,4},{1,5},{2,6},{3,7},{4,0},{5,1},{6,2},{7,3},{8,12},{9,13},{10,... | collective-permute-start | bytes 87560 | tf_op jit(solution)/shard_map/ppermute | solution.py:56
  171.2 2.8 %collective-permute-done.18 = f32[57,128]{1,0:T(8,128)S(1)} collective-permute-done((f32[57,128]{1,0:T(8,128)S(1)}, f32[57,128]{1,0:T(8,128)S(1)}, u32[]{:S(2)}, u32[]{:S(2)}) %collective-permute-start.18) | collective-permute-done | bytes 29216 | tf_op jit(solution)/shard_map/ppermute | solution.py:56
  173.9 4.9 %collective-permute-start.19 = (f32[57,128]{1,0:T(8,128)S(1)}, f32[57,128]{1,0:T(8,128)S(1)}, u32[]{:S(2)}, u32[]{:S(2)}) collective-permute-start(f32[57,128]{1,0:T(8,128)S(1)} %add.205), channel_id=1, source_target_pairs={{0,8},{1,9},{2,10},{3,11},{4,12},{5,13},{6,14},{7,15},{8,0},{9,1},... | collective-permute-start | bytes 87560 | tf_op jit(solution)/shard_map/ppermute | solution.py:56
  178.8 1.9 collective-permute-done.19
  180.7 5.2 %collective-permute-start.20 = (f32[57,128]{1,0:T(8,128)S(1)}, f32[57,128]{1,0:T(8,128)S(1)}, u32[]{:S(2)}, u32[]{:S(2)}) collective-permute-start(f32[57,128]{1,0:T(8,128)S(1)} %add.206), channel_id=1, source_target_pairs={{0,16},{1,17},{2,18},{3,19},{4,20},{5,21},{6,22},{7,23},{8,24},{9,... | collective-permute-start | bytes 87560 | tf_op jit(solution)/shard_map/ppermute | solution.py:105
  185.9 5.7 %collective-permute-start.21 = (f32[57,128]{1,0:T(8,128)S(1)}, f32[57,128]{1,0:T(8,128)S(1)}, u32[]{:S(2)}, u32[]{:S(2)}) collective-permute-start(f32[57,128]{1,0:T(8,128)S(1)} %add.206), channel_id=1, source_target_pairs={{0,32},{1,33},{2,34},{3,35},{4,36},{5,37},{6,38},{7,39},{8,40},{9,... | collective-permute-start | bytes 87560 | tf_op jit(solution)/shard_map/ppermute | solution.py:105
  191.7 0.7 copy.57
  192.7 1.4 collective-permute-done.21
  194.2 0.6 slice_bitcast_fusion
  194.8 0.6 slice_bitcast_fusion.2
  195.4 0.6 slice_bitcast_fusion.1
  196.0 0.6 reshape_squeeze.7
  (152 shorter events, 7.2 us)
Async XLA Ops:
  4.1 39.9 %collective-permute-start.4 = (bf16[57,128]{1,0:T(8,128)(2,1)S(1)}, bf16[57,128]{1,0:T(8,128)(2,1)S(1)}, u32[]{:S(2)}, u32[]{:S(2)}) collective-permute-start(bf16[57,128]{1,0:T(8,128)(2,1)S(1)} %constant_dynamic-update-slice_fusion.6), channel_id=1, source_target_pairs={{0,48},{48,0},{96,144},{144,96},{192,240},{240,192},{288,336},{336... | collective-permute-start | bytes 43784 | tf_op jit(solution)/shard_map/ppermute | solution.py:56
  6.8 20.4 %collective-permute-start = (bf16[1,24,128]{2,1,0:T(8,128)(2,1)S(1)}, bf16[1,24,128]{2,1,0:T(8,128)(2,1)S(1)}, u32[]{:S(2)}, u32[]{:S(2)}) collective-permute-start(bf16[1,24,128]{2,1,0:T(8,128)(2,1)S(1)} %get-tuple-element.98), channel_id=1, source_target_pairs={{0,48},{48,96},{96,144},{144,192},{192,240},{240,288},{288,336},{3... | collective-permute-start | bytes 18440 | tf_op jit(solution)/shard_map/ppermute | solution.py:12
  9.2 19.0 %collective-permute-start.1 = (bf16[1,24,128]{2,1,0:T(8,128)(2,1)S(1)}, bf16[1,24,128]{2,1,0:T(8,128)(2,1)S(1)}, u32[]{:S(2)}, u32[]{:S(2)}) collective-permute-start(bf16[1,24,128]{2,1,0:T(8,128)(2,1)S(1)} %get-tuple-element.97), channel_id=1, source_target_pairs={{48,0},{96,48},{144,96},{192,144},{240,192},{288,240},{336,288},{3... | collective-permute-start | bytes 18440 | tf_op jit(solution)/shard_map/ppermute | solution.py:15
  28.2 6.0 %collective-permute-start.2 = (bf16[26,1,128]{2,1,0:T(2,128)(2,1)S(1)}, bf16[26,1,128]{2,1,0:T(2,128)(2,1)S(1)}, u32[]{:S(2)}, u32[]{:S(2)}) collective-permute-start(bf16[26,1,128]{2,1,0:T(2,128)(2,1)S(1)} %get-tuple-element.95), channel_id=1, source_target_pairs={{0,1},{1,2},{2,3},{3,4},{4,5},{5,6},{6,7},{7,8},{8,9},{9,10},{10,1... | collective-permute-start | bytes 19976 | tf_op jit(solution)/shard_map/ppermute | solution.py:12
  31.7 5.6 %collective-permute-start.3 = (bf16[26,1,128]{2,1,0:T(2,128)(2,1)S(1)}, bf16[26,1,128]{2,1,0:T(2,128)(2,1)S(1)}, u32[]{:S(2)}, u32[]{:S(2)}) collective-permute-start(bf16[26,1,128]{2,1,0:T(2,128)(2,1)S(1)} %get-tuple-element.96), channel_id=1, source_target_pairs={{1,0},{2,1},{3,2},{4,3},{5,4},{6,5},{7,6},{8,7},{9,8},{10,9},{11,1... | collective-permute-start | bytes 19976 | tf_op jit(solution)/shard_map/ppermute | solution.py:15
  44.0 28.5 %copy-start.1 = (bf16[24,24,128]{2,1,0:T(8,128)(2,1)S(1)}, bf16[24,24,128]{2,1,0:T(8,128)(2,1)}, u32[]{:S(2)}) copy-start(bf16[24,24,128]{2,1,0:T(8,128)(2,1)} %param.30) | copy-start | bytes 442372
  44.1 12.1 %collective-permute-start.5 = (bf16[2,57,128]{2,1,0:T(8,128)(2,1)S(1)}, bf16[2,57,128]{2,1,0:T(8,128)(2,1)S(1)}, u32[]{:S(2)}, u32[]{:S(2)}) collective-permute-start(bf16[2,57,128]{2,1,0:T(8,128)(2,1)S(1)} %maximum_select_fusion.6), channel_id=1, source_target_pairs={{0,96},{48,144},{96,0},{144,48},{192,288},{240,336},{288,192},{336... | collective-permute-start | bytes 87560 | tf_op jit(solution)/shard_map/ppermute | solution.py:56
  56.2 6.2 %collective-permute-start.6 = (bf16[2,2,57,128]{3,2,1,0:T(8,128)(2,1)S(1)}, bf16[2,2,57,128]{3,2,1,0:T(8,128)(2,1)S(1)}, u32[]{:S(2)}, u32[]{:S(2)}) collective-permute-start(bf16[2,2,57,128]{3,2,1,0:T(8,128)(2,1)S(1)} %maximum_select_fusion.4), channel_id=1, source_target_pairs={{0,192},{48,240},{96,288},{144,336},{192,0},{240,48},{288,96},{336... | collective-permute-start | bytes 175112 | tf_op jit(solution)/shard_map/ppermute | solution.py:56
  62.4 9.4 %collective-permute-start.7 = (bf16[2,2,2,57,128]{4,3,2,1,0:T(8,128)(2,1)S(1)}, bf16[2,2,2,57,128]{4,3,2,1,0:T(8,128)(2,1)S(1)}, u32[]{:S(2)}, u32[]{:S(2)}) collective-permute-start(bf16[2,2,2,57,128]{4,3,2,1,0:T(8,128)(2,1)S(1)} %maximum_select_fusion.2), channel_id=1, source_target_pairs={{0,384},{48,432},{96,480},{144,528},{192,576},{240,624},{288,672},... | collective-permute-start | bytes 350216 | tf_op jit(solution)/shard_map/ppermute | solution.py:56
  72.4 0.7 copy-start.15
  73.4 1.1 copy-start.6
  74.3 7.7 %copy-start.13 = (f32[128]{0:T(128)}, f32[128]{0:T(128)S(1)}, u32[]{:S(2)}) copy-start(f32[128]{0:T(128)S(1)} %reshape.606) | copy-start | bytes 1540
  75.4 8.4 %copy-start.4 = (f32[576,128]{1,0:T(8,128)S(1)}, f32[576,128]{1,0:T(8,128)}, u32[]{:S(2)}) copy-start(f32[576,128]{1,0:T(8,128)} %bitcast_multiply_fusion.1) | copy-start | bytes 884740
  75.4 9.3 %copy-start.16 = (f32[128]{0:T(128)S(1)}, f32[128]{0:T(128)}, u32[]{:S(2)}) copy-start(f32[128]{0:T(128)} %copy-done.15) | copy-start | bytes 1540
  82.0 1.5 copy-start.9
  83.6 2.0 %copy-start.8 = (bf16[24,24,128]{2,1,0:T(8,128)(2,1)S(1)}, bf16[24,24,128]{2,1,0:T(8,128)(2,1)}, u32[]{:S(2)}) copy-start(bf16[24,24,128]{2,1,0:T(8,128)(2,1)} %param.20) | copy-start | bytes 442372
  84.6 1.0 copy-start.10
  85.1 2.2 %copy-start.2 = (bf16[576,128]{1,0:T(8,128)(2,1)}, bf16[576,128]{1,0:T(8,128)(2,1)S(1)}, u32[]{:S(2)}) copy-start(bf16[576,128]{1,0:T(8,128)(2,1)S(1)} %multiply_convert_fusion.1) | copy-start | bytes 442372
  85.1 2.2 %copy-start.12 = (s32[1024]{0:T(1024)S(1)}, s32[1024]{0:T(1024)}, u32[]{:S(2)}) copy-start(s32[1024]{0:T(1024)} %get-tuple-element.108) | copy-start | bytes 12292
  87.3 5.2 %copy-start.14 = (f32[128]{0:T(128)S(1)}, f32[128]{0:T(128)}, u32[]{:S(2)}) copy-start(f32[128]{0:T(128)} %copy-done.13) | copy-start | bytes 1540
  92.8 0.9 copy-start.7
  93.7 0.9 copy-start.11
  93.7 1.0 copy-start.3
  93.7 1.3 copy-start.17
  94.1 10.9 %copy-start = (f32[1024,384]{1,0:T(8,128)}, f32[1024,384]{1,0:T(8,128)S(1)}, u32[]{:S(2)}) copy-start(f32[1024,384]{1,0:T(8,128)S(1)} %fusion.51) | copy-start | bytes 4718596
  96.1 18.0 %collective-permute-start.12 = (f32[2,2,2,57,128]{4,3,2,1,0:T(8,128)}, f32[2,2,2,57,128]{4,3,2,1,0:T(8,128)}, u32[]{:S(2)}, u32[]{:S(2)}) collective-permute-start(f32[2,2,2,57,128]{4,3,2,1,0:T(8,128)} %bitcast.36), channel_id=1, source_target_pairs={{0,384},{48,432},{96,480},{144,528},{192,576},{240,624},{288,672},... | collective-permute-start | bytes 700424 | tf_op jit(solution)/shard_map/ppermute | solution.py:56
  111.6 2.3 %slice-start = ((f32[1024,384]{1,0:T(8,128)}), f32[1024,128]{1,0:T(8,128)S(1)}, s32[]{:S(2)}) async-start(f32[1024,384]{1,0:T(8,128)} %copy-done), calls=%async_computation | async-start | bytes 1048576 | tf_op jit(solution)/shard_map/slice | solution.py:220
  111.7 25.5 %collective-permute-start.8 = (bf16[1,2,24,128]{3,2,1,0:T(8,128)(2,1)S(1)}, bf16[1,2,24,128]{3,2,1,0:T(8,128)(2,1)S(1)}, u32[]{:S(2)}, u32[]{:S(2)}) collective-permute-start(bf16[1,2,24,128]{3,2,1,0:T(8,128)(2,1)S(1)} %maximum_bitcast_fusion.1), channel_id=1, source_target_pairs={{0,48},{48,96},{96,144},{144,192},{192,240},{240,288},{288,336},{3... | collective-permute-start | bytes 36872 | tf_op jit(solution)/shard_map/ppermute | solution.py:12
  115.1 13.8 %collective-permute-start.13 = (f32[2,2,57,128]{3,2,1,0:T(8,128)S(1)}, f32[2,2,57,128]{3,2,1,0:T(8,128)S(1)}, u32[]{:S(2)}, u32[]{:S(2)}) collective-permute-start(f32[2,2,57,128]{3,2,1,0:T(8,128)S(1)} %select_bitcast_fusion), channel_id=1, source_target_pairs={{0,192},{48,240},{96,288},{144,336},{192,0},{240,48},{288,96},{336... | collective-permute-start | bytes 350216 | tf_op jit(solution)/shard_map/ppermute | solution.py:56
  117.2 74.5 %copy-start.5 = (f32[576,128]{1,0:T(8,128)S(1)}, f32[576,128]{1,0:T(8,128)}, u32[]{:S(2)}) copy-start(f32[576,128]{1,0:T(8,128)} %get-tuple-element.85) | copy-start | bytes 884740
  117.2 20.1 %collective-permute-start.9 = (bf16[1,2,24,128]{3,2,1,0:T(8,128)(2,1)S(1)}, bf16[1,2,24,128]{3,2,1,0:T(8,128)(2,1)S(1)}, u32[]{:S(2)}, u32[]{:S(2)}) collective-permute-start(bf16[1,2,24,128]{3,2,1,0:T(8,128)(2,1)S(1)} %maximum_bitcast_fusion.2), channel_id=1, source_target_pairs={{48,0},{96,48},{144,96},{192,144},{240,192},{288,240},{336,288},{3... | collective-permute-start | bytes 36872 | tf_op jit(solution)/shard_map/ppermute | solution.py:15
  128.9 12.6 %collective-permute-start.14 = (f32[2,57,128]{2,1,0:T(8,128)S(1)}, f32[2,57,128]{2,1,0:T(8,128)S(1)}, u32[]{:S(2)}, u32[]{:S(2)}) collective-permute-start(f32[2,57,128]{2,1,0:T(8,128)S(1)} %select_bitcast_fusion.1), channel_id=1, source_target_pairs={{0,96},{48,144},{96,0},{144,48},{192,288},{240,336},{288,192},{336... | collective-permute-start | bytes 175112 | tf_op jit(solution)/shard_map/ppermute | solution.py:56
  141.5 7.4 %collective-permute-start.15 = (f32[57,128]{1,0:T(8,128)S(1)}, f32[57,128]{1,0:T(8,128)S(1)}, u32[]{:S(2)}, u32[]{:S(2)}) collective-permute-start(f32[57,128]{1,0:T(8,128)S(1)} %select_bitcast_fusion.2), channel_id=1, source_target_pairs={{0,48},{48,0},{96,144},{144,96},{192,240},{240,192},{288,336},{336... | collective-permute-start | bytes 87560 | tf_op jit(solution)/shard_map/ppermute | solution.py:56
  143.5 10.3 %collective-permute-start.10 = (bf16[4,1,24,128]{3,2,1,0:T(8,128)(2,1)S(1)}, bf16[4,1,24,128]{3,2,1,0:T(8,128)(2,1)S(1)}, u32[]{:S(2)}, u32[]{:S(2)}) collective-permute-start(bf16[4,1,24,128]{3,2,1,0:T(8,128)(2,1)S(1)} %get-tuple-element.101), channel_id=1, source_target_pairs={{0,1},{1,2},{2,3},{3,4},{4,5},{5,6},{6,7},{7,8},{8,9},{9,10},{10,1... | collective-permute-start | bytes 73736 | tf_op jit(solution)/shard_map/ppermute | solution.py:12
  147.7 6.1 %collective-permute-start.11 = (bf16[4,1,24,128]{3,2,1,0:T(8,128)(2,1)S(1)}, bf16[4,1,24,128]{3,2,1,0:T(8,128)(2,1)S(1)}, u32[]{:S(2)}, u32[]{:S(2)}) collective-permute-start(bf16[4,1,24,128]{3,2,1,0:T(8,128)(2,1)S(1)} %get-tuple-element.102), channel_id=1, source_target_pairs={{1,0},{2,1},{3,2},{4,3},{5,4},{6,5},{7,6},{8,7},{9,8},{10,9},{11,1... | collective-permute-start | bytes 73736 | tf_op jit(solution)/shard_map/ppermute | solution.py:15
  149.0 6.7 %collective-permute-start.16 = (f32[57,128]{1,0:T(8,128)S(1)}, f32[57,128]{1,0:T(8,128)S(1)}, u32[]{:S(2)}, u32[]{:S(2)}) collective-permute-start(f32[57,128]{1,0:T(8,128)S(1)} %bitcast_add_fusion.2), channel_id=1, source_target_pairs={{0,1},{1,0},{2,3},{3,2},{4,5},{5,4},{6,7},{7,6},{8,9},{9,8},{10,11... | collective-permute-start | bytes 87560 | tf_op jit(solution)/shard_map/ppermute | solution.py:56
  155.7 8.6 %collective-permute-start.17 = (f32[57,128]{1,0:T(8,128)S(1)}, f32[57,128]{1,0:T(8,128)S(1)}, u32[]{:S(2)}, u32[]{:S(2)}) collective-permute-start(f32[57,128]{1,0:T(8,128)S(1)} %add.203), channel_id=1, source_target_pairs={{0,2},{1,3},{2,0},{3,1},{4,6},{5,7},{6,4},{7,5},{8,10},{9,11},{10,... | collective-permute-start | bytes 87560 | tf_op jit(solution)/shard_map/ppermute | solution.py:56
  164.2 9.7 %collective-permute-start.18 = (f32[57,128]{1,0:T(8,128)S(1)}, f32[57,128]{1,0:T(8,128)S(1)}, u32[]{:S(2)}, u32[]{:S(2)}) collective-permute-start(f32[57,128]{1,0:T(8,128)S(1)} %add.204), channel_id=1, source_target_pairs={{0,4},{1,5},{2,6},{3,7},{4,0},{5,1},{6,2},{7,3},{8,12},{9,13},{10,... | collective-permute-start | bytes 87560 | tf_op jit(solution)/shard_map/ppermute | solution.py:56
  173.9 6.7 %collective-permute-start.19 = (f32[57,128]{1,0:T(8,128)S(1)}, f32[57,128]{1,0:T(8,128)S(1)}, u32[]{:S(2)}, u32[]{:S(2)}) collective-permute-start(f32[57,128]{1,0:T(8,128)S(1)} %add.205), channel_id=1, source_target_pairs={{0,8},{1,9},{2,10},{3,11},{4,12},{5,13},{6,14},{7,15},{8,0},{9,1},... | collective-permute-start | bytes 87560 | tf_op jit(solution)/shard_map/ppermute | solution.py:56
  180.7 12.0 %collective-permute-start.20 = (f32[57,128]{1,0:T(8,128)S(1)}, f32[57,128]{1,0:T(8,128)S(1)}, u32[]{:S(2)}, u32[]{:S(2)}) collective-permute-start(f32[57,128]{1,0:T(8,128)S(1)} %add.206), channel_id=1, source_target_pairs={{0,16},{1,17},{2,18},{3,19},{4,20},{5,21},{6,22},{7,23},{8,24},{9,... | collective-permute-start | bytes 87560 | tf_op jit(solution)/shard_map/ppermute | solution.py:105
  185.9 8.2 %collective-permute-start.21 = (f32[57,128]{1,0:T(8,128)S(1)}, f32[57,128]{1,0:T(8,128)S(1)}, u32[]{:S(2)}, u32[]{:S(2)}) collective-permute-start(f32[57,128]{1,0:T(8,128)S(1)} %add.206), channel_id=1, source_target_pairs={{0,32},{1,33},{2,34},{3,35},{4,36},{5,37},{6,38},{7,39},{8,40},{9,... | collective-permute-start | bytes 87560 | tf_op jit(solution)/shard_map/ppermute | solution.py:105

commit v3 on v1

--- a/solution.py
+++ b/solution.py
@@ -51,12 +51,88 @@
     return (grad_inputs, first_part, second_part, gain_part)
 
 
+def digit_groups(count):
+    groups = []
+    stride = 1
+    rest = count
+    while rest > 1:
+        radix = 4 if rest % 4 == 0 else (2 if rest % 2 == 0 else rest)
+        groups.append((stride, radix))
+        stride *= radix
+        rest //= radix
+    return groups
+
+
+def shift_digit(value, axis, stride, radix, offset):
+    count = lax.axis_size(axis)
+    pairs = []
+    for i in range(count):
+        digit = (i // stride) % radix
+        pairs.append((i, i + (((digit + offset) % radix) - digit) * stride))
+    return lax.ppermute(value, axis, pairs)
+
+
+def by_digit(own, received, digit, radix):
+    values = [own] + list(received)
+    ordered = []
+    for position in range(radix):
+        source = (digit - position) % radix
+        pick = values[0]
+        for offset in range(1, radix):
+            pick = jnp.where(source == offset, values[offset], pick)
+        ordered.append(pick)
+    return ordered
+
+
+def gather_dom(packed):
+    index = lax.axis_index("dom")
+    block = packed
+    for stride, radix in digit_groups(lax.axis_size("dom")):
+        digit = (index // stride) % radix
+        received = [shift_digit(block, "dom", stride, radix, o) for o in range(1, radix)]
+        block = jnp.stack(by_digit(block, received, digit, radix))
+    return block.reshape((-1,) + packed.shape)
+
+
+def reduce_scatter_dom(packed):
+    index = lax.axis_index("dom")
+    groups = digit_groups(lax.axis_size("dom"))
+    block = packed.reshape(tuple(r for _, r in reversed(groups)) + packed.shape[1:])
+    for stride, radix in reversed(groups):
+        digit = (index // stride) % radix
+        parts = [block[p] for p in range(radix)]
+        total = parts[0]
+        for p in range(1, radix):
+            total = jnp.where(digit == p, parts[p], total)
+        for offset in range(1, radix):
+            target = (digit + offset) % radix
+            send = parts[0]
+            for p in range(1, radix):
+                send = jnp.where(target == p, parts[p], send)
+            total = total + shift_digit(send, "dom", stride, radix, offset)
+        block = total
+    return block
+
+
+def sum_sub(value):
+    index = lax.axis_index("sub")
+    total = value
+    for stride, radix in digit_groups(lax.axis_size("sub")):
+        digit = (index // stride) % radix
+        received = [shift_digit(total, "sub", stride, radix, o) for o in range(1, radix)]
+        ordered = by_digit(total, received, digit, radix)
+        total = ordered[0]
+        for item in ordered[1:]:
+            total = total + item
+    return total
+
+
 def gather_params(weights, gains):
     latent = weights[0].shape[1]
     gain_row = gains.reshape(1, -1)
     gain_row = jnp.pad(gain_row, ((0, 0), (0, latent - gain_row.shape[1])))
     packed = jnp.concatenate(list(weights) + [gain_row], axis=0)
-    full = lax.all_gather(packed, "dom", axis=0, tiled=False)
+    full = gather_dom(packed)
     count = full.shape[0]
     outs = []
     start = 0
@@ -79,8 +155,8 @@
     gain_block = jnp.transpose(gain_terms.reshape(2, count, width), (1, 0, 2)).reshape(count, 1, 2 * width)
     gain_block = jnp.pad(gain_block, ((0, 0), (0, 0), (0, latent - 2 * width)))
     packed = jnp.concatenate(blocks + [gain_block], axis=1)
-    shard = lax.psum_scatter(packed, "dom", scatter_dimension=0, tiled=True)[0]
-    shard = lax.psum(shard, "sub") * scale
+    shard = reduce_scatter_dom(packed)
+    shard = sum_sub(shard) * scale
     outs = []
     start = 0
     for b in blocks:

time: 544 us -> 225 us (0.41)
  blocking collectives: 334 us -> 0 us
  starting transfers between devices: 39.2 us -> 126 us
  waiting for transfers between devices: 90.7 us -> 30.1 us
  between operations: 15.4 us -> 2.94 us
    psum x1 -> x0, blocking collectives: 296 us -> none  [reduce_params(): shard = lax.psum(shard, 'sub') * scale]
    ppermute x0 -> x20, starting transfers between devices: none -> 90.7 us  [shift_digit(): return lax.ppermute(value, axis, pairs)]
    reduce_scatter x1 -> x0, waiting for transfers between devices: 83.1 us -> none  [reduce_params(): shard = lax.psum_scatter(packed, 'dom', scatter_dimension=0, tiled=True)[0]]
    all_gather x1 -> x0, blocking collectives: 38.2 us -> none  [gather_params(): full = lax.all_gather(packed, 'dom', axis=0, tiled=False)]
    ppermute x0 -> x20, waiting for transfers between devices: none -> 22.5 us  [shift_digit(): return lax.ppermute(value, axis, pairs)]
    ppermute x4, starting transfers between devices: 28.4 us -> 16.5 us  [with_halo(): lax.ppermute(lax.slice_in_dim(block, 0, width, axis=dim), axis, backward)]
    ppermute x4, starting transfers between devices: 10.8 us -> 18.6 us  [with_halo(): lax.ppermute(lax.slice_in_dim(block, block.shape[dim] - width, None, axis...]
  transfers between devices with their start and end apart: 9 -> 28, of which waited for: 3 -> 10; matrix products, arithmetic and copies ran while one was open for 2% -> 6% of each run, Pallas kernels for 0% -> 0%
where the time goes in v3:
time: 225 us; the launch traced here: 222 us
  starting transfers between devices  126 us (56%)
  waiting for transfers between devices  30.1 us (13%)
  other arithmetic  29.2 us (13%)
  local copies, waits for them, and re-layouts  28 us (12%)
  matrix products  5.76 us (3%)
  between operations  2.94 us (1%)
    ppermute x20, starting transfers between devices, shift_digit(): return lax.ppermute(value, axis, pairs)  90.7 us
    ppermute x20, waiting for transfers between devices, shift_digit(): return lax.ppermute(value, axis, pairs)  22.5 us
    ppermute x4, starting transfers between devices, with_halo(): lax.ppermute(lax.slice_in_dim(block, block.shape[dim] - width, None, axis...  18.6 us
    ppermute x4, starting transfers between devices, with_halo(): lax.ppermute(lax.slice_in_dim(block, 0, width, axis=dim), axis, backward)  16.5 us
    scatter-add x2, other arithmetic, shards(): spread = spread.at[source_pad].add(edge_in_grad[:, latent:2 * latent]).at...  14.2 us
    unnamed x62, local copies, waits for them, and re-layouts  8.92 us
    ppermute x4, waiting for transfers between devices, with_halo(): lax.ppermute(lax.slice_in_dim(block, 0, width, axis=dim), axis, backward)  7.61 us
    scatter-add x1, other arithmetic, shards(): jax.ops.segment_sum(message * active, edge_dst, num_segments=block_side *...  6.53 us
  transfers between devices with their start and end apart: 28, of which 10 were waited for; matrix products, arithmetic and copies ran while one was open for 6% of the time, Pallas kernels for 0%

profile of v3, /device:TPU:6, one launch (start us, length us, event | category | flops | bytes accessed | tf_op | source)
XLA Modules:
  0.0 221.7 jit_solution(1504906627591656546)
XLA Ops:
  0.6 0.7 constant_dynamic-update-slice_fusion.10
  1.4 0.7 reshape.298
  2.8 0.7 constant_dynamic-update-slice_fusion.8
  4.2 14.6 %collective-permute-start.4 = (bf16[57,128]{1,0:T(8,128)(2,1)S(1)}, bf16[57,128]{1,0:T(8,128)(2,1)S(1)}, u32[]{:S(2)}, u32[]{:S(2)}) collective-permute-start(bf16[57,128]{1,0:T(8,128)(2,1)S(1)} %constant_dynamic-update-slice_fusion.6), channel_id=1, source_target_pairs={{0,144},{48,0},{96,48},{144,96},{192,336},{240,192},{288,240},{336... | collective-permute-start | bytes 43784 | tf_op jit(solution)/shard_map/ppermute | solution.py:72
  18.8 2.5 %collective-permute-start.5 = (bf16[57,128]{1,0:T(8,128)(2,1)S(1)}, bf16[57,128]{1,0:T(8,128)(2,1)S(1)}, u32[]{:S(2)}, u32[]{:S(2)}) collective-permute-start(bf16[57,128]{1,0:T(8,128)(2,1)S(1)} %constant_dynamic-update-slice_fusion.6), channel_id=1, source_target_pairs={{0,96},{48,144},{96,0},{144,48},{192,288},{240,336},{288,192},{336... | collective-permute-start | bytes 43784 | tf_op jit(solution)/shard_map/ppermute | solution.py:72
  21.3 2.1 collective-permute-start.6
  23.4 0.7 fusion.47
  24.1 9.6 %collective-permute-start = (bf16[1,24,128]{2,1,0:T(8,128)(2,1)S(1)}, bf16[1,24,128]{2,1,0:T(8,128)(2,1)S(1)}, u32[]{:S(2)}, u32[]{:S(2)}) collective-permute-start(bf16[1,24,128]{2,1,0:T(8,128)(2,1)S(1)} %get-tuple-element.102), channel_id=1, source_target_pairs={{0,48},{48,96},{96,144},{144,192},{192,240},{240,288},{288,336},{3... | collective-permute-start | bytes 18440 | tf_op jit(solution)/shard_map/ppermute | solution.py:12
  33.7 3.2 %collective-permute-start.1 = (bf16[1,24,128]{2,1,0:T(8,128)(2,1)S(1)}, bf16[1,24,128]{2,1,0:T(8,128)(2,1)S(1)}, u32[]{:S(2)}, u32[]{:S(2)}) collective-permute-start(bf16[1,24,128]{2,1,0:T(8,128)(2,1)S(1)} %get-tuple-element.101), channel_id=1, source_target_pairs={{48,0},{96,48},{144,96},{192,144},{240,192},{288,240},{336,288},{3... | collective-permute-start | bytes 18440 | tf_op jit(solution)/shard_map/ppermute | solution.py:15
  37.1 1.0 constant_dynamic-update-slice_fusion.5
  38.8 1.3 broadcast_clamp_fusion
  40.1 0.9 constant_dynamic-update-slice_fusion.1
  41.1 3.5 %collective-permute-start.2 = (bf16[26,1,128]{2,1,0:T(2,128)(2,1)S(1)}, bf16[26,1,128]{2,1,0:T(2,128)(2,1)S(1)}, u32[]{:S(2)}, u32[]{:S(2)}) collective-permute-start(bf16[26,1,128]{2,1,0:T(2,128)(2,1)S(1)} %get-tuple-element.99), channel_id=1, source_target_pairs={{0,1},{1,2},{2,3},{3,4},{4,5},{5,6},{6,7},{7,8},{8,9},{9,10},{10,1... | collective-permute-start | bytes 19976 | tf_op jit(solution)/shard_map/ppermute | solution.py:12
  44.6 1.3 collective-permute-start.3
  46.3 3.9 %collective-permute-done.3 = bf16[26,1,128]{2,1,0:T(2,128)(2,1)S(1)} collective-permute-done((bf16[26,1,128]{2,1,0:T(2,128)(2,1)S(1)}, bf16[26,1,128]{2,1,0:T(2,128)(2,1)S(1)}, u32[]{:S(2)}, u32[]{:S(2)}) %collective-permute-start.3) | collective-permute-done | bytes 6688 | tf_op jit(solution)/shard_map/ppermute | solution.py:15
  50.4 3.2 %gather_fusion = bf16[1024,128]{1,0:T(8,128)(2,1)S(1)} fusion(bf16[676,128]{1,0:T(8,128)(2,1)S(1)} %reshape.297, s32[1024]{0:T(1024)S(1)} %get-tuple-element.119), kind=kCustom, calls=%fused_computation | custom fusion | bytes 528384 | tf_op jit(solution)/shard_map/gather | solution.py:204
  53.7 3.2 %gather_fusion.1 = bf16[1024,128]{1,0:T(8,128)(2,1)S(1)} fusion(bf16[676,128]{1,0:T(8,128)(2,1)S(1)} %reshape.297, s32[1024]{0:T(1024)S(1)} %get-tuple-element.81), kind=kCustom, calls=%fused_computation.1 | custom fusion | bytes 528384 | tf_op jit(solution)/shard_map/gather | solution.py:204
  57.0 2.7 %collective-permute-start.7 = (bf16[4,57,128]{2,1,0:T(8,128)(2,1)S(1)}, bf16[4,57,128]{2,1,0:T(8,128)(2,1)S(1)}, u32[]{:S(2)}, u32[]{:S(2)}) collective-permute-start(bf16[4,57,128]{2,1,0:T(8,128)(2,1)S(1)} %pad_maximum_fusion.5), channel_id=1, source_target_pairs={{0,576},{48,624},{96,672},{144,720},{192,0},{240,48},{288,96},{336... | collective-permute-start | bytes 175112 | tf_op jit(solution)/shard_map/ppermute | solution.py:72
  59.7 2.5 %collective-permute-start.8 = (bf16[4,57,128]{2,1,0:T(8,128)(2,1)S(1)}, bf16[4,57,128]{2,1,0:T(8,128)(2,1)S(1)}, u32[]{:S(2)}, u32[]{:S(2)}) collective-permute-start(bf16[4,57,128]{2,1,0:T(8,128)(2,1)S(1)} %pad_maximum_fusion.5), channel_id=1, source_target_pairs={{0,384},{48,432},{96,480},{144,528},{192,576},{240,624},{288,672},... | collective-permute-start | bytes 175112 | tf_op jit(solution)/shard_map/ppermute | solution.py:72
  62.2 4.5 %collective-permute-start.9 = (bf16[4,57,128]{2,1,0:T(8,128)(2,1)S(1)}, bf16[4,57,128]{2,1,0:T(8,128)(2,1)S(1)}, u32[]{:S(2)}, u32[]{:S(2)}) collective-permute-start(bf16[4,57,128]{2,1,0:T(8,128)(2,1)S(1)} %pad_maximum_fusion.5), channel_id=1, source_target_pairs={{0,192},{48,240},{96,288},{144,336},{192,384},{240,432},{288,480},... | collective-permute-start | bytes 175112 | tf_op jit(solution)/shard_map/ppermute | solution.py:72
  67.4 1.7 collective-permute-done.9
  69.7 0.8 bitcast_multiply_fusion.1
  70.5 0.8 fusion.10
  72.3 1.0 copy.45
  73.3 6.5 %scatter_custom_fusion = f32[576,128]{1,0:T(8,128)S(1)} fusion(s32[1024]{0:T(1024)} %param.22, f32[1024,128]{1,0:T(8,128)} %copy.45, f32[]{:T(128)} %constant.340.clone.1), kind=kCustom, calls=%fused_computation.49 | custom fusion | flops 131072 | bytes 295424 | tf_op jit(solution)/shard_map/scatter-add | solution.py:208
  79.9 1.2 fusion.14
  81.8 0.7 fusion.11
  83.5 1.0 fusion.13
  84.4 0.8 slice_add_fusion
  85.2 4.0 %gather_fusion.2 = f32[1024,128]{1,0:T(8,128)} fusion(f32[576,128]{1,0:T(8,128)S(1)} %get-tuple-element.86, s32[1024]{0:T(1024)S(1)} %get-tuple-element.118), kind=kCustom, calls=%fused_computation.2 | custom fusion | bytes 1052672 | tf_op jit(solution)/shard_map/gather | solution.py:229
  89.2 1.2 copy.50
  90.7 0.9 multiply_convert_fusion
  92.3 1.1 fusion.55
  93.8 6.9 %scatter_custom_fusion.1 = f32[676,128]{1,0:T(8,128)} fusion(s32[1024]{0:T(1024)} %get-tuple-element.120, f32[1024,384]{1,0:T(8,128)S(1)} %fusion.54, f32[]{:T(128)} %constant.340.clone.1), kind=kCustom, calls=%fused_computation.20 | custom fusion | flops 131072 | bytes 870912 | tf_op jit(solution)/shard_map/scatter-add | solution.py:237
  100.7 7.3 %scatter_custom_fusion.2 = f32[676,128]{1,0:T(8,128)} fusion(f32[676,128]{1,0:T(8,128)} %scatter_custom_fusion.1, s32[1024]{0:T(1024)} %get-tuple-element.82, f32[1024,384]{1,0:T(8,128)S(1)} %fusion.54), kind=kCustom, calls=%fused_computation.18 | custom fusion | flops 131072 | bytes 870400 | tf_op jit(solution)/shard_map/scatter-add | solution.py:239
  108.0 1.1 reshape.305
  109.9 0.9 constant_dynamic-update-slice_fusion.12
  111.8 0.7 select_select_fusion.2
  112.5 5.2 %collective-permute-start.14 = (f32[4,57,128]{2,1,0:T(8,128)}, f32[4,57,128]{2,1,0:T(8,128)S(1)}, u32[]{:S(2)}, u32[]{:S(2)}) collective-permute-start(f32[4,57,128]{2,1,0:T(8,128)} %get-tuple-element.87), channel_id=1, source_target_pairs={{0,192},{48,240},{96,288},{144,336},{192,384},{240,432},{288,480},... | collective-permute-start | bytes 350216 | tf_op jit(solution)/shard_map/ppermute | solution.py:72
  117.7 2.8 %collective-permute-start.15 = (f32[4,57,128]{2,1,0:T(8,128)S(1)}, f32[4,57,128]{2,1,0:T(8,128)S(1)}, u32[]{:S(2)}, u32[]{:S(2)}) collective-permute-start(f32[4,57,128]{2,1,0:T(8,128)S(1)} %get-tuple-element.88), channel_id=1, source_target_pairs={{0,384},{48,432},{96,480},{144,528},{192,576},{240,624},{288,672},... | collective-permute-start | bytes 350216 | tf_op jit(solution)/shard_map/ppermute | solution.py:72
  120.5 2.1 collective-permute-start.10
  122.6 10.7 %collective-permute-start.11 = (bf16[1,2,24,128]{3,2,1,0:T(8,128)(2,1)S(1)}, bf16[1,2,24,128]{3,2,1,0:T(8,128)(2,1)S(1)}, u32[]{:S(2)}, u32[]{:S(2)}) collective-permute-start(bf16[1,2,24,128]{3,2,1,0:T(8,128)(2,1)S(1)} %maximum_bitcast_fusion.2), channel_id=1, source_target_pairs={{48,0},{96,48},{144,96},{192,144},{240,192},{288,240},{336,288},{3... | collective-permute-start | bytes 36872 | tf_op jit(solution)/shard_map/ppermute | solution.py:15
  134.0 1.9 collective-permute-start.16
  136.2 3.5 %collective-permute-start.12 = (bf16[4,1,24,128]{3,2,1,0:T(8,128)(2,1)S(1)}, bf16[4,1,24,128]{3,2,1,0:T(8,128)(2,1)S(1)}, u32[]{:S(2)}, u32[]{:S(2)}) collective-permute-start(bf16[4,1,24,128]{3,2,1,0:T(8,128)(2,1)S(1)} %get-tuple-element.111), channel_id=1, source_target_pairs={{0,1},{1,2},{2,3},{3,4},{4,5},{5,6},{6,7},{7,8},{8,9},{9,10},{10,1... | collective-permute-start | bytes 73736 | tf_op jit(solution)/shard_map/ppermute | solution.py:12
  139.7 1.3 collective-permute-start.13
  141.2 0.8 copy.58
  142.1 3.7 %collective-permute-done.13 = bf16[4,1,24,128]{3,2,1,0:T(8,128)(2,1)S(1)} collective-permute-done((bf16[4,1,24,128]{3,2,1,0:T(8,128)(2,1)S(1)}, bf16[4,1,24,128]{3,2,1,0:T(8,128)(2,1)S(1)}, u32[]{:S(2)}, u32[]{:S(2)}) %collective-permute-start.13) | collective-permute-done | bytes 24608 | tf_op jit(solution)/shard_map/ppermute | solution.py:15
  146.0 5.1 %collective-permute-start.17 = (f32[57,128]{1,0:T(8,128)S(1)}, f32[57,128]{1,0:T(8,128)S(1)}, u32[]{:S(2)}, u32[]{:S(2)}) collective-permute-start(f32[57,128]{1,0:T(8,128)S(1)} %get-tuple-element.103), channel_id=1, source_target_pairs={{0,48},{48,96},{96,144},{144,0},{192,240},{240,288},{288,336},{336... | collective-permute-start | bytes 87560 | tf_op jit(solution)/shard_map/ppermute | solution.py:72
  151.2 4.4 %collective-permute-start.18 = (f32[57,128]{1,0:T(8,128)S(1)}, f32[57,128]{1,0:T(8,128)S(1)}, u32[]{:S(2)}, u32[]{:S(2)}) collective-permute-start(f32[57,128]{1,0:T(8,128)S(1)} %get-tuple-element.104), channel_id=1, source_target_pairs={{0,96},{48,144},{96,0},{144,48},{192,288},{240,336},{288,192},{336... | collective-permute-start | bytes 87560 | tf_op jit(solution)/shard_map/ppermute | solution.py:72
  155.6 9.7 %collective-permute-start.19 = (f32[57,128]{1,0:T(8,128)S(1)}, f32[57,128]{1,0:T(8,128)S(1)}, u32[]{:S(2)}, u32[]{:S(2)}) collective-permute-start(f32[57,128]{1,0:T(8,128)S(1)} %select_bitcast_fusion.4), channel_id=1, source_target_pairs={{0,144},{48,0},{96,48},{144,96},{192,336},{240,192},{288,240},{336... | collective-permute-start | bytes 87560 | tf_op jit(solution)/shard_map/ppermute | solution.py:72
  165.4 1.4 collective-permute-done.19
  166.9 7.2 %collective-permute-start.20 = (f32[57,128]{1,0:T(8,128)S(1)}, f32[57,128]{1,0:T(8,128)S(1)}, u32[]{:S(2)}, u32[]{:S(2)}) collective-permute-start(f32[57,128]{1,0:T(8,128)S(1)} %fusion.21), channel_id=1, source_target_pairs={{0,3},{1,0},{2,1},{3,2},{4,7},{5,4},{6,5},{7,6},{8,11},{9,8},{10,9... | collective-permute-start | bytes 87560 | tf_op jit(solution)/shard_map/ppermute | solution.py:72
  174.2 1.9 collective-permute-start.21
  176.1 3.3 %collective-permute-start.22 = (f32[57,128]{1,0:T(8,128)S(1)}, f32[57,128]{1,0:T(8,128)S(1)}, u32[]{:S(2)}, u32[]{:S(2)}) collective-permute-start(f32[57,128]{1,0:T(8,128)S(1)} %fusion.21), channel_id=1, source_target_pairs={{0,1},{1,2},{2,3},{3,0},{4,5},{5,6},{6,7},{7,4},{8,9},{9,10},{10,1... | collective-permute-start | bytes 87560 | tf_op jit(solution)/shard_map/ppermute | solution.py:72
  179.4 1.5 collective-permute-done.21
  180.9 2.8 %collective-permute-done.22 = f32[57,128]{1,0:T(8,128)S(1)} collective-permute-done((f32[57,128]{1,0:T(8,128)S(1)}, f32[57,128]{1,0:T(8,128)S(1)}, u32[]{:S(2)}, u32[]{:S(2)}) %collective-permute-start.22) | collective-permute-done | bytes 29216 | tf_op jit(solution)/shard_map/ppermute | solution.py:72
  183.7 8.1 %collective-permute-start.23 = (f32[57,128]{1,0:T(8,128)S(1)}, f32[57,128]{1,0:T(8,128)S(1)}, u32[]{:S(2)}, u32[]{:S(2)}) collective-permute-start(f32[57,128]{1,0:T(8,128)S(1)} %select_add_fusion.1), channel_id=1, source_target_pairs={{0,12},{1,13},{2,14},{3,15},{4,0},{5,1},{6,2},{7,3},{8,4},{9,5},{1... | collective-permute-start | bytes 87560 | tf_op jit(solution)/shard_map/ppermute | solution.py:72
  191.8 1.9 collective-permute-start.24
  193.7 3.1 %collective-permute-start.25 = (f32[57,128]{1,0:T(8,128)S(1)}, f32[57,128]{1,0:T(8,128)S(1)}, u32[]{:S(2)}, u32[]{:S(2)}) collective-permute-start(f32[57,128]{1,0:T(8,128)S(1)} %select_add_fusion.1), channel_id=1, source_target_pairs={{0,4},{1,5},{2,6},{3,7},{4,8},{5,9},{6,10},{7,11},{8,12},{9,13},{1... | collective-permute-start | bytes 87560 | tf_op jit(solution)/shard_map/ppermute | solution.py:72
  196.9 0.7 collective-permute-done.24
  197.6 6.7 %collective-permute-done.25 = f32[57,128]{1,0:T(8,128)S(1)} collective-permute-done((f32[57,128]{1,0:T(8,128)S(1)}, f32[57,128]{1,0:T(8,128)S(1)}, u32[]{:S(2)}, u32[]{:S(2)}) %collective-permute-start.25) | collective-permute-done | bytes 29216 | tf_op jit(solution)/shard_map/ppermute | solution.py:72
  204.4 5.1 %collective-permute-start.26 = (f32[57,128]{1,0:T(8,128)S(1)}, f32[57,128]{1,0:T(8,128)S(1)}, u32[]{:S(2)}, u32[]{:S(2)}) collective-permute-start(f32[57,128]{1,0:T(8,128)S(1)} %select_add_fusion), channel_id=1, source_target_pairs={{0,32},{1,33},{2,34},{3,35},{4,36},{5,37},{6,38},{7,39},{8,40},{9,... | collective-permute-start | bytes 87560 | tf_op jit(solution)/shard_map/ppermute | solution.py:72
  209.5 1.9 collective-permute-start.27
  212.2 7.0 %collective-permute-done.27 = f32[57,128]{1,0:T(8,128)S(1)} collective-permute-done((f32[57,128]{1,0:T(8,128)S(1)}, f32[57,128]{1,0:T(8,128)S(1)}, u32[]{:S(2)}, u32[]{:S(2)}) %collective-permute-start.27) | collective-permute-done | bytes 29216 | tf_op jit(solution)/shard_map/ppermute | solution.py:72
  (162 shorter events, 13.3 us)
Async XLA Ops:
  0.6 45.5 %copy-start.15 = (bf16[1024,128]{1,0:T(8,128)(2,1)S(1)}, bf16[1024,128]{1,0:T(8,128)(2,1)}, u32[]{:S(2)}) copy-start(bf16[1024,128]{1,0:T(8,128)(2,1)} %param.31) | copy-start | bytes 786436
  4.2 52.7 %collective-permute-start.4 = (bf16[57,128]{1,0:T(8,128)(2,1)S(1)}, bf16[57,128]{1,0:T(8,128)(2,1)S(1)}, u32[]{:S(2)}, u32[]{:S(2)}) collective-permute-start(bf16[57,128]{1,0:T(8,128)(2,1)S(1)} %constant_dynamic-update-slice_fusion.6), channel_id=1, source_target_pairs={{0,144},{48,0},{96,48},{144,96},{192,336},{240,192},{288,240},{336... | collective-permute-start | bytes 43784 | tf_op jit(solution)/shard_map/ppermute | solution.py:72
  18.8 38.1 %collective-permute-start.5 = (bf16[57,128]{1,0:T(8,128)(2,1)S(1)}, bf16[57,128]{1,0:T(8,128)(2,1)S(1)}, u32[]{:S(2)}, u32[]{:S(2)}) collective-permute-start(bf16[57,128]{1,0:T(8,128)(2,1)S(1)} %constant_dynamic-update-slice_fusion.6), channel_id=1, source_target_pairs={{0,96},{48,144},{96,0},{144,48},{192,288},{240,336},{288,192},{336... | collective-permute-start | bytes 43784 | tf_op jit(solution)/shard_map/ppermute | solution.py:72
  21.3 35.7 %collective-permute-start.6 = (bf16[57,128]{1,0:T(8,128)(2,1)S(1)}, bf16[57,128]{1,0:T(8,128)(2,1)S(1)}, u32[]{:S(2)}, u32[]{:S(2)}) collective-permute-start(bf16[57,128]{1,0:T(8,128)(2,1)S(1)} %constant_dynamic-update-slice_fusion.6), channel_id=1, source_target_pairs={{0,48},{48,96},{96,144},{144,0},{192,240},{240,288},{288,336},{336... | collective-permute-start | bytes 43784 | tf_op jit(solution)/shard_map/ppermute | solution.py:72
  24.1 16.0 %collective-permute-start = (bf16[1,24,128]{2,1,0:T(8,128)(2,1)S(1)}, bf16[1,24,128]{2,1,0:T(8,128)(2,1)S(1)}, u32[]{:S(2)}, u32[]{:S(2)}) collective-permute-start(bf16[1,24,128]{2,1,0:T(8,128)(2,1)S(1)} %get-tuple-element.102), channel_id=1, source_target_pairs={{0,48},{48,96},{96,144},{144,192},{192,240},{240,288},{288,336},{3... | collective-permute-start | bytes 18440 | tf_op jit(solution)/shard_map/ppermute | solution.py:12
  33.7 7.4 %collective-permute-start.1 = (bf16[1,24,128]{2,1,0:T(8,128)(2,1)S(1)}, bf16[1,24,128]{2,1,0:T(8,128)(2,1)S(1)}, u32[]{:S(2)}, u32[]{:S(2)}) collective-permute-start(bf16[1,24,128]{2,1,0:T(8,128)(2,1)S(1)} %get-tuple-element.101), channel_id=1, source_target_pairs={{48,0},{96,48},{144,96},{192,144},{240,192},{288,240},{336,288},{3... | collective-permute-start | bytes 18440 | tf_op jit(solution)/shard_map/ppermute | solution.py:15
  41.1 5.2 %collective-permute-start.2 = (bf16[26,1,128]{2,1,0:T(2,128)(2,1)S(1)}, bf16[26,1,128]{2,1,0:T(2,128)(2,1)S(1)}, u32[]{:S(2)}, u32[]{:S(2)}) collective-permute-start(bf16[26,1,128]{2,1,0:T(2,128)(2,1)S(1)} %get-tuple-element.99), channel_id=1, source_target_pairs={{0,1},{1,2},{2,3},{3,4},{4,5},{5,6},{6,7},{7,8},{8,9},{9,10},{10,1... | collective-permute-start | bytes 19976 | tf_op jit(solution)/shard_map/ppermute | solution.py:12
  44.6 5.6 %collective-permute-start.3 = (bf16[26,1,128]{2,1,0:T(2,128)(2,1)S(1)}, bf16[26,1,128]{2,1,0:T(2,128)(2,1)S(1)}, u32[]{:S(2)}, u32[]{:S(2)}) collective-permute-start(bf16[26,1,128]{2,1,0:T(2,128)(2,1)S(1)} %get-tuple-element.100), channel_id=1, source_target_pairs={{1,0},{2,1},{3,2},{4,3},{5,4},{6,5},{7,6},{8,7},{9,8},{10,9},{11,1... | collective-permute-start | bytes 19976 | tf_op jit(solution)/shard_map/ppermute | solution.py:15
  56.9 12.8 %copy-start.1 = (bf16[24,24,128]{2,1,0:T(8,128)(2,1)S(1)}, bf16[24,24,128]{2,1,0:T(8,128)(2,1)}, u32[]{:S(2)}) copy-start(bf16[24,24,128]{2,1,0:T(8,128)(2,1)} %param.30) | copy-start | bytes 442372
  57.0 9.9 %collective-permute-start.7 = (bf16[4,57,128]{2,1,0:T(8,128)(2,1)S(1)}, bf16[4,57,128]{2,1,0:T(8,128)(2,1)S(1)}, u32[]{:S(2)}, u32[]{:S(2)}) collective-permute-start(bf16[4,57,128]{2,1,0:T(8,128)(2,1)S(1)} %pad_maximum_fusion.5), channel_id=1, source_target_pairs={{0,576},{48,624},{96,672},{144,720},{192,0},{240,48},{288,96},{336... | collective-permute-start | bytes 175112 | tf_op jit(solution)/shard_map/ppermute | solution.py:72
  59.7 7.7 %collective-permute-start.8 = (bf16[4,57,128]{2,1,0:T(8,128)(2,1)S(1)}, bf16[4,57,128]{2,1,0:T(8,128)(2,1)S(1)}, u32[]{:S(2)}, u32[]{:S(2)}) collective-permute-start(bf16[4,57,128]{2,1,0:T(8,128)(2,1)S(1)} %pad_maximum_fusion.5), channel_id=1, source_target_pairs={{0,384},{48,432},{96,480},{144,528},{192,576},{240,624},{288,672},... | collective-permute-start | bytes 175112 | tf_op jit(solution)/shard_map/ppermute | solution.py:72
  62.2 6.8 %collective-permute-start.9 = (bf16[4,57,128]{2,1,0:T(8,128)(2,1)S(1)}, bf16[4,57,128]{2,1,0:T(8,128)(2,1)S(1)}, u32[]{:S(2)}, u32[]{:S(2)}) collective-permute-start(bf16[4,57,128]{2,1,0:T(8,128)(2,1)S(1)} %pad_maximum_fusion.5), channel_id=1, source_target_pairs={{0,192},{48,240},{96,288},{144,336},{192,384},{240,432},{288,480},... | collective-permute-start | bytes 175112 | tf_op jit(solution)/shard_map/ppermute | solution.py:72
  69.7 2.2 %copy-start.19 = (f32[128]{0:T(128)}, f32[128]{0:T(128)S(1)}, u32[]{:S(2)}) copy-start(f32[128]{0:T(128)S(1)} %reshape.317) | copy-start | bytes 1540
  71.3 1.1 copy-start.10
  72.2 18.3 %copy-start.18 = (f32[128]{0:T(128)}, f32[128]{0:T(128)S(1)}, u32[]{:S(2)}) copy-start(f32[128]{0:T(128)S(1)} %reshape.316) | copy-start | bytes 1540
  73.3 8.4 %copy-start.8 = (f32[576,128]{1,0:T(8,128)S(1)}, f32[576,128]{1,0:T(8,128)}, u32[]{:S(2)}) copy-start(f32[576,128]{1,0:T(8,128)} %bitcast_multiply_fusion.1) | copy-start | bytes 884740
  73.3 9.2 %copy-start.17 = (f32[24,24]{1,0:T(8,128)S(1)}, f32[24,24]{1,0:T(8,128)}, u32[]{:S(2)}) copy-start(f32[24,24]{1,0:T(8,128)} %fusion.10) | copy-start | bytes 6916
  73.3 9.3 %copy-start.20 = (f32[128]{0:T(128)S(1)}, f32[128]{0:T(128)}, u32[]{:S(2)}) copy-start(f32[128]{0:T(128)} %copy-done.19) | copy-start | bytes 1540
  79.9 1.5 copy-start.13
  81.5 2.0 copy-start.12
  82.5 1.0 copy-start.14
  83.0 2.2 copy-start.6
  90.7 2.7 %copy-start.11 = (bf16[16,24,128]{2,1,0:T(8,128)(2,1)S(1)}, bf16[16,24,128]{2,1,0:T(8,128)(2,1)}, u32[]{:S(2)}) copy-start(bf16[16,24,128]{2,1,0:T(8,128)(2,1)} %copy-done.10) | copy-start | bytes 294916
  91.6 0.7 copy-start.4
  93.8 15.4 %copy-start = (f32[1024,384]{1,0:T(8,128)}, f32[1024,384]{1,0:T(8,128)S(1)}, u32[]{:S(2)}) copy-start(f32[1024,384]{1,0:T(8,128)S(1)} %fusion.54) | copy-start | bytes 4718596
  108.0 2.8 %copy-start.5 = (bf16[1024,128]{0,1:T(8,128)(2,1)S(1)}, bf16[1024,128]{0,1:T(8,128)(2,1)}, u32[]{:S(2)}) copy-start(bf16[1024,128]{0,1:T(8,128)(2,1)} %copy-done.4) | copy-start | bytes 786436
  109.1 0.8 copy-start.2
  109.1 2.0 copy-start.16
  109.1 2.0 copy-start.7
  109.2 2.3 %copy-start.21 = (f32[128]{0:T(128)S(1)}, f32[128]{0:T(128)}, u32[]{:S(2)}) copy-start(f32[128]{0:T(128)} %get-tuple-element.79) | copy-start | bytes 1540
  110.8 25.1 %slice-start = ((f32[1024,384]{1,0:T(8,128)}), f32[1024,128]{1,0:T(8,128)S(1)}, s32[]{:S(2)}) async-start(f32[1024,384]{1,0:T(8,128)} %copy-done), calls=%async_computation | async-start | bytes 1048576 | tf_op jit(solution)/shard_map/slice | solution.py:233
  112.5 28.6 %copy-start.3 = (f32[26,26,128]{2,1,0:T(8,128)S(1)}, f32[26,26,128]{2,1,0:T(8,128)}, u32[]{:S(2)}) copy-start(f32[26,26,128]{2,1,0:T(8,128)} %copy-done.2) | copy-start | bytes 1038340
  112.5 33.4 %collective-permute-start.14 = (f32[4,57,128]{2,1,0:T(8,128)}, f32[4,57,128]{2,1,0:T(8,128)S(1)}, u32[]{:S(2)}, u32[]{:S(2)}) collective-permute-start(f32[4,57,128]{2,1,0:T(8,128)} %get-tuple-element.87), channel_id=1, source_target_pairs={{0,192},{48,240},{96,288},{144,336},{192,384},{240,432},{288,480},... | collective-permute-start | bytes 350216 | tf_op jit(solution)/shard_map/ppermute | solution.py:72
  117.7 28.2 %collective-permute-start.15 = (f32[4,57,128]{2,1,0:T(8,128)S(1)}, f32[4,57,128]{2,1,0:T(8,128)S(1)}, u32[]{:S(2)}, u32[]{:S(2)}) collective-permute-start(f32[4,57,128]{2,1,0:T(8,128)S(1)} %get-tuple-element.88), channel_id=1, source_target_pairs={{0,384},{48,432},{96,480},{144,528},{192,576},{240,624},{288,672},... | collective-permute-start | bytes 350216 | tf_op jit(solution)/shard_map/ppermute | solution.py:72
  120.5 15.6 %collective-permute-start.10 = (bf16[1,2,24,128]{3,2,1,0:T(8,128)(2,1)S(1)}, bf16[1,2,24,128]{3,2,1,0:T(8,128)(2,1)S(1)}, u32[]{:S(2)}, u32[]{:S(2)}) collective-permute-start(bf16[1,2,24,128]{3,2,1,0:T(8,128)(2,1)S(1)} %maximum_bitcast_fusion.1), channel_id=1, source_target_pairs={{0,48},{48,96},{96,144},{144,192},{192,240},{240,288},{288,336},{3... | collective-permute-start | bytes 36872 | tf_op jit(solution)/shard_map/ppermute | solution.py:12
  122.6 13.5 %collective-permute-start.11 = (bf16[1,2,24,128]{3,2,1,0:T(8,128)(2,1)S(1)}, bf16[1,2,24,128]{3,2,1,0:T(8,128)(2,1)S(1)}, u32[]{:S(2)}, u32[]{:S(2)}) collective-permute-start(bf16[1,2,24,128]{3,2,1,0:T(8,128)(2,1)S(1)} %maximum_bitcast_fusion.2), channel_id=1, source_target_pairs={{48,0},{96,48},{144,96},{192,144},{240,192},{288,240},{336,288},{3... | collective-permute-start | bytes 36872 | tf_op jit(solution)/shard_map/ppermute | solution.py:15
  134.0 11.9 %collective-permute-start.16 = (f32[4,57,128]{2,1,0:T(8,128)}, f32[4,57,128]{2,1,0:T(8,128)S(1)}, u32[]{:S(2)}, u32[]{:S(2)}) collective-permute-start(f32[4,57,128]{2,1,0:T(8,128)} %select_select_fusion), channel_id=1, source_target_pairs={{0,576},{48,624},{96,672},{144,720},{192,0},{240,48},{288,96},{336... | collective-permute-start | bytes 350216 | tf_op jit(solution)/shard_map/ppermute | solution.py:72
  136.2 5.8 %collective-permute-start.12 = (bf16[4,1,24,128]{3,2,1,0:T(8,128)(2,1)S(1)}, bf16[4,1,24,128]{3,2,1,0:T(8,128)(2,1)S(1)}, u32[]{:S(2)}, u32[]{:S(2)}) collective-permute-start(bf16[4,1,24,128]{3,2,1,0:T(8,128)(2,1)S(1)} %get-tuple-element.111), channel_id=1, source_target_pairs={{0,1},{1,2},{2,3},{3,4},{4,5},{5,6},{6,7},{7,8},{8,9},{9,10},{10,1... | collective-permute-start | bytes 73736 | tf_op jit(solution)/shard_map/ppermute | solution.py:12
  139.7 6.1 %collective-permute-start.13 = (bf16[4,1,24,128]{3,2,1,0:T(8,128)(2,1)S(1)}, bf16[4,1,24,128]{3,2,1,0:T(8,128)(2,1)S(1)}, u32[]{:S(2)}, u32[]{:S(2)}) collective-permute-start(bf16[4,1,24,128]{3,2,1,0:T(8,128)(2,1)S(1)} %get-tuple-element.112), channel_id=1, source_target_pairs={{1,0},{2,1},{3,2},{4,3},{5,4},{6,5},{7,6},{8,7},{9,8},{10,9},{11,1... | collective-permute-start | bytes 73736 | tf_op jit(solution)/shard_map/ppermute | solution.py:15
  141.2 70.2 %copy-start.9 = (f32[576,128]{1,0:T(8,128)S(1)}, f32[576,128]{1,0:T(8,128)}, u32[]{:S(2)}) copy-start(f32[576,128]{1,0:T(8,128)} %get-tuple-element.85) | copy-start | bytes 884740
  146.0 19.4 %collective-permute-start.17 = (f32[57,128]{1,0:T(8,128)S(1)}, f32[57,128]{1,0:T(8,128)S(1)}, u32[]{:S(2)}, u32[]{:S(2)}) collective-permute-start(f32[57,128]{1,0:T(8,128)S(1)} %get-tuple-element.103), channel_id=1, source_target_pairs={{0,48},{48,96},{96,144},{144,0},{192,240},{240,288},{288,336},{336... | collective-permute-start | bytes 87560 | tf_op jit(solution)/shard_map/ppermute | solution.py:72
  151.2 14.3 %collective-permute-start.18 = (f32[57,128]{1,0:T(8,128)S(1)}, f32[57,128]{1,0:T(8,128)S(1)}, u32[]{:S(2)}, u32[]{:S(2)}) collective-permute-start(f32[57,128]{1,0:T(8,128)S(1)} %get-tuple-element.104), channel_id=1, source_target_pairs={{0,96},{48,144},{96,0},{144,48},{192,288},{240,336},{288,192},{336... | collective-permute-start | bytes 87560 | tf_op jit(solution)/shard_map/ppermute | solution.py:72
  155.6 11.3 %collective-permute-start.19 = (f32[57,128]{1,0:T(8,128)S(1)}, f32[57,128]{1,0:T(8,128)S(1)}, u32[]{:S(2)}, u32[]{:S(2)}) collective-permute-start(f32[57,128]{1,0:T(8,128)S(1)} %select_bitcast_fusion.4), channel_id=1, source_target_pairs={{0,144},{48,0},{96,48},{144,96},{192,336},{240,192},{288,240},{336... | collective-permute-start | bytes 87560 | tf_op jit(solution)/shard_map/ppermute | solution.py:72
  166.9 12.5 %collective-permute-start.20 = (f32[57,128]{1,0:T(8,128)S(1)}, f32[57,128]{1,0:T(8,128)S(1)}, u32[]{:S(2)}, u32[]{:S(2)}) collective-permute-start(f32[57,128]{1,0:T(8,128)S(1)} %fusion.21), channel_id=1, source_target_pairs={{0,3},{1,0},{2,1},{3,2},{4,7},{5,4},{6,5},{7,6},{8,11},{9,8},{10,9... | collective-permute-start | bytes 87560 | tf_op jit(solution)/shard_map/ppermute | solution.py:72
  174.2 6.7 %collective-permute-start.21 = (f32[57,128]{1,0:T(8,128)S(1)}, f32[57,128]{1,0:T(8,128)S(1)}, u32[]{:S(2)}, u32[]{:S(2)}) collective-permute-start(f32[57,128]{1,0:T(8,128)S(1)} %fusion.21), channel_id=1, source_target_pairs={{0,2},{1,3},{2,0},{3,1},{4,6},{5,7},{6,4},{7,5},{8,10},{9,11},{10,... | collective-permute-start | bytes 87560 | tf_op jit(solution)/shard_map/ppermute | solution.py:72
  176.1 7.6 %collective-permute-start.22 = (f32[57,128]{1,0:T(8,128)S(1)}, f32[57,128]{1,0:T(8,128)S(1)}, u32[]{:S(2)}, u32[]{:S(2)}) collective-permute-start(f32[57,128]{1,0:T(8,128)S(1)} %fusion.21), channel_id=1, source_target_pairs={{0,1},{1,2},{2,3},{3,0},{4,5},{5,6},{6,7},{7,4},{8,9},{9,10},{10,1... | collective-permute-start | bytes 87560 | tf_op jit(solution)/shard_map/ppermute | solution.py:72
  183.7 13.2 %collective-permute-start.23 = (f32[57,128]{1,0:T(8,128)S(1)}, f32[57,128]{1,0:T(8,128)S(1)}, u32[]{:S(2)}, u32[]{:S(2)}) collective-permute-start(f32[57,128]{1,0:T(8,128)S(1)} %select_add_fusion.1), channel_id=1, source_target_pairs={{0,12},{1,13},{2,14},{3,15},{4,0},{5,1},{6,2},{7,3},{8,4},{9,5},{1... | collective-permute-start | bytes 87560 | tf_op jit(solution)/shard_map/ppermute | solution.py:72
  191.8 5.8 %collective-permute-start.24 = (f32[57,128]{1,0:T(8,128)S(1)}, f32[57,128]{1,0:T(8,128)S(1)}, u32[]{:S(2)}, u32[]{:S(2)}) collective-permute-start(f32[57,128]{1,0:T(8,128)S(1)} %select_add_fusion.1), channel_id=1, source_target_pairs={{0,8},{1,9},{2,10},{3,11},{4,12},{5,13},{6,14},{7,15},{8,0},{9,1},... | collective-permute-start | bytes 87560 | tf_op jit(solution)/shard_map/ppermute | solution.py:72
  193.7 10.6 %collective-permute-start.25 = (f32[57,128]{1,0:T(8,128)S(1)}, f32[57,128]{1,0:T(8,128)S(1)}, u32[]{:S(2)}, u32[]{:S(2)}) collective-permute-start(f32[57,128]{1,0:T(8,128)S(1)} %select_add_fusion.1), channel_id=1, source_target_pairs={{0,4},{1,5},{2,6},{3,7},{4,8},{5,9},{6,10},{7,11},{8,12},{9,13},{1... | collective-permute-start | bytes 87560 | tf_op jit(solution)/shard_map/ppermute | solution.py:72
  204.4 7.8 %collective-permute-start.26 = (f32[57,128]{1,0:T(8,128)S(1)}, f32[57,128]{1,0:T(8,128)S(1)}, u32[]{:S(2)}, u32[]{:S(2)}) collective-permute-start(f32[57,128]{1,0:T(8,128)S(1)} %select_add_fusion), channel_id=1, source_target_pairs={{0,32},{1,33},{2,34},{3,35},{4,36},{5,37},{6,38},{7,39},{8,40},{9,... | collective-permute-start | bytes 87560 | tf_op jit(solution)/shard_map/ppermute | solution.py:72
  209.5 9.7 %collective-permute-start.27 = (f32[57,128]{1,0:T(8,128)S(1)}, f32[57,128]{1,0:T(8,128)S(1)}, u32[]{:S(2)}, u32[]{:S(2)}) collective-permute-start(f32[57,128]{1,0:T(8,128)S(1)} %select_add_fusion), channel_id=1, source_target_pairs={{0,16},{1,17},{2,18},{3,19},{4,20},{5,21},{6,22},{7,23},{8,24},{9,... | collective-permute-start | bytes 87560 | tf_op jit(solution)/shard_map/ppermute | solution.py:72

commit v4 on v1

--- a/solution.py
+++ b/solution.py
@@ -51,12 +51,30 @@
     return (grad_inputs, first_part, second_part, gain_part)
 
 
+def gather_dom(packed):
+    count = lax.axis_size("dom")
+    spread = jnp.broadcast_to(packed[None], (count,) + packed.shape)
+    return lax.all_to_all(spread, "dom", 0, 0, tiled=True)
+
+
+def reduce_scatter_dom(packed):
+    return jnp.sum(lax.all_to_all(packed, "dom", 0, 0, tiled=True), axis=0)
+
+
+def sum_sub(value):
+    count = lax.axis_size("sub")
+    flat = value.reshape(count, -1)
+    piece = jnp.sum(lax.all_to_all(flat, "sub", 0, 0, tiled=True), axis=0)
+    spread = jnp.broadcast_to(piece[None], flat.shape)
+    return lax.all_to_all(spread, "sub", 0, 0, tiled=True).reshape(value.shape)
+
+
 def gather_params(weights, gains):
     latent = weights[0].shape[1]
     gain_row = gains.reshape(1, -1)
     gain_row = jnp.pad(gain_row, ((0, 0), (0, latent - gain_row.shape[1])))
     packed = jnp.concatenate(list(weights) + [gain_row], axis=0)
-    full = lax.all_gather(packed, "dom", axis=0, tiled=False)
+    full = gather_dom(packed)
     count = full.shape[0]
     outs = []
     start = 0
@@ -79,8 +97,8 @@
     gain_block = jnp.transpose(gain_terms.reshape(2, count, width), (1, 0, 2)).reshape(count, 1, 2 * width)
     gain_block = jnp.pad(gain_block, ((0, 0), (0, 0), (0, latent - 2 * width)))
     packed = jnp.concatenate(blocks + [gain_block], axis=1)
-    shard = lax.psum_scatter(packed, "dom", scatter_dimension=0, tiled=True)[0]
-    shard = lax.psum(shard, "sub") * scale
+    shard = reduce_scatter_dom(packed)
+    shard = sum_sub(shard) * scale
     outs = []
     start = 0
     for b in blocks:

time: 544 us -> 197 us (0.36)
  blocking collectives: 334 us -> 0 us
  waiting for transfers between devices: 90.7 us -> 33.5 us
  starting transfers between devices: 39.2 us -> 91.8 us
  between operations: 15.4 us -> 2.06 us
  local copies, waits for them, and re-layouts: 27 us -> 33.6 us
    psum x1 -> x0, blocking collectives: 296 us -> none  [reduce_params(): shard = lax.psum(shard, 'sub') * scale]
    reduce_scatter x1 -> x0, waiting for transfers between devices: 83.1 us -> none  [reduce_params(): shard = lax.psum_scatter(packed, 'dom', scatter_dimension=0, tiled=True)[0]]
    all_to_all x0 -> x4, starting transfers between devices: none -> 52.5 us  [the longest x1 23.4 us: sum_sub(): piece = jnp.sum(lax.all_to_all(flat, 'sub', 0, 0, tiled=True), axis=0)]
    all_gather x1 -> x0, blocking collectives: 38.2 us -> none  [gather_params(): full = lax.all_gather(packed, 'dom', axis=0, tiled=False)]
    all_to_all x0 -> x4, waiting for transfers between devices: none -> 25.7 us  [the longest x1 13.2 us: sum_sub(): piece = jnp.sum(lax.all_to_all(flat, 'sub', 0, 0, tiled=True), axis=0)]
  transfers between devices with their start and end apart: 9 -> 12, of which waited for: 3 -> 4; matrix products, arithmetic and copies ran while one was open for 2% -> 9% of each run, Pallas kernels for 0% -> 0%
where the time goes in v4:
time: 197 us; the launch traced here: 195 us
  starting transfers between devices  91.8 us (47%)
  local copies, waits for them, and re-layouts  33.6 us (17%)
  waiting for transfers between devices  33.5 us (17%)
  other arithmetic  25.1 us (13%)
  matrix products  9.34 us (5%)
  between operations  2.06 us (1%)
    ppermute x4, starting transfers between devices, with_halo(): lax.ppermute(lax.slice_in_dim(block, 0, width, axis=dim), axis, backward)  28.1 us
    all_to_all x1, starting transfers between devices, sum_sub(): piece = jnp.sum(lax.all_to_all(flat, 'sub', 0, 0, tiled=True), axis=0)  23.4 us
    scatter-add x2, other arithmetic, shards(): spread = spread.at[source_pad].add(edge_in_grad[:, latent:2 * latent]).at...  13.9 us
    all_to_all x1, waiting for transfers between devices, sum_sub(): piece = jnp.sum(lax.all_to_all(flat, 'sub', 0, 0, tiled=True), axis=0)  13.2 us
    all_to_all x1, starting transfers between devices, gather_dom(): return lax.all_to_all(spread, 'dom', 0, 0, tiled=True)  12.6 us
    all_to_all x1, waiting for transfers between devices, sum_sub(): return lax.all_to_all(spread, 'sub', 0, 0, tiled=True).reshape(value.shape)  12.5 us
    all_to_all x1, starting transfers between devices, reduce_scatter_dom(): return jnp.sum(lax.all_to_all(packed, 'dom', 0, 0, tiled=True), axis=0)  12 us
    ppermute x4, starting transfers between devices, with_halo(): lax.ppermute(lax.slice_in_dim(block, block.shape[dim] - width, None, axis...  11.1 us
  transfers between devices with their start and end apart: 12, of which 4 were waited for; matrix products, arithmetic and copies ran while one was open for 9% of the time, Pallas kernels for 0%

profile of v4, /device:TPU:6, one launch (start us, length us, event | category | flops | bytes accessed | tf_op | source)
XLA Modules:
  0.0 195.4 jit_solution(7793488937435934675)
XLA Ops:
  0.6 0.8 fusion.36
  1.4 1.9 collective-permute-start
  3.3 14.8 %collective-permute-start.1 = (bf16[1,24,128]{2,1,0:T(8,128)(2,1)S(1)}, bf16[1,24,128]{2,1,0:T(8,128)(2,1)S(1)}, u32[]{:S(2)}, u32[]{:S(2)}) collective-permute-start(bf16[1,24,128]{2,1,0:T(8,128)(2,1)S(1)} %get-tuple-element.100), channel_id=1, source_target_pairs={{48,0},{96,48},{144,96},{192,144},{240,192},{288,240},{336,288},{3... | collective-permute-start | bytes 18440 | tf_op jit(solution)/shard_map/ppermute | solution.py:15
  18.2 0.7 constant_dynamic-update-slice_fusion.10
  18.9 0.7 reshape.277
  19.6 0.7 constant_dynamic-update-slice_fusion.9
  20.3 0.7 constant_dynamic-update-slice_fusion.8
  21.0 0.7 constant_dynamic-update-slice_fusion.7
  21.7 0.8 broadcast_in_dim.29
  22.4 12.6 %all-to-all-start = ((bf16[16,57,128]{2,1,0:T(8,128)(2,1)}), bf16[16,57,128]{2,1,0:T(8,128)(2,1)S(1)}, u32[]{:S(2)}, u32[]{:S(2)}) async-start(bf16[16,57,128]{2,1,0:T(8,128)(2,1)} %broadcast_in_dim.29), calls=%async_computation | async-start | bytes 524288 | tf_op jit(solution)/shard_map/all_to_all | solution.py:57
  35.0 0.7 broadcast_clamp_fusion
  35.7 1.0 constant_dynamic-update-slice_fusion.5
  37.4 0.9 constant_dynamic-update-slice_fusion.1
  38.4 3.5 %collective-permute-start.2 = (bf16[26,1,128]{2,1,0:T(2,128)(2,1)S(1)}, bf16[26,1,128]{2,1,0:T(2,128)(2,1)S(1)}, u32[]{:S(2)}, u32[]{:S(2)}) collective-permute-start(bf16[26,1,128]{2,1,0:T(2,128)(2,1)S(1)} %get-tuple-element.98), channel_id=1, source_target_pairs={{0,1},{1,2},{2,3},{3,4},{4,5},{5,6},{6,7},{7,8},{8,9},{9,10},{10,1... | collective-permute-start | bytes 19976 | tf_op jit(solution)/shard_map/ppermute | solution.py:12
  41.9 1.3 collective-permute-start.3
  43.4 4.1 %collective-permute-done.3 = bf16[26,1,128]{2,1,0:T(2,128)(2,1)S(1)} collective-permute-done((bf16[26,1,128]{2,1,0:T(2,128)(2,1)S(1)}, bf16[26,1,128]{2,1,0:T(2,128)(2,1)S(1)}, u32[]{:S(2)}, u32[]{:S(2)}) %collective-permute-start.3) | collective-permute-done | bytes 6688 | tf_op jit(solution)/shard_map/ppermute | solution.py:15
  47.7 3.2 %gather_fusion = bf16[1024,128]{1,0:T(8,128)(2,1)S(1)} fusion(bf16[676,128]{1,0:T(8,128)(2,1)S(1)} %reshape.276, s32[1024]{0:T(1024)S(1)} %get-tuple-element.112), kind=kCustom, calls=%fused_computation | custom fusion | bytes 528384 | tf_op jit(solution)/shard_map/gather | solution.py:146
  50.9 3.2 %gather_fusion.1 = bf16[1024,128]{1,0:T(8,128)(2,1)S(1)} fusion(bf16[676,128]{1,0:T(8,128)(2,1)S(1)} %reshape.276, s32[1024]{0:T(1024)S(1)} %get-tuple-element.88), kind=kCustom, calls=%fused_computation.1 | custom fusion | bytes 528384 | tf_op jit(solution)/shard_map/gather | solution.py:146
  54.6 0.7 bitcast_multiply_fusion.1
  55.5 0.4 fusion.41
  55.8 0.3 fusion.39
  56.5 1.0 copy.55
  57.5 6.5 %scatter_custom_fusion = f32[576,128]{1,0:T(8,128)S(1)} fusion(s32[1024]{0:T(1024)} %param.22, f32[1024,128]{1,0:T(8,128)} %copy.55, f32[]{:T(128)} %constant.150.clone.1), kind=kCustom, calls=%fused_computation.48 | custom fusion | flops 131072 | bytes 295424 | tf_op jit(solution)/shard_map/scatter-add | solution.py:150
  64.1 1.2 fusion.14
  65.3 1.1 fusion.40
  66.4 0.3 multiply_reduce_fusion.5
  66.7 0.3 fusion.11
  67.1 0.4 multiply_convert_fusion.1
  67.5 1.0 fusion.1
  68.8 1.0 fusion.13
  69.7 0.8 slice_add_fusion
  70.5 4.0 %gather_fusion.2 = f32[1024,128]{1,0:T(8,128)} fusion(f32[576,128]{1,0:T(8,128)S(1)} %get-tuple-element.93, s32[1024]{0:T(1024)S(1)} %get-tuple-element.111), kind=kCustom, calls=%fused_computation.2 | custom fusion | bytes 1052672 | tf_op jit(solution)/shard_map/gather | solution.py:171
  74.5 1.2 copy.58
  76.2 1.0 fusion
  77.3 1.1 fusion.44
  78.4 0.4 fusion.43
  78.8 6.8 %scatter_custom_fusion.1 = f32[676,128]{1,0:T(8,128)} fusion(s32[1024]{0:T(1024)S(1)} %get-tuple-element.113, f32[1024,384]{1,0:T(8,128)S(1)} %fusion.43, f32[]{:T(128)} %constant.150.clone.1), kind=kCustom, calls=%fused_computation.20 | custom fusion | flops 131072 | bytes 870404 | tf_op jit(solution)/shard_map/scatter-add | solution.py:179
  85.5 7.2 %scatter_custom_fusion.2 = f32[676,128]{1,0:T(8,128)} fusion(f32[676,128]{1,0:T(8,128)} %scatter_custom_fusion.1, s32[1024]{0:T(1024)S(1)} %get-tuple-element.89, f32[1024,384]{1,0:T(8,128)S(1)} %fusion.43), kind=kCustom, calls=%fused_computation.18 | custom fusion | flops 131072 | bytes 870400 | tf_op jit(solution)/shard_map/scatter-add | solution.py:181
  92.7 1.0 reshape.283
  93.9 1.6 constant_dynamic-update-slice_fusion.12
  95.5 0.9 fusion.3
  96.4 0.7 constant_dynamic-update-slice_fusion.11
  97.1 0.9 fusion.2
  98.3 1.5 dynamic-update-slice.16
  99.8 12.0 %all-to-all-start.1 = ((f32[16,57,128]{2,1,0:T(8,128)}), f32[16,57,128]{2,1,0:T(8,128)S(1)}, u32[]{:S(2)}, u32[]{:S(2)}) async-start(f32[16,57,128]{2,1,0:T(8,128)} %dynamic-update-slice.16), calls=%async_computation.1 | async-start | bytes 1048576 | tf_op jit(solution)/shard_map/all_to_all | solution.py:61
  111.9 2.1 %collective-permute-start.4 = (bf16[1,2,24,128]{3,2,1,0:T(8,128)(2,1)S(1)}, bf16[1,2,24,128]{3,2,1,0:T(8,128)(2,1)S(1)}, u32[]{:S(2)}, u32[]{:S(2)}) collective-permute-start(bf16[1,2,24,128]{3,2,1,0:T(8,128)(2,1)S(1)} %maximum_bitcast_fusion.1), channel_id=1, source_target_pairs={{0,48},{48,96},{96,144},{144,192},{192,240},{240,288},{288,336},{3... | collective-permute-start | bytes 36872 | tf_op jit(solution)/shard_map/ppermute | solution.py:12
  114.0 10.7 %collective-permute-start.5 = (bf16[1,2,24,128]{3,2,1,0:T(8,128)(2,1)S(1)}, bf16[1,2,24,128]{3,2,1,0:T(8,128)(2,1)S(1)}, u32[]{:S(2)}, u32[]{:S(2)}) collective-permute-start(bf16[1,2,24,128]{3,2,1,0:T(8,128)(2,1)S(1)} %maximum_bitcast_fusion.2), channel_id=1, source_target_pairs={{48,0},{96,48},{144,96},{192,144},{240,192},{288,240},{336,288},{3... | collective-permute-start | bytes 36872 | tf_op jit(solution)/shard_map/ppermute | solution.py:15
  124.7 0.8 slice.259
  125.5 1.2 copy.71
  126.8 3.6 %collective-permute-start.6 = (bf16[4,1,24,128]{3,2,1,0:T(8,128)(2,1)S(1)}, bf16[4,1,24,128]{3,2,1,0:T(8,128)(2,1)S(1)}, u32[]{:S(2)}, u32[]{:S(2)}) collective-permute-start(bf16[4,1,24,128]{3,2,1,0:T(8,128)(2,1)S(1)} %get-tuple-element.104), channel_id=1, source_target_pairs={{0,1},{1,2},{2,3},{3,4},{4,5},{5,6},{6,7},{7,8},{8,9},{9,10},{10,1... | collective-permute-start | bytes 73736 | tf_op jit(solution)/shard_map/ppermute | solution.py:12
  130.5 1.3 collective-permute-start.7
  132.0 0.8 copy.66
  132.8 3.6 %collective-permute-done.7 = bf16[4,1,24,128]{3,2,1,0:T(8,128)(2,1)S(1)} collective-permute-done((bf16[4,1,24,128]{3,2,1,0:T(8,128)(2,1)S(1)}, bf16[4,1,24,128]{3,2,1,0:T(8,128)(2,1)S(1)}, u32[]{:S(2)}, u32[]{:S(2)}) %collective-permute-start.7) | collective-permute-done | bytes 24608 | tf_op jit(solution)/shard_map/ppermute | solution.py:15
  136.7 0.8 all_to_all.18
  137.5 23.4 %all-to-all-start.2 = ((f32[48,1,152]{2,1,0:T(1,128)}), f32[48,1,152]{2,1,0:T(1,128)S(1)}, u32[]{:S(2)}, u32[]{:S(2)}) async-start(f32[48,1,152]{2,1,0:T(1,128)} %all_to_all.18), calls=%async_computation.2 | async-start | bytes 98304 | tf_op jit(solution)/shard_map/all_to_all | solution.py:67
  160.9 13.2 %all-to-all-done.2 = f32[48,1,152]{2,1,0:T(1,128)S(1)} async-done(((f32[48,1,152]{2,1,0:T(1,128)}), f32[48,1,152]{2,1,0:T(1,128)S(1)}, u32[]{:S(2)}, u32[]{:S(2)}) %all-to-all-start.2) | async-done | bytes 29216 | tf_op jit(solution)/shard_map/all_to_all | solution.py:67
  174.2 0.6 broadcast_in_dim.33
  174.9 4.5 %all-to-all-start.3 = ((f32[48,1,152]{2,1,0:T(1,128)}), f32[48,1,152]{2,1,0:T(1,128)S(1)}, u32[]{:S(2)}, u32[]{:S(2)}) async-start(f32[48,1,152]{2,1,0:T(1,128)} %broadcast_in_dim.33), calls=%async_computation.3 | async-start | bytes 98304 | tf_op jit(solution)/shard_map/all_to_all | solution.py:69
  179.5 0.7 copy.65
  180.2 12.5 %all-to-all-done.3 = f32[48,1,152]{2,1,0:T(1,128)S(1)} async-done(((f32[48,1,152]{2,1,0:T(1,128)}), f32[48,1,152]{2,1,0:T(1,128)S(1)}, u32[]{:S(2)}, u32[]{:S(2)}) %all-to-all-start.3) | async-done | bytes 29216 | tf_op jit(solution)/shard_map/all_to_all | solution.py:69
  192.9 0.6 slice.260
  193.5 0.6 fusion.38
  194.1 0.6 slice.262
  194.7 0.6 reshape_squeeze.7
  (104 shorter events, 3.4 us)
Async XLA Ops:
  0.6 42.6 %copy-start.13 = (bf16[1024,128]{1,0:T(8,128)(2,1)S(1)}, bf16[1024,128]{1,0:T(8,128)(2,1)}, u32[]{:S(2)}) copy-start(bf16[1024,128]{1,0:T(8,128)(2,1)} %param.31) | copy-start | bytes 786436
  1.4 36.0 %collective-permute-start = (bf16[1,24,128]{2,1,0:T(8,128)(2,1)S(1)}, bf16[1,24,128]{2,1,0:T(8,128)(2,1)S(1)}, u32[]{:S(2)}, u32[]{:S(2)}) collective-permute-start(bf16[1,24,128]{2,1,0:T(8,128)(2,1)S(1)} %get-tuple-element.101), channel_id=1, source_target_pairs={{0,48},{48,96},{96,144},{144,192},{192,240},{240,288},{288,336},{3... | collective-permute-start | bytes 18440 | tf_op jit(solution)/shard_map/ppermute | solution.py:12
  3.3 35.0 %collective-permute-start.1 = (bf16[1,24,128]{2,1,0:T(8,128)(2,1)S(1)}, bf16[1,24,128]{2,1,0:T(8,128)(2,1)S(1)}, u32[]{:S(2)}, u32[]{:S(2)}) collective-permute-start(bf16[1,24,128]{2,1,0:T(8,128)(2,1)S(1)} %get-tuple-element.100), channel_id=1, source_target_pairs={{48,0},{96,48},{144,96},{192,144},{240,192},{288,240},{336,288},{3... | collective-permute-start | bytes 18440 | tf_op jit(solution)/shard_map/ppermute | solution.py:15
  22.4 31.8 %all-to-all-start = ((bf16[16,57,128]{2,1,0:T(8,128)(2,1)}), bf16[16,57,128]{2,1,0:T(8,128)(2,1)S(1)}, u32[]{:S(2)}, u32[]{:S(2)}) async-start(bf16[16,57,128]{2,1,0:T(8,128)(2,1)} %broadcast_in_dim.29), calls=%async_computation | async-start | bytes 524288 | tf_op jit(solution)/shard_map/all_to_all | solution.py:57
  38.4 5.0 %collective-permute-start.2 = (bf16[26,1,128]{2,1,0:T(2,128)(2,1)S(1)}, bf16[26,1,128]{2,1,0:T(2,128)(2,1)S(1)}, u32[]{:S(2)}, u32[]{:S(2)}) collective-permute-start(bf16[26,1,128]{2,1,0:T(2,128)(2,1)S(1)} %get-tuple-element.98), channel_id=1, source_target_pairs={{0,1},{1,2},{2,3},{3,4},{4,5},{5,6},{6,7},{7,8},{8,9},{9,10},{10,1... | collective-permute-start | bytes 19976 | tf_op jit(solution)/shard_map/ppermute | solution.py:12
  41.9 5.6 %collective-permute-start.3 = (bf16[26,1,128]{2,1,0:T(2,128)(2,1)S(1)}, bf16[26,1,128]{2,1,0:T(2,128)(2,1)S(1)}, u32[]{:S(2)}, u32[]{:S(2)}) collective-permute-start(bf16[26,1,128]{2,1,0:T(2,128)(2,1)S(1)} %get-tuple-element.99), channel_id=1, source_target_pairs={{1,0},{2,1},{3,2},{4,3},{5,4},{6,5},{7,6},{8,7},{9,8},{10,9},{11,1... | collective-permute-start | bytes 19976 | tf_op jit(solution)/shard_map/ppermute | solution.py:15
  50.9 3.7 %copy-start = (bf16[24,24,128]{2,1,0:T(8,128)(2,1)S(1)}, bf16[24,24,128]{2,1,0:T(8,128)(2,1)}, u32[]{:S(2)}) copy-start(bf16[24,24,128]{2,1,0:T(8,128)(2,1)} %param.30) | copy-start | bytes 442372
  54.3 9.8 %copy-start.5 = (bf16[16,57,128]{2,1,0:T(8,128)(2,1)}, bf16[16,57,128]{2,1,0:T(8,128)(2,1)S(1)}, u32[]{:S(2)}) copy-start(bf16[16,57,128]{2,1,0:T(8,128)(2,1)S(1)} %all-to-all-done) | copy-start | bytes 700420
  55.5 1.0 copy-start.8
  57.5 9.2 %copy-start.6 = (f32[576,128]{1,0:T(8,128)S(1)}, f32[576,128]{1,0:T(8,128)}, u32[]{:S(2)}) copy-start(f32[576,128]{1,0:T(8,128)} %bitcast_multiply_fusion.1) | copy-start | bytes 884740
  64.1 2.3 %copy-start.11 = (bf16[576,128]{1,0:T(8,128)(2,1)}, bf16[576,128]{1,0:T(8,128)(2,1)S(1)}, u32[]{:S(2)}) copy-start(bf16[576,128]{1,0:T(8,128)(2,1)S(1)} %convert_element_type.80) | copy-start | bytes 442372
  66.4 2.4 %copy-start.10 = (bf16[24,24,128]{2,1,0:T(8,128)(2,1)S(1)}, bf16[24,24,128]{2,1,0:T(8,128)(2,1)}, u32[]{:S(2)}) copy-start(bf16[24,24,128]{2,1,0:T(8,128)(2,1)} %param.20) | copy-start | bytes 442372
  67.0 1.7 copy-start.12
  67.5 3.0 %copy-start.3 = (bf16[576,128]{1,0:T(8,128)(2,1)}, bf16[576,128]{1,0:T(8,128)(2,1)S(1)}, u32[]{:S(2)}) copy-start(bf16[576,128]{1,0:T(8,128)(2,1)S(1)} %multiply_convert_fusion.1) | copy-start | bytes 442372
  76.0 2.4 %copy-start.9 = (bf16[16,24,128]{2,1,0:T(8,128)(2,1)S(1)}, bf16[16,24,128]{2,1,0:T(8,128)(2,1)}, u32[]{:S(2)}) copy-start(bf16[16,24,128]{2,1,0:T(8,128)(2,1)} %copy-done.8) | copy-start | bytes 294916
  76.2 1.1 copy-start.1
  85.5 10.0 %copy-start.2 = (bf16[1024,128]{0,1:T(8,128)(2,1)S(1)}, bf16[1024,128]{0,1:T(8,128)(2,1)}, u32[]{:S(2)}) copy-start(bf16[1024,128]{0,1:T(8,128)(2,1)} %copy-done.1) | copy-start | bytes 786436
  92.7 3.7 %copy-start.14 = (f32[256,128]{1,0:T(8,128)S(1)}, f32[256,128]{1,0:T(8,128)}, u32[]{:S(2)}) copy-start(f32[256,128]{1,0:T(8,128)} %fusion.13) | copy-start | bytes 393220
  93.8 3.3 %copy-start.4 = (bf16[576,128]{1,0:T(8,128)(2,1)S(1)}, bf16[576,128]{1,0:T(8,128)(2,1)}, u32[]{:S(2)}) copy-start(bf16[576,128]{1,0:T(8,128)(2,1)} %copy-done.3) | copy-start | bytes 442372
  99.8 36.9 %all-to-all-start.1 = ((f32[16,57,128]{2,1,0:T(8,128)}), f32[16,57,128]{2,1,0:T(8,128)S(1)}, u32[]{:S(2)}, u32[]{:S(2)}) async-start(f32[16,57,128]{2,1,0:T(8,128)} %dynamic-update-slice.16), calls=%async_computation.1 | async-start | bytes 1048576 | tf_op jit(solution)/shard_map/all_to_all | solution.py:61
  111.9 14.9 %collective-permute-start.4 = (bf16[1,2,24,128]{3,2,1,0:T(8,128)(2,1)S(1)}, bf16[1,2,24,128]{3,2,1,0:T(8,128)(2,1)S(1)}, u32[]{:S(2)}, u32[]{:S(2)}) collective-permute-start(bf16[1,2,24,128]{3,2,1,0:T(8,128)(2,1)S(1)} %maximum_bitcast_fusion.1), channel_id=1, source_target_pairs={{0,48},{48,96},{96,144},{144,192},{192,240},{240,288},{288,336},{3... | collective-permute-start | bytes 36872 | tf_op jit(solution)/shard_map/ppermute | solution.py:12
  114.0 12.8 %collective-permute-start.5 = (bf16[1,2,24,128]{3,2,1,0:T(8,128)(2,1)S(1)}, bf16[1,2,24,128]{3,2,1,0:T(8,128)(2,1)S(1)}, u32[]{:S(2)}, u32[]{:S(2)}) collective-permute-start(bf16[1,2,24,128]{3,2,1,0:T(8,128)(2,1)S(1)} %maximum_bitcast_fusion.2), channel_id=1, source_target_pairs={{48,0},{96,48},{144,96},{192,144},{240,192},{288,240},{336,288},{3... | collective-permute-start | bytes 36872 | tf_op jit(solution)/shard_map/ppermute | solution.py:15
  126.8 6.0 %collective-permute-start.6 = (bf16[4,1,24,128]{3,2,1,0:T(8,128)(2,1)S(1)}, bf16[4,1,24,128]{3,2,1,0:T(8,128)(2,1)S(1)}, u32[]{:S(2)}, u32[]{:S(2)}) collective-permute-start(bf16[4,1,24,128]{3,2,1,0:T(8,128)(2,1)S(1)} %get-tuple-element.104), channel_id=1, source_target_pairs={{0,1},{1,2},{2,3},{3,4},{4,5},{5,6},{6,7},{7,8},{8,9},{9,10},{10,1... | collective-permute-start | bytes 73736 | tf_op jit(solution)/shard_map/ppermute | solution.py:12
  130.5 6.0 %collective-permute-start.7 = (bf16[4,1,24,128]{3,2,1,0:T(8,128)(2,1)S(1)}, bf16[4,1,24,128]{3,2,1,0:T(8,128)(2,1)S(1)}, u32[]{:S(2)}, u32[]{:S(2)}) collective-permute-start(bf16[4,1,24,128]{3,2,1,0:T(8,128)(2,1)S(1)} %get-tuple-element.105), channel_id=1, source_target_pairs={{1,0},{2,1},{3,2},{4,3},{5,4},{6,5},{7,6},{8,7},{9,8},{10,9},{11,1... | collective-permute-start | bytes 73736 | tf_op jit(solution)/shard_map/ppermute | solution.py:15
  131.8 47.6 %copy-start.7 = (f32[576,128]{1,0:T(8,128)S(1)}, f32[576,128]{1,0:T(8,128)}, u32[]{:S(2)}) copy-start(f32[576,128]{1,0:T(8,128)} %get-tuple-element.92) | copy-start | bytes 884740
  137.5 36.7 %all-to-all-start.2 = ((f32[48,1,152]{2,1,0:T(1,128)}), f32[48,1,152]{2,1,0:T(1,128)S(1)}, u32[]{:S(2)}, u32[]{:S(2)}) async-start(f32[48,1,152]{2,1,0:T(1,128)} %all_to_all.18), calls=%async_computation.2 | async-start | bytes 98304 | tf_op jit(solution)/shard_map/all_to_all | solution.py:67
  174.9 17.8 %all-to-all-start.3 = ((f32[48,1,152]{2,1,0:T(1,128)}), f32[48,1,152]{2,1,0:T(1,128)S(1)}, u32[]{:S(2)}, u32[]{:S(2)}) async-start(f32[48,1,152]{2,1,0:T(1,128)} %broadcast_in_dim.33), calls=%async_computation.3 | async-start | bytes 98304 | tf_op jit(solution)/shard_map/all_to_all | solution.py:69

commit v5 on v4

--- a/solution.py
+++ b/solution.py
@@ -109,6 +109,28 @@
     return tuple(outs)
 
 
+def one_hot(index, count):
+    return (index[:, None] == jnp.arange(count, dtype=index.dtype)[None, :]).astype(jnp.bfloat16)
+
+
+def select_rows(pick, table):
+    if table.dtype == jnp.bfloat16:
+        return jnp.dot(pick, table, preferred_element_type=jnp.float32).astype(jnp.bfloat16)
+    return jnp.dot(
+        pick.astype(jnp.float32), table, precision=lax.Precision.HIGHEST, preferred_element_type=jnp.float32
+    )
+
+
+def sum_rows(pick, values):
+    return lax.dot_general(
+        pick.astype(jnp.float32),
+        values,
+        (((0,), (0,)), ((), ())),
+        precision=lax.Precision.HIGHEST,
+        preferred_element_type=jnp.float32,
+    )
+
+
 def shards(
     node_feat,
     edge_feat,
@@ -143,13 +165,17 @@
     active = (jnp.arange(edge_dst.shape[0], dtype=jnp.int32) < edge_count[0]).astype(jnp.float32)[
         :, None
     ]
-    inputs = jnp.concatenate([edge_feat, padded[source_pad], padded[target_pad]], axis=1)
+    padded_count = padded_side * padded_side
+    pick_source = one_hot(source_pad, padded_count)
+    pick_target = one_hot(target_pad, padded_count)
+    pick_local = one_hot(edge_dst, block_side * block_side)
+    inputs = jnp.concatenate(
+        [edge_feat, select_rows(pick_source, padded), select_rows(pick_target, padded)], axis=1
+    )
     pre_e, hidden_e, normed_e, inv_e, message = mlp_forward(
         inputs, full_edge_in, full_edge_out, gain_edge
     )
-    aggregate = jax.ops.segment_sum(
-        message * active, edge_dst, num_segments=block_side * block_side
-    )
+    aggregate = sum_rows(pick_local, message * active)
     node_rows = node_feat.reshape(block_side * block_side, latent)
     node_input = jnp.concatenate([node_rows, aggregate.astype(jnp.bfloat16)], axis=1)
     pre_n, hidden_n, normed_n, inv_n, _ = mlp_forward(
@@ -168,17 +194,14 @@
         full_node_out,
     )
     cot_float = edge_cot.astype(jnp.float32)
-    upstream = active * (cot_float + node_in_grad[:, latent:][edge_dst])
+    upstream = active * (cot_float + select_rows(pick_local, node_in_grad[:, latent:]))
     edge_in_grad, edge_first, edge_second, edge_gain = mlp_backward(
         upstream, inputs, pre_e, hidden_e, normed_e, inv_e, gain_edge, full_edge_in, full_edge_out
     )
     edge_grad = (cot_float + edge_in_grad[:, :latent]).astype(jnp.bfloat16)
-    spread = jnp.zeros((padded_side * padded_side, latent), jnp.float32)
-    spread = (
-        spread.at[source_pad]
-        .add(edge_in_grad[:, latent : 2 * latent])
-        .at[target_pad]
-        .add(edge_in_grad[:, 2 * latent :])
+    spread = sum_rows(
+        jnp.concatenate([pick_source, pick_target], axis=0),
+        jnp.concatenate([edge_in_grad[:, latent : 2 * latent], edge_in_grad[:, 2 * latent :]], axis=0),
     )
     spread = spread.reshape(padded_side, padded_side, latent)
     outgoing = jnp.stack(

time: 197 us -> 173 us (0.88)
  other arithmetic: 25.1 us -> 5.99 us
  waiting for transfers between devices: 33.5 us -> 48.7 us
  local copies, waits for them, and re-layouts: 33.6 us -> 18.5 us
  starting transfers between devices: 91.8 us -> 78.6 us
  matrix products: 9.34 us -> 17.8 us
    scatter-add x3 -> x0, other arithmetic: 20.5 us -> none  [the longest x2 13.9 us: shards(): spread = spread.at[source_pad].add(edge_in_grad[:, latent:2 * latent]).at...]
    ppermute x4, waiting for transfers between devices: 0.01 us -> 15.2 us  [with_halo(): lax.ppermute(lax.slice_in_dim(block, block.shape[dim] - width, None, axis...]
    dot_general x0 -> x5, matrix products: none -> 11.8 us  [the longest x2 7.69 us: sum_rows(): lax.dot_general(pick.astype(jnp.float32), values, (((0,), (0,)), ((), ())...]
    all_to_all x1, starting transfers between devices: 23.4 us -> 11.6 us  [sum_sub(): piece = jnp.sum(lax.all_to_all(flat, 'sub', 0, 0, tiled=True), axis=0)]
    gather x4 -> x0, local copies, waits for them, and re-layouts: 11.6 us -> none  [the longest x2 5.23 us: shards(): upstream = active * (cot_float + node_in_grad[:, latent:][edge_dst])]
    eq x0 -> x1, other arithmetic: none -> 2.08 us  [one_hot(): index[:, None] == jnp.arange(count, dtype=index.dtype)[None, :]]
    unnamed x48 -> x47, local copies, waits for them, and re-layouts: 10.2 us -> 8.56 us
  transfers between devices with their start and end apart: 12 -> 12, of which waited for: 4 -> 5; matrix products, arithmetic and copies ran while one was open for 9% -> 7% of each run, Pallas kernels for 0% -> 0%
where the time goes in v5:
time: 173 us; the launch traced here: 172 us
  starting transfers between devices  78.6 us (45%)
  waiting for transfers between devices  48.7 us (28%)
  local copies, waits for them, and re-layouts  18.5 us (11%)
  matrix products  17.8 us (10%)
  other arithmetic  5.99 us (3%)
  between operations  2.02 us (1%)
    ppermute x4, starting transfers between devices, with_halo(): lax.ppermute(lax.slice_in_dim(block, 0, width, axis=dim), axis, backward)  27.1 us
    ppermute x4, waiting for transfers between devices, with_halo(): lax.ppermute(lax.slice_in_dim(block, block.shape[dim] - width, None, axis...  15.2 us
    all_to_all x1, waiting for transfers between devices, sum_sub(): piece = jnp.sum(lax.all_to_all(flat, 'sub', 0, 0, tiled=True), axis=0)  13.2 us
    all_to_all x1, starting transfers between devices, gather_dom(): return lax.all_to_all(spread, 'dom', 0, 0, tiled=True)  13 us
    all_to_all x1, waiting for transfers between devices, sum_sub(): return lax.all_to_all(spread, 'sub', 0, 0, tiled=True).reshape(value.shape)  12.5 us
    all_to_all x1, starting transfers between devices, reduce_scatter_dom(): return jnp.sum(lax.all_to_all(packed, 'dom', 0, 0, tiled=True), axis=0)  12 us
    all_to_all x1, starting transfers between devices, sum_sub(): piece = jnp.sum(lax.all_to_all(flat, 'sub', 0, 0, tiled=True), axis=0)  11.6 us
    ppermute x4, starting transfers between devices, with_halo(): lax.ppermute(lax.slice_in_dim(block, block.shape[dim] - width, None, axis...  10.2 us
  transfers between devices with their start and end apart: 12, of which 5 were waited for; matrix products, arithmetic and copies ran while one was open for 7% of the time, Pallas kernels for 0%

profile of v5, /device:TPU:6, one launch (start us, length us, event | category | flops | bytes accessed | tf_op | source)
XLA Modules:
  0.0 171.6 jit_solution(7576813789548212203)
XLA Ops:
  0.7 0.8 fusion.59
  1.4 14.8 %collective-permute-start.1 = (bf16[1,24,128]{2,1,0:T(8,128)(2,1)S(1)}, bf16[1,24,128]{2,1,0:T(8,128)(2,1)S(1)}, u32[]{:S(2)}, u32[]{:S(2)}) collective-permute-start(bf16[1,24,128]{2,1,0:T(8,128)(2,1)S(1)} %get-tuple-element.97), channel_id=1, source_target_pairs={{48,0},{96,48},{144,96},{192,144},{240,192},{288,240},{336,288},{3... | collective-permute-start | bytes 18440 | tf_op jit(solution)/shard_map/ppermute | solution.py:15
  16.3 1.9 %collective-permute-start = (bf16[1,24,128]{2,1,0:T(8,128)(2,1)S(1)}, bf16[1,24,128]{2,1,0:T(8,128)(2,1)S(1)}, u32[]{:S(2)}, u32[]{:S(2)}) collective-permute-start(bf16[1,24,128]{2,1,0:T(8,128)(2,1)S(1)} %get-tuple-element.98), channel_id=1, source_target_pairs={{0,48},{48,96},{96,144},{144,192},{192,240},{240,288},{288,336},{3... | collective-permute-start | bytes 18440 | tf_op jit(solution)/shard_map/ppermute | solution.py:12
  18.2 0.7 reshape.280
  18.9 0.7 constant_dynamic-update-slice_fusion.7
  19.6 0.7 constant_dynamic-update-slice_fusion.6
  20.3 0.7 constant_dynamic-update-slice_fusion.5
  21.0 0.7 constant_dynamic-update-slice_fusion.4
  21.7 0.8 broadcast_in_dim.15
  22.5 13.0 %all-to-all-start = ((bf16[16,57,128]{2,1,0:T(8,128)(2,1)}), bf16[16,57,128]{2,1,0:T(8,128)(2,1)S(1)}, u32[]{:S(2)}, u32[]{:S(2)}) async-start(bf16[16,57,128]{2,1,0:T(8,128)(2,1)} %broadcast_in_dim.15), calls=%async_computation | async-start | bytes 524288 | tf_op jit(solution)/shard_map/all_to_all | solution.py:57
  35.5 0.7 select_add_fusion
  36.2 2.1 %iota_compare_fusion = (pred[1024,676]{1,0:T(32,128)(4,1)}, pred[1024,676]{1,0:T(32,128)(4,1)}) fusion(s32[1024]{0:T(1024)S(1)} %get-tuple-element.108, s32[1024]{0:T(1024)S(1)} %get-tuple-element.107), kind=kLoop, calls=%fused_computation.4 | loop fusion | flops 1384448 | bytes 1392640 | tf_op jit(solution)/shard_map/eq | solution.py:113
  39.1 3.5 %collective-permute-start.2 = (bf16[26,1,128]{2,1,0:T(2,128)(2,1)S(1)}, bf16[26,1,128]{2,1,0:T(2,128)(2,1)S(1)}, u32[]{:S(2)}, u32[]{:S(2)}) collective-permute-start(bf16[26,1,128]{2,1,0:T(2,128)(2,1)S(1)} %get-tuple-element.95), channel_id=1, source_target_pairs={{0,1},{1,2},{2,3},{3,4},{4,5},{5,6},{6,7},{7,8},{8,9},{9,10},{10,1... | collective-permute-start | bytes 19976 | tf_op jit(solution)/shard_map/ppermute | solution.py:12
  42.6 1.3 collective-permute-start.3
  44.2 4.0 %collective-permute-done.3 = bf16[26,1,128]{2,1,0:T(2,128)(2,1)S(1)} collective-permute-done((bf16[26,1,128]{2,1,0:T(2,128)(2,1)S(1)}, bf16[26,1,128]{2,1,0:T(2,128)(2,1)S(1)}, u32[]{:S(2)}, u32[]{:S(2)}) %collective-permute-start.3) | collective-permute-done | bytes 6688 | tf_op jit(solution)/shard_map/ppermute | solution.py:15
  48.3 0.8 convolution_convert_fusion
  49.2 0.8 convolution_convert_fusion.1
  50.4 0.2 fusion.28
  50.8 0.4 fusion.26
  51.3 0.3 fusion.62
  51.7 1.7 fusion.14
  53.4 0.2 fusion.36
  53.6 0.3 fusion.63
  54.0 0.3 multiply_reduce_fusion.5
  54.3 0.8 fusion.29
  55.0 0.4 multiply_convert_fusion.1
  55.4 0.2 fusion.13
  55.6 1.0 fusion.35
  56.5 0.2 fusion.64
  56.8 2.4 %multiply_reduce_fusion = (f32[128]{0:T(128)}, f32[1024]{0:T(1024)S(1)}, f32[1024]{0:T(1024)S(1)}, f32[1024,128]{0,1:T(8,128)S(1)}) fusion(f32[1024,128]{0,1:T(8,128)S(1)} %get-tuple-element.110, f32[1024]{0:T(1024)S(1)} %add_rsqrt_fusion.1, f32[1024]{0:T(1024)S(1)} %broadcast_multiply_fusion.5, f32[128]{0:T(128)S(1)} %reshape.297, ...), kind=kOutput, calls=%fused_computation.31 | convolution fusion | flops 907999104 | bytes 1631232 | tf_op jit(solution)/shard_map/dot_general | solution.py:119
  59.2 0.9 multiply_convert_fusion
  60.1 0.3 fusion.12
  60.4 1.1 fusion.25
  61.4 0.4 fusion.65
  61.9 1.0 copy-done.1
  62.9 0.2 copy-done.2
  63.1 6.0 %fusion = f32[676,128]{1,0:T(8,128)} fusion(pred[1024,676]{1,0:T(32,128)(4,1)S(1)} %copy-done.1, pred[1024,676]{1,0:T(32,128)(4,1)S(1)} %copy-done.2, f32[1024,128]{1,0:T(8,128)S(1)} %get-tuple-element.89, f32[1024,128]{1,0:T(8,128)S(1)} %get-tuple-element.90), kind=kOutput, calls=%fused_computation | convolution fusion | flops 2128158720 | bytes 2779136 | tf_op jit(solution)/shard_map/dot_general | solution.py:125
  69.1 1.0 reshape.286
  70.6 0.7 constant_dynamic-update-slice_fusion.9
  71.3 0.9 fusion.18
  72.3 1.6 constant_dynamic-update-slice_fusion.8
  73.9 0.9 fusion.17
  74.7 1.5 dynamic-update-slice.16
  76.3 12.0 %all-to-all-start.1 = ((f32[16,57,128]{2,1,0:T(8,128)}), f32[16,57,128]{2,1,0:T(8,128)S(1)}, u32[]{:S(2)}, u32[]{:S(2)}) async-start(f32[16,57,128]{2,1,0:T(8,128)} %dynamic-update-slice.16), calls=%async_computation.1 | async-start | bytes 1048576 | tf_op jit(solution)/shard_map/all_to_all | solution.py:61
  88.3 0.2 copy.69
  88.5 9.7 %collective-permute-start.5 = (bf16[1,2,24,128]{3,2,1,0:T(8,128)(2,1)S(1)}, bf16[1,2,24,128]{3,2,1,0:T(8,128)(2,1)S(1)}, u32[]{:S(2)}, u32[]{:S(2)}) collective-permute-start(bf16[1,2,24,128]{3,2,1,0:T(8,128)(2,1)S(1)} %maximum_bitcast_fusion.2), channel_id=1, source_target_pairs={{48,0},{96,48},{144,96},{192,144},{240,192},{288,240},{336,288},{3... | collective-permute-start | bytes 36872 | tf_op jit(solution)/shard_map/ppermute | solution.py:15
  98.3 1.9 %collective-permute-start.4 = (bf16[1,2,24,128]{3,2,1,0:T(8,128)(2,1)S(1)}, bf16[1,2,24,128]{3,2,1,0:T(8,128)(2,1)S(1)}, u32[]{:S(2)}, u32[]{:S(2)}) collective-permute-start(bf16[1,2,24,128]{3,2,1,0:T(8,128)(2,1)S(1)} %maximum_bitcast_fusion.1), channel_id=1, source_target_pairs={{0,48},{48,96},{96,144},{144,192},{192,240},{240,288},{288,336},{3... | collective-permute-start | bytes 36872 | tf_op jit(solution)/shard_map/ppermute | solution.py:12
  100.3 15.2 %collective-permute-done.4 = bf16[1,2,24,128]{3,2,1,0:T(8,128)(2,1)S(1)} collective-permute-done((bf16[1,2,24,128]{3,2,1,0:T(8,128)(2,1)S(1)}, bf16[1,2,24,128]{3,2,1,0:T(8,128)(2,1)S(1)}, u32[]{:S(2)}, u32[]{:S(2)}) %collective-permute-start.4) | collective-permute-done | bytes 12320 | tf_op jit(solution)/shard_map/ppermute | solution.py:12
  115.5 2.9 %collective-permute-start.6 = (bf16[4,1,24,128]{3,2,1,0:T(8,128)(2,1)S(1)}, bf16[4,1,24,128]{3,2,1,0:T(8,128)(2,1)S(1)}, u32[]{:S(2)}, u32[]{:S(2)}) collective-permute-start(bf16[4,1,24,128]{3,2,1,0:T(8,128)(2,1)S(1)} %get-tuple-element.101), channel_id=1, source_target_pairs={{0,1},{1,2},{2,3},{3,4},{4,5},{5,6},{6,7},{7,8},{8,9},{9,10},{10,1... | collective-permute-start | bytes 73736 | tf_op jit(solution)/shard_map/ppermute | solution.py:12
  118.4 1.3 collective-permute-start.7
  119.8 0.8 copy.64
  120.7 3.8 %collective-permute-done.7 = bf16[4,1,24,128]{3,2,1,0:T(8,128)(2,1)S(1)} collective-permute-done((bf16[4,1,24,128]{3,2,1,0:T(8,128)(2,1)S(1)}, bf16[4,1,24,128]{3,2,1,0:T(8,128)(2,1)S(1)}, u32[]{:S(2)}, u32[]{:S(2)}) %collective-permute-start.7) | collective-permute-done | bytes 24608 | tf_op jit(solution)/shard_map/ppermute | solution.py:15
  124.8 0.8 all_to_all.18
  125.5 11.6 %all-to-all-start.2 = ((f32[48,1,152]{2,1,0:T(1,128)}), f32[48,1,152]{2,1,0:T(1,128)S(1)}, u32[]{:S(2)}, u32[]{:S(2)}) async-start(f32[48,1,152]{2,1,0:T(1,128)} %all_to_all.18), calls=%async_computation.2 | async-start | bytes 98304 | tf_op jit(solution)/shard_map/all_to_all | solution.py:67
  137.2 13.2 %all-to-all-done.2 = f32[48,1,152]{2,1,0:T(1,128)S(1)} async-done(((f32[48,1,152]{2,1,0:T(1,128)}), f32[48,1,152]{2,1,0:T(1,128)S(1)}, u32[]{:S(2)}, u32[]{:S(2)}) %all-to-all-start.2) | async-done | bytes 29216 | tf_op jit(solution)/shard_map/all_to_all | solution.py:67
  150.5 0.6 broadcast_in_dim.16
  151.1 4.5 %all-to-all-start.3 = ((f32[48,1,152]{2,1,0:T(1,128)}), f32[48,1,152]{2,1,0:T(1,128)S(1)}, u32[]{:S(2)}, u32[]{:S(2)}) async-start(f32[48,1,152]{2,1,0:T(1,128)} %broadcast_in_dim.16), calls=%async_computation.3 | async-start | bytes 98304 | tf_op jit(solution)/shard_map/all_to_all | solution.py:69
  155.7 0.7 copy.63
  156.4 12.5 %all-to-all-done.3 = f32[48,1,152]{2,1,0:T(1,128)S(1)} async-done(((f32[48,1,152]{2,1,0:T(1,128)}), f32[48,1,152]{2,1,0:T(1,128)S(1)}, u32[]{:S(2)}, u32[]{:S(2)}) %all-to-all-start.3) | async-done | bytes 29216 | tf_op jit(solution)/shard_map/all_to_all | solution.py:69
  168.9 0.1 multiply_reduce_fusion.6
  169.2 0.6 slice.256
  169.8 0.6 fusion.61
  170.4 0.6 slice.254
  171.0 0.6 reshape_squeeze.7
  (97 shorter events, 2.5 us)
Async XLA Ops:
  0.6 38.3 %copy-start.3 = (bf16[24,24,128]{2,1,0:T(8,128)(2,1)S(1)}, bf16[24,24,128]{2,1,0:T(8,128)(2,1)}, u32[]{:S(2)}) copy-start(bf16[24,24,128]{2,1,0:T(8,128)(2,1)} %param.20) | copy-start | bytes 442372
  0.6 43.2 %copy-start.4 = (bf16[1024,128]{1,0:T(8,128)(2,1)S(1)}, bf16[1024,128]{1,0:T(8,128)(2,1)}, u32[]{:S(2)}) copy-start(bf16[1024,128]{1,0:T(8,128)(2,1)} %param.21) | copy-start | bytes 786436
  1.4 37.6 %collective-permute-start.1 = (bf16[1,24,128]{2,1,0:T(8,128)(2,1)S(1)}, bf16[1,24,128]{2,1,0:T(8,128)(2,1)S(1)}, u32[]{:S(2)}, u32[]{:S(2)}) collective-permute-start(bf16[1,24,128]{2,1,0:T(8,128)(2,1)S(1)} %get-tuple-element.97), channel_id=1, source_target_pairs={{48,0},{96,48},{144,96},{192,144},{240,192},{288,240},{336,288},{3... | collective-permute-start | bytes 18440 | tf_op jit(solution)/shard_map/ppermute | solution.py:15
  16.3 22.7 %collective-permute-start = (bf16[1,24,128]{2,1,0:T(8,128)(2,1)S(1)}, bf16[1,24,128]{2,1,0:T(8,128)(2,1)S(1)}, u32[]{:S(2)}, u32[]{:S(2)}) collective-permute-start(bf16[1,24,128]{2,1,0:T(8,128)(2,1)S(1)} %get-tuple-element.98), channel_id=1, source_target_pairs={{0,48},{48,96},{96,144},{144,192},{192,240},{240,288},{288,336},{3... | collective-permute-start | bytes 18440 | tf_op jit(solution)/shard_map/ppermute | solution.py:12
  22.4 21.6 %copy-start.5 = (bf16[1024,128]{1,0:T(8,128)(2,1)S(1)}, bf16[1024,128]{1,0:T(8,128)(2,1)}, u32[]{:S(2)}) copy-start(bf16[1024,128]{1,0:T(8,128)(2,1)} %param.31) | copy-start | bytes 786436
  22.5 27.6 %all-to-all-start = ((bf16[16,57,128]{2,1,0:T(8,128)(2,1)}), bf16[16,57,128]{2,1,0:T(8,128)(2,1)S(1)}, u32[]{:S(2)}, u32[]{:S(2)}) async-start(bf16[16,57,128]{2,1,0:T(8,128)(2,1)} %broadcast_in_dim.15), calls=%async_computation | async-start | bytes 524288 | tf_op jit(solution)/shard_map/all_to_all | solution.py:57
  39.1 5.1 %collective-permute-start.2 = (bf16[26,1,128]{2,1,0:T(2,128)(2,1)S(1)}, bf16[26,1,128]{2,1,0:T(2,128)(2,1)S(1)}, u32[]{:S(2)}, u32[]{:S(2)}) collective-permute-start(bf16[26,1,128]{2,1,0:T(2,128)(2,1)S(1)} %get-tuple-element.95), channel_id=1, source_target_pairs={{0,1},{1,2},{2,3},{3,4},{4,5},{5,6},{6,7},{7,8},{8,9},{9,10},{10,1... | collective-permute-start | bytes 19976 | tf_op jit(solution)/shard_map/ppermute | solution.py:12
  42.6 5.6 %collective-permute-start.3 = (bf16[26,1,128]{2,1,0:T(2,128)(2,1)S(1)}, bf16[26,1,128]{2,1,0:T(2,128)(2,1)S(1)}, u32[]{:S(2)}, u32[]{:S(2)}) collective-permute-start(bf16[26,1,128]{2,1,0:T(2,128)(2,1)S(1)} %get-tuple-element.96), channel_id=1, source_target_pairs={{1,0},{2,1},{3,2},{4,3},{5,4},{6,5},{7,6},{8,7},{9,8},{10,9},{11,1... | collective-permute-start | bytes 19976 | tf_op jit(solution)/shard_map/ppermute | solution.py:15
  48.3 2.0 %copy-start = (bf16[24,24,128]{2,1,0:T(8,128)(2,1)S(1)}, bf16[24,24,128]{2,1,0:T(8,128)(2,1)}, u32[]{:S(2)}) copy-start(bf16[24,24,128]{2,1,0:T(8,128)(2,1)} %param.30) | copy-start | bytes 442372
  49.2 2.1 %copy-start.11 = (bf16[1024,128]{0,1:T(8,128)(2,1)}, bf16[1024,128]{0,1:T(8,128)(2,1)S(1)}, u32[]{:S(2)}) copy-start(bf16[1024,128]{0,1:T(8,128)(2,1)S(1)} %convolution_convert_fusion) | copy-start | bytes 786436
  50.0 1.2 copy-start.13
  50.7 6.1 %copy-start.8 = (f32[128]{0:T(128)}, f32[128]{0:T(128)S(1)}, u32[]{:S(2)}) copy-start(f32[128]{0:T(128)S(1)} %reshape.297) | copy-start | bytes 1540
  50.8 0.8 copy-start.7
  59.2 1.1 copy-start.12
  59.2 1.2 copy-start.14
  61.8 1.1 copy-start.1
  61.8 1.4 copy-start.2
  63.1 7.1 %copy-start.9 = (f32[128]{0:T(128)S(1)}, f32[128]{0:T(128)}, u32[]{:S(2)}) copy-start(f32[128]{0:T(128)} %get-tuple-element.86) | copy-start | bytes 1540
  63.1 7.2 %copy-start.10 = (f32[128]{0:T(128)S(1)}, f32[128]{0:T(128)}, u32[]{:S(2)}) copy-start(f32[128]{0:T(128)} %get-tuple-element.83) | copy-start | bytes 1540
  69.1 1.5 copy-start.6
  76.3 48.5 %all-to-all-start.1 = ((f32[16,57,128]{2,1,0:T(8,128)}), f32[16,57,128]{2,1,0:T(8,128)S(1)}, u32[]{:S(2)}, u32[]{:S(2)}) async-start(f32[16,57,128]{2,1,0:T(8,128)} %dynamic-update-slice.16), calls=%async_computation.1 | async-start | bytes 1048576 | tf_op jit(solution)/shard_map/all_to_all | solution.py:61
  88.5 11.7 %collective-permute-start.5 = (bf16[1,2,24,128]{3,2,1,0:T(8,128)(2,1)S(1)}, bf16[1,2,24,128]{3,2,1,0:T(8,128)(2,1)S(1)}, u32[]{:S(2)}, u32[]{:S(2)}) collective-permute-start(bf16[1,2,24,128]{3,2,1,0:T(8,128)(2,1)S(1)} %maximum_bitcast_fusion.2), channel_id=1, source_target_pairs={{48,0},{96,48},{144,96},{192,144},{240,192},{288,240},{336,288},{3... | collective-permute-start | bytes 36872 | tf_op jit(solution)/shard_map/ppermute | solution.py:15
  98.3 17.2 %collective-permute-start.4 = (bf16[1,2,24,128]{3,2,1,0:T(8,128)(2,1)S(1)}, bf16[1,2,24,128]{3,2,1,0:T(8,128)(2,1)S(1)}, u32[]{:S(2)}, u32[]{:S(2)}) collective-permute-start(bf16[1,2,24,128]{3,2,1,0:T(8,128)(2,1)S(1)} %maximum_bitcast_fusion.1), channel_id=1, source_target_pairs={{0,48},{48,96},{96,144},{144,192},{192,240},{240,288},{288,336},{3... | collective-permute-start | bytes 36872 | tf_op jit(solution)/shard_map/ppermute | solution.py:12
  115.5 5.2 %collective-permute-start.6 = (bf16[4,1,24,128]{3,2,1,0:T(8,128)(2,1)S(1)}, bf16[4,1,24,128]{3,2,1,0:T(8,128)(2,1)S(1)}, u32[]{:S(2)}, u32[]{:S(2)}) collective-permute-start(bf16[4,1,24,128]{3,2,1,0:T(8,128)(2,1)S(1)} %get-tuple-element.101), channel_id=1, source_target_pairs={{0,1},{1,2},{2,3},{3,4},{4,5},{5,6},{6,7},{7,8},{8,9},{9,10},{10,1... | collective-permute-start | bytes 73736 | tf_op jit(solution)/shard_map/ppermute | solution.py:12
  118.4 6.1 %collective-permute-start.7 = (bf16[4,1,24,128]{3,2,1,0:T(8,128)(2,1)S(1)}, bf16[4,1,24,128]{3,2,1,0:T(8,128)(2,1)S(1)}, u32[]{:S(2)}, u32[]{:S(2)}) collective-permute-start(bf16[4,1,24,128]{3,2,1,0:T(8,128)(2,1)S(1)} %get-tuple-element.102), channel_id=1, source_target_pairs={{1,0},{2,1},{3,2},{4,3},{5,4},{6,5},{7,6},{8,7},{9,8},{10,9},{11,1... | collective-permute-start | bytes 73736 | tf_op jit(solution)/shard_map/ppermute | solution.py:15
  125.5 24.9 %all-to-all-start.2 = ((f32[48,1,152]{2,1,0:T(1,128)}), f32[48,1,152]{2,1,0:T(1,128)S(1)}, u32[]{:S(2)}, u32[]{:S(2)}) async-start(f32[48,1,152]{2,1,0:T(1,128)} %all_to_all.18), calls=%async_computation.2 | async-start | bytes 98304 | tf_op jit(solution)/shard_map/all_to_all | solution.py:67
  151.1 17.8 %all-to-all-start.3 = ((f32[48,1,152]{2,1,0:T(1,128)}), f32[48,1,152]{2,1,0:T(1,128)S(1)}, u32[]{:S(2)}, u32[]{:S(2)}) async-start(f32[48,1,152]{2,1,0:T(1,128)} %broadcast_in_dim.16), calls=%async_computation.3 | async-start | bytes 98304 | tf_op jit(solution)/shard_map/all_to_all | solution.py:69

commit v6 on v5

--- a/solution.py
+++ b/solution.py
@@ -63,10 +63,8 @@
 
 def sum_sub(value):
     count = lax.axis_size("sub")
-    flat = value.reshape(count, -1)
-    piece = jnp.sum(lax.all_to_all(flat, "sub", 0, 0, tiled=True), axis=0)
-    spread = jnp.broadcast_to(piece[None], flat.shape)
-    return lax.all_to_all(spread, "sub", 0, 0, tiled=True).reshape(value.shape)
+    spread = jnp.broadcast_to(value[None], (count,) + value.shape)
+    return jnp.sum(lax.all_to_all(spread, "sub", 0, 0, tiled=True), axis=0)
 
 
 def gather_params(weights, gains):

time: 173 us -> 179 us (1.035)
  the two profiles are of different devices: /device:TPU:6 before, /device:TPU:154 now
where the time goes in v6:
time: 179 us; the launch traced here: 178 us
  starting transfers between devices  62.8 us (35%)
  waiting for transfers between devices  40.9 us (23%)
  blocking collectives  36.2 us (20%)
  local copies, waits for them, and re-layouts  15.7 us (9%)
  matrix products  14.5 us (8%)
  other arithmetic  5.55 us (3%)
  between operations  1.98 us (1%)
    all_to_all x1, blocking collectives, reduce_scatter_dom(): return jnp.sum(lax.all_to_all(packed, 'dom', 0, 0, tiled=True), axis=0)  36.2 us
    ppermute x4, waiting for transfers between devices, with_halo(): lax.ppermute(lax.slice_in_dim(block, block.shape[dim] - width, None, axis...  32.6 us
    ppermute x4, starting transfers between devices, with_halo(): lax.ppermute(lax.slice_in_dim(block, 0, width, axis=dim), axis, backward)  26.8 us
    all_to_all x1, starting transfers between devices, gather_dom(): return lax.all_to_all(spread, 'dom', 0, 0, tiled=True)  12.9 us
    ppermute x4, starting transfers between devices, with_halo(): lax.ppermute(lax.slice_in_dim(block, block.shape[dim] - width, None, axis...  12.7 us
    all_to_all x1, starting transfers between devices, sum_sub(): return jnp.sum(lax.all_to_all(spread, 'sub', 0, 0, tiled=True), axis=0)  10.4 us
    dot_general x2, matrix products, sum_rows(): lax.dot_general(pick.astype(jnp.float32), values, (((0,), (0,)), ((), ())...  7.5 us
    unnamed x37, local copies, waits for them, and re-layouts  7.44 us
  transfers between devices with their start and end apart: 10, of which 4 were waited for; matrix products, arithmetic and copies ran while one was open for 12% of the time, Pallas kernels for 0%

profile of v6, /device:TPU:154, one launch (start us, length us, event | category | flops | bytes accessed | tf_op | source)
XLA Modules:
  0.0 177.7 jit_solution(6723989832181619364)
XLA Ops:
  0.6 0.8 fusion.59
  1.4 1.9 %collective-permute-start = (bf16[1,24,128]{2,1,0:T(8,128)(2,1)S(1)}, bf16[1,24,128]{2,1,0:T(8,128)(2,1)S(1)}, u32[]{:S(2)}, u32[]{:S(2)}) collective-permute-start(bf16[1,24,128]{2,1,0:T(8,128)(2,1)S(1)} %get-tuple-element.105), channel_id=1, source_target_pairs={{0,48},{48,96},{96,144},{144,192},{192,240},{240,288},{288,336},{3... | collective-permute-start | bytes 18440 | tf_op jit(solution)/shard_map/ppermute | solution.py:12
  3.3 12.1 %collective-permute-start.1 = (bf16[1,24,128]{2,1,0:T(8,128)(2,1)S(1)}, bf16[1,24,128]{2,1,0:T(8,128)(2,1)S(1)}, u32[]{:S(2)}, u32[]{:S(2)}) collective-permute-start(bf16[1,24,128]{2,1,0:T(8,128)(2,1)S(1)} %get-tuple-element.104), channel_id=1, source_target_pairs={{48,0},{96,48},{144,96},{192,144},{240,192},{288,240},{336,288},{3... | collective-permute-start | bytes 18440 | tf_op jit(solution)/shard_map/ppermute | solution.py:15
  15.5 0.7 constant_dynamic-update-slice_fusion.7
  16.2 0.7 reshape.267
  16.9 0.7 constant_dynamic-update-slice_fusion.6
  17.6 0.7 constant_dynamic-update-slice_fusion.5
  18.3 0.7 constant_dynamic-update-slice_fusion.4
  19.0 0.8 broadcast_in_dim.15
  19.7 12.9 %all-to-all-start = ((bf16[16,57,128]{2,1,0:T(8,128)(2,1)}), bf16[16,57,128]{2,1,0:T(8,128)(2,1)S(1)}, u32[]{:S(2)}, u32[]{:S(2)}) async-start(bf16[16,57,128]{2,1,0:T(8,128)(2,1)} %broadcast_in_dim.15), calls=%async_computation | async-start | bytes 524288 | tf_op jit(solution)/shard_map/all_to_all | solution.py:57
  32.7 0.7 select_add_fusion
  34.0 0.9 constant_dynamic-update-slice_fusion.1
  35.0 4.7 %collective-permute-start.2 = (bf16[26,1,128]{2,1,0:T(2,128)(2,1)S(1)}, bf16[26,1,128]{2,1,0:T(2,128)(2,1)S(1)}, u32[]{:S(2)}, u32[]{:S(2)}) collective-permute-start(bf16[26,1,128]{2,1,0:T(2,128)(2,1)S(1)} %get-tuple-element.102), channel_id=1, source_target_pairs={{0,1},{1,2},{2,3},{3,4},{4,5},{5,6},{6,7},{7,8},{8,9},{9,10},{10,1... | collective-permute-start | bytes 19976 | tf_op jit(solution)/shard_map/ppermute | solution.py:12
  39.7 1.9 %collective-permute-start.3 = (bf16[26,1,128]{2,1,0:T(2,128)(2,1)S(1)}, bf16[26,1,128]{2,1,0:T(2,128)(2,1)S(1)}, u32[]{:S(2)}, u32[]{:S(2)}) collective-permute-start(bf16[26,1,128]{2,1,0:T(2,128)(2,1)S(1)} %get-tuple-element.103), channel_id=1, source_target_pairs={{1,0},{2,1},{3,2},{4,3},{5,4},{6,5},{7,6},{8,7},{9,8},{10,9},{11,1... | collective-permute-start | bytes 19976 | tf_op jit(solution)/shard_map/ppermute | solution.py:15
  41.7 1.1 copy.65
  42.8 0.1 copy.69
  43.0 3.6 %collective-permute-done.3 = bf16[26,1,128]{2,1,0:T(2,128)(2,1)S(1)} collective-permute-done((bf16[26,1,128]{2,1,0:T(2,128)(2,1)S(1)}, bf16[26,1,128]{2,1,0:T(2,128)(2,1)S(1)}, u32[]{:S(2)}, u32[]{:S(2)}) %collective-permute-start.3) | collective-permute-done | bytes 6688 | tf_op jit(solution)/shard_map/ppermute | solution.py:15
  46.6 0.1 pad_maximum_fusion.4
  46.7 0.8 convolution_convert_fusion
  47.6 0.8 convolution_convert_fusion.1
  48.5 1.6 all-to-all-done
  50.4 0.2 fusion.28
  50.6 0.4 fusion.26
  51.0 0.3 fusion.62
  51.5 1.7 fusion.14
  53.3 0.2 fusion.36
  53.5 0.3 fusion.63
  53.9 0.3 multiply_reduce_fusion.5
  54.1 0.3 fusion.29
  54.6 0.4 multiply_convert_fusion.1
  55.0 0.2 fusion.13
  55.2 0.2 fusion.64
  55.4 0.3 fusion.35
  55.7 1.9 %multiply_reduce_fusion = (f32[128]{0:T(128)S(1)}, f32[1024]{0:T(1024)S(1)}, f32[1024]{0:T(1024)S(1)}, f32[1024,128]{0,1:T(8,128)S(1)}) fusion(f32[1024,128]{0,1:T(8,128)S(1)} %get-tuple-element.117, f32[1024]{0:T(1024)S(1)} %add_rsqrt_fusion.1, f32[1024]{0:T(1024)S(1)} %broadcast_multiply_fusion.6, f32[128]{0:T(128)S(1)} %reshape.284, ...), kind=kOutput, calls=%fused_computation.31 | convolution fusion | flops 907999104 | bytes 1631232 | tf_op jit(solution)/shard_map/dot_general | solution.py:117
  57.6 0.2 multiply_convert_fusion
  57.8 0.3 fusion.12
  58.1 0.5 copy-done.7
  58.6 0.4 fusion.25
  59.0 0.3 fusion.18
  59.3 0.2 fusion.17
  60.0 36.2 %all_to_all.15 = f32[16,57,128]{2,1,0:T(8,128)S(1)} all-to-all(f32[16,57,128]{2,1,0:T(8,128)S(1)} %dynamic-update-slice.16), channel_id=1, replica_groups=mesh['dom'=16,'sub'=48] {'dom'}, dimensions={0} | all-to-all | bytes 933888 | tf_op jit(solution)/shard_map/all_to_all | solution.py:61
  96.3 1.3 broadcast_in_dim.16
  97.6 10.4 %all-to-all-start.2 = ((f32[48,57,128]{2,1,0:T(8,128)}), f32[48,57,128]{2,1,0:T(8,128)S(1)}, u32[]{:S(2)}, u32[]{:S(2)}) async-start(f32[48,57,128]{2,1,0:T(8,128)} %broadcast_in_dim.16), calls=%async_computation.2 | async-start | bytes 3145728 | tf_op jit(solution)/shard_map/all_to_all | solution.py:67
  108.0 1.2 iota_compare_fusion
  109.2 0.4 fusion.65
  109.5 0.1 fusion.55
  109.7 5.8 %fusion = f32[676,128]{1,0:T(8,128)} fusion(pred[1024,676]{1,0:T(32,128)(4,1)S(1)} %get-tuple-element.121, pred[1024,676]{1,0:T(32,128)(4,1)S(1)} %get-tuple-element.122, f32[1024,128]{1,0:T(8,128)S(1)} %get-tuple-element.96, f32[1024,128]{1,0:T(8,128)S(1)} %get-tuple-element.97), kind=kOutput, calls=%fused_computation | convolution fusion | flops 2128158720 | bytes 2779136 | tf_op jit(solution)/shard_map/dot_general | solution.py:123
  115.4 1.0 reshape.273
  116.6 1.9 %collective-permute-start.4 = (bf16[1,2,24,128]{3,2,1,0:T(8,128)(2,1)S(1)}, bf16[1,2,24,128]{3,2,1,0:T(8,128)(2,1)S(1)}, u32[]{:S(2)}, u32[]{:S(2)}) collective-permute-start(bf16[1,2,24,128]{3,2,1,0:T(8,128)(2,1)S(1)} %maximum_bitcast_fusion.1), channel_id=1, source_target_pairs={{0,48},{48,96},{96,144},{144,192},{192,240},{240,288},{288,336},{3... | collective-permute-start | bytes 36872 | tf_op jit(solution)/shard_map/ppermute | solution.py:12
  118.5 10.9 %collective-permute-start.5 = (bf16[1,2,24,128]{3,2,1,0:T(8,128)(2,1)S(1)}, bf16[1,2,24,128]{3,2,1,0:T(8,128)(2,1)S(1)}, u32[]{:S(2)}, u32[]{:S(2)}) collective-permute-start(bf16[1,2,24,128]{3,2,1,0:T(8,128)(2,1)S(1)} %maximum_bitcast_fusion.2), channel_id=1, source_target_pairs={{48,0},{96,48},{144,96},{192,144},{240,192},{288,240},{336,288},{3... | collective-permute-start | bytes 36872 | tf_op jit(solution)/shard_map/ppermute | solution.py:15
  129.4 0.2 copy.84
  129.6 0.8 fusion.22
  130.3 32.6 %collective-permute-done.4 = bf16[1,2,24,128]{3,2,1,0:T(8,128)(2,1)S(1)} collective-permute-done((bf16[1,2,24,128]{3,2,1,0:T(8,128)(2,1)S(1)}, bf16[1,2,24,128]{3,2,1,0:T(8,128)(2,1)S(1)}, u32[]{:S(2)}, u32[]{:S(2)}) %collective-permute-start.4) | collective-permute-done | bytes 12320 | tf_op jit(solution)/shard_map/ppermute | solution.py:12
  163.0 4.2 %collective-permute-start.6 = (bf16[4,1,24,128]{3,2,1,0:T(8,128)(2,1)S(1)}, bf16[4,1,24,128]{3,2,1,0:T(8,128)(2,1)S(1)}, u32[]{:S(2)}, u32[]{:S(2)}) collective-permute-start(bf16[4,1,24,128]{3,2,1,0:T(8,128)(2,1)S(1)} %get-tuple-element.108), channel_id=1, source_target_pairs={{0,1},{1,2},{2,3},{3,4},{4,5},{5,6},{6,7},{7,8},{8,9},{9,10},{10,1... | collective-permute-start | bytes 73736 | tf_op jit(solution)/shard_map/ppermute | solution.py:12
  167.2 1.9 %collective-permute-start.7 = (bf16[4,1,24,128]{3,2,1,0:T(8,128)(2,1)S(1)}, bf16[4,1,24,128]{3,2,1,0:T(8,128)(2,1)S(1)}, u32[]{:S(2)}, u32[]{:S(2)}) collective-permute-start(bf16[4,1,24,128]{3,2,1,0:T(8,128)(2,1)S(1)} %get-tuple-element.109), channel_id=1, source_target_pairs={{1,0},{2,1},{3,2},{4,3},{5,4},{6,5},{7,6},{8,7},{9,8},{10,9},{11,1... | collective-permute-start | bytes 73736 | tf_op jit(solution)/shard_map/ppermute | solution.py:15
  169.1 1.0 slice_add_fusion
  170.3 0.8 copy.78
  171.1 3.0 %collective-permute-done.7 = bf16[4,1,24,128]{3,2,1,0:T(8,128)(2,1)S(1)} collective-permute-done((bf16[4,1,24,128]{3,2,1,0:T(8,128)(2,1)S(1)}, bf16[4,1,24,128]{3,2,1,0:T(8,128)(2,1)S(1)}, u32[]{:S(2)}, u32[]{:S(2)}) %collective-permute-start.7) | collective-permute-done | bytes 24608 | tf_op jit(solution)/shard_map/ppermute | solution.py:15
  174.5 0.7 copy.77
  175.1 0.1 reduce_sum.119
  175.3 0.6 slice.254
  175.9 0.6 fusion.61
  176.5 0.6 slice.256
  177.1 0.6 reshape_squeeze.7
  (82 shorter events, 1.9 us)
Async XLA Ops:
  0.6 42.2 %copy-start.4 = (bf16[1024,128]{1,0:T(8,128)(2,1)S(1)}, bf16[1024,128]{1,0:T(8,128)(2,1)}, u32[]{:S(2)}) copy-start(bf16[1024,128]{1,0:T(8,128)(2,1)} %param.31) | copy-start | bytes 786436
  1.4 32.6 %collective-permute-start = (bf16[1,24,128]{2,1,0:T(8,128)(2,1)S(1)}, bf16[1,24,128]{2,1,0:T(8,128)(2,1)S(1)}, u32[]{:S(2)}, u32[]{:S(2)}) collective-permute-start(bf16[1,24,128]{2,1,0:T(8,128)(2,1)S(1)} %get-tuple-element.105), channel_id=1, source_target_pairs={{0,48},{48,96},{96,144},{144,192},{192,240},{240,288},{288,336},{3... | collective-permute-start | bytes 18440 | tf_op jit(solution)/shard_map/ppermute | solution.py:12
  3.3 31.7 %collective-permute-start.1 = (bf16[1,24,128]{2,1,0:T(8,128)(2,1)S(1)}, bf16[1,24,128]{2,1,0:T(8,128)(2,1)S(1)}, u32[]{:S(2)}, u32[]{:S(2)}) collective-permute-start(bf16[1,24,128]{2,1,0:T(8,128)(2,1)S(1)} %get-tuple-element.104), channel_id=1, source_target_pairs={{48,0},{96,48},{144,96},{192,144},{240,192},{288,240},{336,288},{3... | collective-permute-start | bytes 18440 | tf_op jit(solution)/shard_map/ppermute | solution.py:15
  19.7 30.3 %all-to-all-start = ((bf16[16,57,128]{2,1,0:T(8,128)(2,1)}), bf16[16,57,128]{2,1,0:T(8,128)(2,1)S(1)}, u32[]{:S(2)}, u32[]{:S(2)}) async-start(bf16[16,57,128]{2,1,0:T(8,128)(2,1)} %broadcast_in_dim.15), calls=%async_computation | async-start | bytes 524288 | tf_op jit(solution)/shard_map/all_to_all | solution.py:57
  35.0 7.9 %collective-permute-start.2 = (bf16[26,1,128]{2,1,0:T(2,128)(2,1)S(1)}, bf16[26,1,128]{2,1,0:T(2,128)(2,1)S(1)}, u32[]{:S(2)}, u32[]{:S(2)}) collective-permute-start(bf16[26,1,128]{2,1,0:T(2,128)(2,1)S(1)} %get-tuple-element.102), channel_id=1, source_target_pairs={{0,1},{1,2},{2,3},{3,4},{4,5},{5,6},{6,7},{7,8},{8,9},{9,10},{10,1... | collective-permute-start | bytes 19976 | tf_op jit(solution)/shard_map/ppermute | solution.py:12
  39.7 6.8 %collective-permute-start.3 = (bf16[26,1,128]{2,1,0:T(2,128)(2,1)S(1)}, bf16[26,1,128]{2,1,0:T(2,128)(2,1)S(1)}, u32[]{:S(2)}, u32[]{:S(2)}) collective-permute-start(bf16[26,1,128]{2,1,0:T(2,128)(2,1)S(1)} %get-tuple-element.103), channel_id=1, source_target_pairs={{1,0},{2,1},{3,2},{4,3},{5,4},{6,5},{7,6},{8,7},{9,8},{10,9},{11,1... | collective-permute-start | bytes 19976 | tf_op jit(solution)/shard_map/ppermute | solution.py:15
  46.7 3.6 %copy-start = (bf16[24,24,128]{2,1,0:T(8,128)(2,1)S(1)}, bf16[24,24,128]{2,1,0:T(8,128)(2,1)}, u32[]{:S(2)}) copy-start(bf16[24,24,128]{2,1,0:T(8,128)(2,1)} %param.30) | copy-start | bytes 442372
  47.6 2.9 %copy-start.6 = (bf16[1024,128]{0,1:T(8,128)(2,1)}, bf16[1024,128]{0,1:T(8,128)(2,1)S(1)}, u32[]{:S(2)}) copy-start(bf16[1024,128]{0,1:T(8,128)(2,1)S(1)} %convolution_convert_fusion) | copy-start | bytes 786436
  48.4 2.1 %copy-start.8 = (bf16[1024,128]{0,1:T(8,128)(2,1)}, bf16[1024,128]{0,1:T(8,128)(2,1)S(1)}, u32[]{:S(2)}) copy-start(bf16[1024,128]{0,1:T(8,128)(2,1)S(1)} %convolution_convert_fusion.1) | copy-start | bytes 786436
  50.6 1.0 copy-start.5
  51.0 2.3 %copy-start.3 = (bf16[24,24,128]{2,1,0:T(8,128)(2,1)S(1)}, bf16[24,24,128]{2,1,0:T(8,128)(2,1)}, u32[]{:S(2)}) copy-start(bf16[24,24,128]{2,1,0:T(8,128)(2,1)} %param.20) | copy-start | bytes 442372
  55.4 2.2 %copy-start.1 = (f32[576,256]{1,0:T(8,128)}, f32[576,256]{1,0:T(8,128)S(1)}, u32[]{:S(2)}) copy-start(f32[576,256]{1,0:T(8,128)S(1)} %fusion.64) | copy-start | bytes 1769476
  57.6 1.0 copy-start.7
  57.6 1.0 copy-start.9
  97.6 77.5 %all-to-all-start.2 = ((f32[48,57,128]{2,1,0:T(8,128)}), f32[48,57,128]{2,1,0:T(8,128)S(1)}, u32[]{:S(2)}, u32[]{:S(2)}) async-start(f32[48,57,128]{2,1,0:T(8,128)} %broadcast_in_dim.16), calls=%async_computation.2 | async-start | bytes 3145728 | tf_op jit(solution)/shard_map/all_to_all | solution.py:67
  116.6 46.4 %collective-permute-start.4 = (bf16[1,2,24,128]{3,2,1,0:T(8,128)(2,1)S(1)}, bf16[1,2,24,128]{3,2,1,0:T(8,128)(2,1)S(1)}, u32[]{:S(2)}, u32[]{:S(2)}) collective-permute-start(bf16[1,2,24,128]{3,2,1,0:T(8,128)(2,1)S(1)} %maximum_bitcast_fusion.1), channel_id=1, source_target_pairs={{0,48},{48,96},{96,144},{144,192},{192,240},{240,288},{288,336},{3... | collective-permute-start | bytes 36872 | tf_op jit(solution)/shard_map/ppermute | solution.py:12
  118.5 44.5 %collective-permute-start.5 = (bf16[1,2,24,128]{3,2,1,0:T(8,128)(2,1)S(1)}, bf16[1,2,24,128]{3,2,1,0:T(8,128)(2,1)S(1)}, u32[]{:S(2)}, u32[]{:S(2)}) collective-permute-start(bf16[1,2,24,128]{3,2,1,0:T(8,128)(2,1)S(1)} %maximum_bitcast_fusion.2), channel_id=1, source_target_pairs={{48,0},{96,48},{144,96},{192,144},{240,192},{288,240},{336,288},{3... | collective-permute-start | bytes 36872 | tf_op jit(solution)/shard_map/ppermute | solution.py:15
  130.3 39.9 %copy-start.2 = (bf16[1024,128]{0,1:T(8,128)(2,1)S(1)}, bf16[1024,128]{0,1:T(8,128)(2,1)}, u32[]{:S(2)}) copy-start(bf16[1024,128]{0,1:T(8,128)(2,1)} %fusion.22) | copy-start | bytes 786436
  163.0 8.1 %collective-permute-start.6 = (bf16[4,1,24,128]{3,2,1,0:T(8,128)(2,1)S(1)}, bf16[4,1,24,128]{3,2,1,0:T(8,128)(2,1)S(1)}, u32[]{:S(2)}, u32[]{:S(2)}) collective-permute-start(bf16[4,1,24,128]{3,2,1,0:T(8,128)(2,1)S(1)} %get-tuple-element.108), channel_id=1, source_target_pairs={{0,1},{1,2},{2,3},{3,4},{4,5},{5,6},{6,7},{7,8},{8,9},{9,10},{10,1... | collective-permute-start | bytes 73736 | tf_op jit(solution)/shard_map/ppermute | solution.py:12
  167.2 6.9 %collective-permute-start.7 = (bf16[4,1,24,128]{3,2,1,0:T(8,128)(2,1)S(1)}, bf16[4,1,24,128]{3,2,1,0:T(8,128)(2,1)S(1)}, u32[]{:S(2)}, u32[]{:S(2)}) collective-permute-start(bf16[4,1,24,128]{3,2,1,0:T(8,128)(2,1)S(1)} %get-tuple-element.109), channel_id=1, source_target_pairs={{1,0},{2,1},{3,2},{4,3},{5,4},{6,5},{7,6},{8,7},{9,8},{10,9},{11,1... | collective-permute-start | bytes 73736 | tf_op jit(solution)/shard_map/ppermute | solution.py:15

commit v7 on v6

--- a/solution.py
+++ b/solution.py
@@ -51,6 +51,20 @@
     return (grad_inputs, first_part, second_part, gain_part)
 
 
+def exchange(value, axis, mask):
+    count = lax.axis_size(axis)
+    return lax.ppermute(value, axis, [(i, i ^ mask) for i in range(count)])
+
+
+def bit_masks(count):
+    masks = []
+    mask = 1
+    while mask < count:
+        masks.append(mask)
+        mask *= 2
+    return masks
+
+
 def gather_dom(packed):
     count = lax.axis_size("dom")
     spread = jnp.broadcast_to(packed[None], (count,) + packed.shape)
@@ -63,8 +77,26 @@
 
 def sum_sub(value):
     count = lax.axis_size("sub")
-    spread = jnp.broadcast_to(value[None], (count,) + value.shape)
-    return jnp.sum(lax.all_to_all(spread, "sub", 0, 0, tiled=True), axis=0)
+    index = lax.axis_index("sub")
+    total = value
+    mask = 1
+    while count % (2 * mask) == 0:
+        total = total + exchange(total, "sub", mask)
+        mask *= 2
+    rest = count // mask
+    if rest > 1:
+        member = index // mask
+        shifted = [total] + [
+            lax.ppermute(total, "sub", [(i, (i + k * mask) % count) for i in range(count)])
+            for k in range(1, rest)
+        ]
+        stacked = jnp.stack(shifted)
+        ordered = lax.dynamic_index_in_dim(stacked, member % rest, keepdims=False)
+        for source in range(1, rest):
+            pick = (member - source) % rest
+            ordered = ordered + lax.dynamic_index_in_dim(stacked, pick, keepdims=False)
+        total = ordered
+    return total
 
 
 def gather_params(weights, gains):

time: 179 us -> 166 us (0.927)
  the two profiles are of different devices: /device:TPU:154 before, /device:TPU:6 now
where the time goes in v7:
time: 166 us; the launch traced here: 165 us
  starting transfers between devices  96.3 us (58%)
  waiting for transfers between devices  29.5 us (18%)
  local copies, waits for them, and re-layouts  16.4 us (10%)
  matrix products  15.7 us (9%)
  other arithmetic  4.72 us (3%)
  between operations  2.18 us (1%)
    ppermute x4, starting transfers between devices, with_halo(): lax.ppermute(lax.slice_in_dim(block, 0, width, axis=dim), axis, backward)  27.1 us
    ppermute x4, starting transfers between devices, exchange(): return lax.ppermute(value, axis, [(i, i ^ mask) for i in range(count)])  23.3 us
    all_to_all x1, starting transfers between devices, gather_dom(): return lax.all_to_all(spread, 'dom', 0, 0, tiled=True)  13 us
    all_to_all x1, starting transfers between devices, reduce_scatter_dom(): return jnp.sum(lax.all_to_all(packed, 'dom', 0, 0, tiled=True), axis=0)  12 us
    ppermute x4, starting transfers between devices, with_halo(): lax.ppermute(lax.slice_in_dim(block, block.shape[dim] - width, None, axis...  10.8 us
    ppermute x4, waiting for transfers between devices, with_halo(): lax.ppermute(lax.slice_in_dim(block, block.shape[dim] - width, None, axis...  10.2 us
    ppermute x2, starting transfers between devices, sum_sub(): lax.ppermute(total, 'sub', [(i, (i + k * mask) % count) for i in range(co...  9.94 us
    unnamed x39, local copies, waits for them, and re-layouts  9.01 us
  transfers between devices with their start and end apart: 16, of which 7 were waited for; matrix products, arithmetic and copies ran while one was open for 10% of the time, Pallas kernels for 0%

profile of v7, /device:TPU:6, one launch (start us, length us, event | category | flops | bytes accessed | tf_op | source)
XLA Modules:
  0.0 164.8 jit_solution(12879488789437196796)
XLA Ops:
  0.7 0.8 fusion.59
  1.4 14.8 %collective-permute-start.1 = (bf16[1,24,128]{2,1,0:T(8,128)(2,1)S(1)}, bf16[1,24,128]{2,1,0:T(8,128)(2,1)S(1)}, u32[]{:S(2)}, u32[]{:S(2)}) collective-permute-start(bf16[1,24,128]{2,1,0:T(8,128)(2,1)S(1)} %get-tuple-element.90), channel_id=1, source_target_pairs={{48,0},{96,48},{144,96},{192,144},{240,192},{288,240},{336,288},{3... | collective-permute-start | bytes 18440 | tf_op jit(solution)/shard_map/ppermute | solution.py:15
  16.3 1.9 %collective-permute-start = (bf16[1,24,128]{2,1,0:T(8,128)(2,1)S(1)}, bf16[1,24,128]{2,1,0:T(8,128)(2,1)S(1)}, u32[]{:S(2)}, u32[]{:S(2)}) collective-permute-start(bf16[1,24,128]{2,1,0:T(8,128)(2,1)S(1)} %get-tuple-element.91), channel_id=1, source_target_pairs={{0,48},{48,96},{96,144},{144,192},{192,240},{240,288},{288,336},{3... | collective-permute-start | bytes 18440 | tf_op jit(solution)/shard_map/ppermute | solution.py:12
  18.2 0.7 reshape.274
  18.9 0.7 constant_dynamic-update-slice_fusion.7
  19.6 0.7 constant_dynamic-update-slice_fusion.6
  20.3 0.7 constant_dynamic-update-slice_fusion.5
  21.0 0.7 constant_dynamic-update-slice_fusion.4
  21.7 0.8 broadcast_in_dim.13
  22.5 13.0 %all-to-all-start = ((bf16[16,57,128]{2,1,0:T(8,128)(2,1)}), bf16[16,57,128]{2,1,0:T(8,128)(2,1)S(1)}, u32[]{:S(2)}, u32[]{:S(2)}) async-start(bf16[16,57,128]{2,1,0:T(8,128)(2,1)} %broadcast_in_dim.13), calls=%async_computation | async-start | bytes 524288 | tf_op jit(solution)/shard_map/all_to_all | solution.py:71
  35.5 0.7 select_add_fusion
  36.2 2.1 %iota_compare_fusion = (pred[1024,676]{1,0:T(32,128)(4,1)}, pred[1024,676]{1,0:T(32,128)(4,1)}) fusion(s32[1024]{0:T(1024)S(1)} %get-tuple-element.101, s32[1024]{0:T(1024)S(1)} %get-tuple-element.100), kind=kLoop, calls=%fused_computation.4 | loop fusion | flops 1384448 | bytes 1392640 | tf_op jit(solution)/shard_map/eq | solution.py:143
  39.1 3.5 %collective-permute-start.2 = (bf16[26,1,128]{2,1,0:T(2,128)(2,1)S(1)}, bf16[26,1,128]{2,1,0:T(2,128)(2,1)S(1)}, u32[]{:S(2)}, u32[]{:S(2)}) collective-permute-start(bf16[26,1,128]{2,1,0:T(2,128)(2,1)S(1)} %get-tuple-element.88), channel_id=1, source_target_pairs={{0,1},{1,2},{2,3},{3,4},{4,5},{5,6},{6,7},{7,8},{8,9},{9,10},{10,1... | collective-permute-start | bytes 19976 | tf_op jit(solution)/shard_map/ppermute | solution.py:12
  42.5 1.3 collective-permute-start.3
  44.3 3.9 %collective-permute-done.3 = bf16[26,1,128]{2,1,0:T(2,128)(2,1)S(1)} collective-permute-done((bf16[26,1,128]{2,1,0:T(2,128)(2,1)S(1)}, bf16[26,1,128]{2,1,0:T(2,128)(2,1)S(1)}, u32[]{:S(2)}, u32[]{:S(2)}) %collective-permute-start.3) | collective-permute-done | bytes 6688 | tf_op jit(solution)/shard_map/ppermute | solution.py:15
  48.3 0.8 convolution_convert_fusion
  49.2 0.8 convolution_convert_fusion.1
  50.8 0.4 fusion.26
  51.2 0.3 fusion.61
  51.6 1.7 %fusion.14 = bf16[576,128]{1,0:T(8,128)(2,1)S(1)} fusion(s32[1024]{0:T(1024)S(1)} %copy-done.8, f32[1024,128]{0,1:T(8,128)S(1)} %get-tuple-element.103, f32[1024]{0:T(1024)S(1)} %fusion.44, f32[128]{0:T(128)S(1)} %reshape.291, f32[1024]{0:T(1024)S(1)} %add_rsqrt_fusion.1, f32[1024]{0:T(1024)S(1)} %broadcast_multiply_fusion.5), kind=kOutput, calls=%fused_computation.20 | convolution fusion | flops 907747328 | bytes 688640 | tf_op jit(solution)/shard_map/dot_general | solution.py:155
  53.4 0.2 fusion.36
  53.6 0.3 fusion.62
  53.9 0.3 multiply_reduce_fusion.5
  54.2 0.4 fusion.29
  54.6 0.4 multiply_convert_fusion.1
  55.1 1.0 fusion.35
  56.1 0.2 fusion.63
  56.3 1.9 %multiply_reduce_fusion = (f32[128]{0:T(128)S(1)}, f32[1024]{0:T(1024)S(1)}, f32[1024]{0:T(1024)S(1)}, f32[1024,128]{0,1:T(8,128)S(1)}) fusion(f32[1024,128]{0,1:T(8,128)S(1)} %get-tuple-element.103, f32[1024]{0:T(1024)S(1)} %add_rsqrt_fusion.1, f32[1024]{0:T(1024)S(1)} %broadcast_multiply_fusion.5, f32[128]{0:T(128)S(1)} %reshape.291, ...), kind=kOutput, calls=%fused_computation.31 | convolution fusion | flops 907999104 | bytes 1631232 | tf_op jit(solution)/shard_map/dot_general | solution.py:149
  58.4 0.3 fusion.12
  58.7 0.5 copy-done.10
  59.2 0.4 fusion.25
  59.6 0.4 fusion.64
  60.3 0.7 constant_dynamic-update-slice_fusion.9
  61.0 0.9 fusion.18
  61.9 1.6 constant_dynamic-update-slice_fusion.8
  63.5 0.9 fusion.17
  64.4 1.5 dynamic-update-slice.16
  65.8 12.0 %all-to-all-start.1 = ((f32[16,57,128]{2,1,0:T(8,128)}), f32[16,57,128]{2,1,0:T(8,128)S(1)}, u32[]{:S(2)}, u32[]{:S(2)}) async-start(f32[16,57,128]{2,1,0:T(8,128)} %dynamic-update-slice.16), calls=%async_computation.1 | async-start | bytes 1048576 | tf_op jit(solution)/shard_map/all_to_all | solution.py:75
  78.0 1.0 copy-done.3
  79.0 0.2 copy-done.4
  79.3 5.1 %fusion = f32[676,128]{1,0:T(8,128)S(1)} fusion(pred[1024,676]{1,0:T(32,128)(4,1)S(1)} %copy-done.3, pred[1024,676]{1,0:T(32,128)(4,1)S(1)} %copy-done.4, f32[1024,128]{1,0:T(8,128)S(1)} %get-tuple-element.82, f32[1024,128]{1,0:T(8,128)S(1)} %get-tuple-element.83), kind=kOutput, calls=%fused_computation | convolution fusion | flops 2128158720 | bytes 2779136 | tf_op jit(solution)/shard_map/dot_general | solution.py:155
  84.4 0.2 copy.56
  84.7 9.7 %collective-permute-start.5 = (bf16[1,2,24,128]{3,2,1,0:T(8,128)(2,1)S(1)}, bf16[1,2,24,128]{3,2,1,0:T(8,128)(2,1)S(1)}, u32[]{:S(2)}, u32[]{:S(2)}) collective-permute-start(bf16[1,2,24,128]{3,2,1,0:T(8,128)(2,1)S(1)} %maximum_bitcast_fusion.2), channel_id=1, source_target_pairs={{48,0},{96,48},{144,96},{192,144},{240,192},{288,240},{336,288},{3... | collective-permute-start | bytes 36872 | tf_op jit(solution)/shard_map/ppermute | solution.py:15
  94.4 1.9 %collective-permute-start.4 = (bf16[1,2,24,128]{3,2,1,0:T(8,128)(2,1)S(1)}, bf16[1,2,24,128]{3,2,1,0:T(8,128)(2,1)S(1)}, u32[]{:S(2)}, u32[]{:S(2)}) collective-permute-start(bf16[1,2,24,128]{3,2,1,0:T(8,128)(2,1)S(1)} %maximum_bitcast_fusion.1), channel_id=1, source_target_pairs={{0,48},{48,96},{96,144},{144,192},{192,240},{240,288},{288,336},{3... | collective-permute-start | bytes 36872 | tf_op jit(solution)/shard_map/ppermute | solution.py:12
  96.4 10.2 %collective-permute-done.4 = bf16[1,2,24,128]{3,2,1,0:T(8,128)(2,1)S(1)} collective-permute-done((bf16[1,2,24,128]{3,2,1,0:T(8,128)(2,1)S(1)}, bf16[1,2,24,128]{3,2,1,0:T(8,128)(2,1)S(1)}, u32[]{:S(2)}, u32[]{:S(2)}) %collective-permute-start.4) | collective-permute-done | bytes 12320 | tf_op jit(solution)/shard_map/ppermute | solution.py:12
  106.7 3.5 %collective-permute-start.6 = (bf16[4,1,24,128]{3,2,1,0:T(8,128)(2,1)S(1)}, bf16[4,1,24,128]{3,2,1,0:T(8,128)(2,1)S(1)}, u32[]{:S(2)}, u32[]{:S(2)}) collective-permute-start(bf16[4,1,24,128]{3,2,1,0:T(8,128)(2,1)S(1)} %get-tuple-element.94), channel_id=1, source_target_pairs={{0,1},{1,2},{2,3},{3,4},{4,5},{5,6},{6,7},{7,8},{8,9},{9,10},{10,1... | collective-permute-start | bytes 73736 | tf_op jit(solution)/shard_map/ppermute | solution.py:12
  110.2 1.3 collective-permute-start.7
  111.6 0.8 copy.51
  112.6 4.9 %collective-permute-start.8 = (f32[57,128]{1,0:T(8,128)S(1)}, f32[57,128]{1,0:T(8,128)S(1)}, u32[]{:S(2)}, u32[]{:S(2)}) collective-permute-start(f32[57,128]{1,0:T(8,128)S(1)} %reduce_sum.109), channel_id=1, source_target_pairs={{0,1},{1,0},{2,3},{3,2},{4,5},{5,4},{6,7},{7,6},{8,9},{9,8},{10,11... | collective-permute-start | bytes 87560 | tf_op jit(solution)/shard_map/ppermute | solution.py:56
  117.6 1.7 %collective-permute-done.8 = f32[57,128]{1,0:T(8,128)S(1)} collective-permute-done((f32[57,128]{1,0:T(8,128)S(1)}, f32[57,128]{1,0:T(8,128)S(1)}, u32[]{:S(2)}, u32[]{:S(2)}) %collective-permute-start.8) | collective-permute-done | bytes 29216 | tf_op jit(solution)/shard_map/ppermute | solution.py:56
  119.3 6.8 %collective-permute-start.9 = (f32[57,128]{1,0:T(8,128)S(1)}, f32[57,128]{1,0:T(8,128)S(1)}, u32[]{:S(2)}, u32[]{:S(2)}) collective-permute-start(f32[57,128]{1,0:T(8,128)S(1)} %add.158), channel_id=1, source_target_pairs={{0,2},{1,3},{2,0},{3,1},{4,6},{5,7},{6,4},{7,5},{8,10},{9,11},{10,... | collective-permute-start | bytes 87560 | tf_op jit(solution)/shard_map/ppermute | solution.py:56
  126.3 1.8 %collective-permute-done.9 = f32[57,128]{1,0:T(8,128)S(1)} collective-permute-done((f32[57,128]{1,0:T(8,128)S(1)}, f32[57,128]{1,0:T(8,128)S(1)}, u32[]{:S(2)}, u32[]{:S(2)}) %collective-permute-start.9) | collective-permute-done | bytes 29216 | tf_op jit(solution)/shard_map/ppermute | solution.py:56
  128.1 6.7 %collective-permute-start.10 = (f32[57,128]{1,0:T(8,128)S(1)}, f32[57,128]{1,0:T(8,128)S(1)}, u32[]{:S(2)}, u32[]{:S(2)}) collective-permute-start(f32[57,128]{1,0:T(8,128)S(1)} %add.159), channel_id=1, source_target_pairs={{0,4},{1,5},{2,6},{3,7},{4,0},{5,1},{6,2},{7,3},{8,12},{9,13},{10,... | collective-permute-start | bytes 87560 | tf_op jit(solution)/shard_map/ppermute | solution.py:56
  134.8 3.0 %collective-permute-done.10 = f32[57,128]{1,0:T(8,128)S(1)} collective-permute-done((f32[57,128]{1,0:T(8,128)S(1)}, f32[57,128]{1,0:T(8,128)S(1)}, u32[]{:S(2)}, u32[]{:S(2)}) %collective-permute-start.10) | collective-permute-done | bytes 29216 | tf_op jit(solution)/shard_map/ppermute | solution.py:56
  137.8 4.9 %collective-permute-start.11 = (f32[57,128]{1,0:T(8,128)S(1)}, f32[57,128]{1,0:T(8,128)S(1)}, u32[]{:S(2)}, u32[]{:S(2)}) collective-permute-start(f32[57,128]{1,0:T(8,128)S(1)} %add.160), channel_id=1, source_target_pairs={{0,8},{1,9},{2,10},{3,11},{4,12},{5,13},{6,14},{7,15},{8,0},{9,1},... | collective-permute-start | bytes 87560 | tf_op jit(solution)/shard_map/ppermute | solution.py:56
  142.7 1.9 %collective-permute-done.11 = f32[57,128]{1,0:T(8,128)S(1)} collective-permute-done((f32[57,128]{1,0:T(8,128)S(1)}, f32[57,128]{1,0:T(8,128)S(1)}, u32[]{:S(2)}, u32[]{:S(2)}) %collective-permute-start.11) | collective-permute-done | bytes 29216 | tf_op jit(solution)/shard_map/ppermute | solution.py:56
  144.6 8.0 %collective-permute-start.13 = (f32[57,128]{1,0:T(8,128)S(1)}, f32[57,128]{1,0:T(8,128)S(1)}, u32[]{:S(2)}, u32[]{:S(2)}) collective-permute-start(f32[57,128]{1,0:T(8,128)S(1)} %add.161), channel_id=1, source_target_pairs={{0,32},{1,33},{2,34},{3,35},{4,36},{5,37},{6,38},{7,39},{8,40},{9,... | collective-permute-start | bytes 87560 | tf_op jit(solution)/shard_map/ppermute | solution.py:90
  152.6 1.9 %collective-permute-start.12 = (f32[57,128]{1,0:T(8,128)S(1)}, f32[57,128]{1,0:T(8,128)S(1)}, u32[]{:S(2)}, u32[]{:S(2)}) collective-permute-start(f32[57,128]{1,0:T(8,128)S(1)} %add.161), channel_id=1, source_target_pairs={{0,16},{1,17},{2,18},{3,19},{4,20},{5,21},{6,22},{7,23},{8,24},{9,... | collective-permute-start | bytes 87560 | tf_op jit(solution)/shard_map/ppermute | solution.py:90
  154.6 0.7 copy.50
  155.3 7.0 %collective-permute-done.12 = f32[57,128]{1,0:T(8,128)S(1)} collective-permute-done((f32[57,128]{1,0:T(8,128)S(1)}, f32[57,128]{1,0:T(8,128)S(1)}, u32[]{:S(2)}, u32[]{:S(2)}) %collective-permute-start.12) | collective-permute-done | bytes 29216 | tf_op jit(solution)/shard_map/ppermute | solution.py:90
  162.4 0.6 slice_bitcast_fusion.7
  163.0 0.6 slice_bitcast_fusion.8
  163.6 0.6 slice_bitcast_fusion.6
  164.2 0.6 reshape_squeeze.7
  (99 shorter events, 2.9 us)
Async XLA Ops:
  0.6 38.3 %copy-start.5 = (bf16[24,24,128]{2,1,0:T(8,128)(2,1)S(1)}, bf16[24,24,128]{2,1,0:T(8,128)(2,1)}, u32[]{:S(2)}) copy-start(bf16[24,24,128]{2,1,0:T(8,128)(2,1)} %param.20) | copy-start | bytes 442372
  0.6 43.3 %copy-start.6 = (bf16[1024,128]{1,0:T(8,128)(2,1)S(1)}, bf16[1024,128]{1,0:T(8,128)(2,1)}, u32[]{:S(2)}) copy-start(bf16[1024,128]{1,0:T(8,128)(2,1)} %param.21) | copy-start | bytes 786436
  1.4 37.6 %collective-permute-start.1 = (bf16[1,24,128]{2,1,0:T(8,128)(2,1)S(1)}, bf16[1,24,128]{2,1,0:T(8,128)(2,1)S(1)}, u32[]{:S(2)}, u32[]{:S(2)}) collective-permute-start(bf16[1,24,128]{2,1,0:T(8,128)(2,1)S(1)} %get-tuple-element.90), channel_id=1, source_target_pairs={{48,0},{96,48},{144,96},{192,144},{240,192},{288,240},{336,288},{3... | collective-permute-start | bytes 18440 | tf_op jit(solution)/shard_map/ppermute | solution.py:15
  16.3 22.7 %collective-permute-start = (bf16[1,24,128]{2,1,0:T(8,128)(2,1)S(1)}, bf16[1,24,128]{2,1,0:T(8,128)(2,1)S(1)}, u32[]{:S(2)}, u32[]{:S(2)}) collective-permute-start(bf16[1,24,128]{2,1,0:T(8,128)(2,1)S(1)} %get-tuple-element.91), channel_id=1, source_target_pairs={{0,48},{48,96},{96,144},{144,192},{192,240},{240,288},{288,336},{3... | collective-permute-start | bytes 18440 | tf_op jit(solution)/shard_map/ppermute | solution.py:12
  22.5 21.7 %copy-start.7 = (bf16[1024,128]{1,0:T(8,128)(2,1)S(1)}, bf16[1024,128]{1,0:T(8,128)(2,1)}, u32[]{:S(2)}) copy-start(bf16[1024,128]{1,0:T(8,128)(2,1)} %param.31) | copy-start | bytes 786436
  22.5 27.6 %all-to-all-start = ((bf16[16,57,128]{2,1,0:T(8,128)(2,1)}), bf16[16,57,128]{2,1,0:T(8,128)(2,1)S(1)}, u32[]{:S(2)}, u32[]{:S(2)}) async-start(bf16[16,57,128]{2,1,0:T(8,128)(2,1)} %broadcast_in_dim.13), calls=%async_computation | async-start | bytes 524288 | tf_op jit(solution)/shard_map/all_to_all | solution.py:71
  39.1 5.2 %collective-permute-start.2 = (bf16[26,1,128]{2,1,0:T(2,128)(2,1)S(1)}, bf16[26,1,128]{2,1,0:T(2,128)(2,1)S(1)}, u32[]{:S(2)}, u32[]{:S(2)}) collective-permute-start(bf16[26,1,128]{2,1,0:T(2,128)(2,1)S(1)} %get-tuple-element.88), channel_id=1, source_target_pairs={{0,1},{1,2},{2,3},{3,4},{4,5},{5,6},{6,7},{7,8},{8,9},{9,10},{10,1... | collective-permute-start | bytes 19976 | tf_op jit(solution)/shard_map/ppermute | solution.py:12
  42.5 5.6 %collective-permute-start.3 = (bf16[26,1,128]{2,1,0:T(2,128)(2,1)S(1)}, bf16[26,1,128]{2,1,0:T(2,128)(2,1)S(1)}, u32[]{:S(2)}, u32[]{:S(2)}) collective-permute-start(bf16[26,1,128]{2,1,0:T(2,128)(2,1)S(1)} %get-tuple-element.89), channel_id=1, source_target_pairs={{1,0},{2,1},{3,2},{4,3},{5,4},{6,5},{7,6},{8,7},{9,8},{10,9},{11,1... | collective-permute-start | bytes 19976 | tf_op jit(solution)/shard_map/ppermute | solution.py:15
  48.3 2.0 %copy-start = (bf16[24,24,128]{2,1,0:T(8,128)(2,1)S(1)}, bf16[24,24,128]{2,1,0:T(8,128)(2,1)}, u32[]{:S(2)}) copy-start(bf16[24,24,128]{2,1,0:T(8,128)(2,1)} %param.30) | copy-start | bytes 442372
  50.0 1.2 copy-start.9
  50.8 0.8 copy-start.8
  56.3 2.1 %copy-start.1 = (f32[576,256]{1,0:T(8,128)}, f32[576,256]{1,0:T(8,128)S(1)}, u32[]{:S(2)}) copy-start(f32[576,256]{1,0:T(8,128)S(1)} %fusion.63) | copy-start | bytes 1769476
  58.2 1.0 copy-start.10
  65.8 46.7 %all-to-all-start.1 = ((f32[16,57,128]{2,1,0:T(8,128)}), f32[16,57,128]{2,1,0:T(8,128)S(1)}, u32[]{:S(2)}, u32[]{:S(2)}) async-start(f32[16,57,128]{2,1,0:T(8,128)} %dynamic-update-slice.16), calls=%async_computation.1 | async-start | bytes 1048576 | tf_op jit(solution)/shard_map/all_to_all | solution.py:75
  77.9 1.1 copy-start.3
  77.9 1.4 copy-start.4
  84.4 27.1 %copy-start.2 = (f32[576,256]{1,0:T(8,128)S(1)}, f32[576,256]{1,0:T(8,128)}, u32[]{:S(2)}) copy-start(f32[576,256]{1,0:T(8,128)} %copy-done.1) | copy-start | bytes 1769476
  84.7 11.7 %collective-permute-start.5 = (bf16[1,2,24,128]{3,2,1,0:T(8,128)(2,1)S(1)}, bf16[1,2,24,128]{3,2,1,0:T(8,128)(2,1)S(1)}, u32[]{:S(2)}, u32[]{:S(2)}) collective-permute-start(bf16[1,2,24,128]{3,2,1,0:T(8,128)(2,1)S(1)} %maximum_bitcast_fusion.2), channel_id=1, source_target_pairs={{48,0},{96,48},{144,96},{192,144},{240,192},{288,240},{336,288},{3... | collective-permute-start | bytes 36872 | tf_op jit(solution)/shard_map/ppermute | solution.py:15
  94.4 12.2 %collective-permute-start.4 = (bf16[1,2,24,128]{3,2,1,0:T(8,128)(2,1)S(1)}, bf16[1,2,24,128]{3,2,1,0:T(8,128)(2,1)S(1)}, u32[]{:S(2)}, u32[]{:S(2)}) collective-permute-start(bf16[1,2,24,128]{3,2,1,0:T(8,128)(2,1)S(1)} %maximum_bitcast_fusion.1), channel_id=1, source_target_pairs={{0,48},{48,96},{96,144},{144,192},{192,240},{240,288},{288,336},{3... | collective-permute-start | bytes 36872 | tf_op jit(solution)/shard_map/ppermute | solution.py:12
  106.7 10.7 %collective-permute-start.6 = (bf16[4,1,24,128]{3,2,1,0:T(8,128)(2,1)S(1)}, bf16[4,1,24,128]{3,2,1,0:T(8,128)(2,1)S(1)}, u32[]{:S(2)}, u32[]{:S(2)}) collective-permute-start(bf16[4,1,24,128]{3,2,1,0:T(8,128)(2,1)S(1)} %get-tuple-element.94), channel_id=1, source_target_pairs={{0,1},{1,2},{2,3},{3,4},{4,5},{5,6},{6,7},{7,8},{8,9},{9,10},{10,1... | collective-permute-start | bytes 73736 | tf_op jit(solution)/shard_map/ppermute | solution.py:12
  110.2 7.2 %collective-permute-start.7 = (bf16[4,1,24,128]{3,2,1,0:T(8,128)(2,1)S(1)}, bf16[4,1,24,128]{3,2,1,0:T(8,128)(2,1)S(1)}, u32[]{:S(2)}, u32[]{:S(2)}) collective-permute-start(bf16[4,1,24,128]{3,2,1,0:T(8,128)(2,1)S(1)} %get-tuple-element.95), channel_id=1, source_target_pairs={{1,0},{2,1},{3,2},{4,3},{5,4},{6,5},{7,6},{8,7},{9,8},{10,9},{11,1... | collective-permute-start | bytes 73736 | tf_op jit(solution)/shard_map/ppermute | solution.py:15
  112.6 6.8 %collective-permute-start.8 = (f32[57,128]{1,0:T(8,128)S(1)}, f32[57,128]{1,0:T(8,128)S(1)}, u32[]{:S(2)}, u32[]{:S(2)}) collective-permute-start(f32[57,128]{1,0:T(8,128)S(1)} %reduce_sum.109), channel_id=1, source_target_pairs={{0,1},{1,0},{2,3},{3,2},{4,5},{5,4},{6,7},{7,6},{8,9},{9,8},{10,11... | collective-permute-start | bytes 87560 | tf_op jit(solution)/shard_map/ppermute | solution.py:56
  119.3 8.7 %collective-permute-start.9 = (f32[57,128]{1,0:T(8,128)S(1)}, f32[57,128]{1,0:T(8,128)S(1)}, u32[]{:S(2)}, u32[]{:S(2)}) collective-permute-start(f32[57,128]{1,0:T(8,128)S(1)} %add.158), channel_id=1, source_target_pairs={{0,2},{1,3},{2,0},{3,1},{4,6},{5,7},{6,4},{7,5},{8,10},{9,11},{10,... | collective-permute-start | bytes 87560 | tf_op jit(solution)/shard_map/ppermute | solution.py:56
  128.1 9.7 %collective-permute-start.10 = (f32[57,128]{1,0:T(8,128)S(1)}, f32[57,128]{1,0:T(8,128)S(1)}, u32[]{:S(2)}, u32[]{:S(2)}) collective-permute-start(f32[57,128]{1,0:T(8,128)S(1)} %add.159), channel_id=1, source_target_pairs={{0,4},{1,5},{2,6},{3,7},{4,0},{5,1},{6,2},{7,3},{8,12},{9,13},{10,... | collective-permute-start | bytes 87560 | tf_op jit(solution)/shard_map/ppermute | solution.py:56
  137.8 6.8 %collective-permute-start.11 = (f32[57,128]{1,0:T(8,128)S(1)}, f32[57,128]{1,0:T(8,128)S(1)}, u32[]{:S(2)}, u32[]{:S(2)}) collective-permute-start(f32[57,128]{1,0:T(8,128)S(1)} %add.160), channel_id=1, source_target_pairs={{0,8},{1,9},{2,10},{3,11},{4,12},{5,13},{6,14},{7,15},{8,0},{9,1},... | collective-permute-start | bytes 87560 | tf_op jit(solution)/shard_map/ppermute | solution.py:56
  144.6 10.7 %collective-permute-start.13 = (f32[57,128]{1,0:T(8,128)S(1)}, f32[57,128]{1,0:T(8,128)S(1)}, u32[]{:S(2)}, u32[]{:S(2)}) collective-permute-start(f32[57,128]{1,0:T(8,128)S(1)} %add.161), channel_id=1, source_target_pairs={{0,32},{1,33},{2,34},{3,35},{4,36},{5,37},{6,38},{7,39},{8,40},{9,... | collective-permute-start | bytes 87560 | tf_op jit(solution)/shard_map/ppermute | solution.py:90
  152.6 9.7 %collective-permute-start.12 = (f32[57,128]{1,0:T(8,128)S(1)}, f32[57,128]{1,0:T(8,128)S(1)}, u32[]{:S(2)}, u32[]{:S(2)}) collective-permute-start(f32[57,128]{1,0:T(8,128)S(1)} %add.161), channel_id=1, source_target_pairs={{0,16},{1,17},{2,18},{3,19},{4,20},{5,21},{6,22},{7,23},{8,24},{9,... | collective-permute-start | bytes 87560 | tf_op jit(solution)/shard_map/ppermute | solution.py:90

commit v8 on v6

--- a/solution.py
+++ b/solution.py
@@ -6,7 +6,7 @@
 
 def with_halo(block, sides, width):
     for axis, dim in sides:
-        count = lax.axis_size(axis)
+        count = axis_count(axis)
         forward = [(i, i + 1) for i in range(count - 1)]
         backward = [(target, source) for source, target in forward]
         low = lax.ppermute(
@@ -51,6 +51,32 @@
     return (grad_inputs, first_part, second_part, gain_part)
 
 
+SUB = ("sub_hi", "sub_lo")
+
+
+def axis_count(axis):
+    if isinstance(axis, tuple):
+        total = 1
+        for name in axis:
+            total *= lax.axis_size(name)
+        return total
+    return lax.axis_size(axis)
+
+
+def exchange(value, axis, mask):
+    count = axis_count(axis)
+    return lax.ppermute(value, axis, [(i, i ^ mask) for i in range(count)])
+
+
+def bit_masks(count):
+    masks = []
+    mask = 1
+    while mask < count:
+        masks.append(mask)
+        mask *= 2
+    return masks
+
+
 def gather_dom(packed):
     count = lax.axis_size("dom")
     spread = jnp.broadcast_to(packed[None], (count,) + packed.shape)
@@ -62,9 +88,12 @@
 
 
 def sum_sub(value):
-    count = lax.axis_size("sub")
-    spread = jnp.broadcast_to(value[None], (count,) + value.shape)
-    return jnp.sum(lax.all_to_all(spread, "sub", 0, 0, tiled=True), axis=0)
+    total = value
+    for axis in reversed(SUB):
+        count = lax.axis_size(axis)
+        spread = jnp.broadcast_to(total[None], (count,) + total.shape)
+        total = jnp.sum(lax.all_to_all(spread, axis, 0, 0, tiled=True), axis=0)
+    return total
 
 
 def gather_params(weights, gains):
@@ -151,7 +180,7 @@
     block_side = node_feat.shape[0]
     latent = node_feat.shape[2]
     padded_side = block_side + 2
-    padded = with_halo(node_feat, (("dom", 0), ("sub", 1)), 1).reshape(
+    padded = with_halo(node_feat, (("dom", 0), (SUB, 1)), 1).reshape(
         padded_side * padded_side, latent
     )
     node_row = edge_dst // block_side
@@ -208,7 +237,7 @@
             jnp.stack([spread[-1, 1:-1], spread[1:-1, -1]]),
         ]
     )
-    incoming = with_halo(outgoing.astype(jnp.bfloat16), (("dom", 0), ("sub", 1)), 1).astype(
+    incoming = with_halo(outgoing.astype(jnp.bfloat16), (("dom", 0), (SUB, 1)), 1).astype(
         outgoing.dtype
     )
     inner = spread[1:-1, 1:-1]
@@ -216,7 +245,7 @@
     inner = inner.at[:, 0].add(incoming[2, 0]).at[:, -1].add(incoming[1, 3])
     node_total = node_upstream + node_in_grad[:, :latent]
     node_grad = (node_total.reshape(block_side, block_side, latent) + inner).astype(jnp.bfloat16)
-    nodes_all = block_side * block_side * lax.axis_size("dom") * lax.axis_size("sub")
+    nodes_all = block_side * block_side * lax.axis_size("dom") * axis_count(SUB)
     grad_scale = lax.rsqrt(jnp.float32(nodes_all))
     results = reduce_params(
         (edge_first, edge_second, node_first, node_second), jnp.stack([edge_gain, node_gain]), grad_scale
@@ -226,26 +255,31 @@
 
 def solution(mesh):
     in_specs = (
-        P("dom", "sub", None),
-        P(("dom", "sub"), None),
-        P(("dom", "sub")),
-        P(("dom", "sub")),
-        P(("dom", "sub")),
+        P("dom", SUB, None),
+        P(("dom",) + SUB, None),
+        P(("dom",) + SUB),
+        P(("dom",) + SUB),
+        P(("dom",) + SUB),
         P("dom", None),
         P("dom", None),
         P("dom", None),
         P("dom", None),
         P(None, "dom"),
-        P("dom", "sub", None),
-        P(("dom", "sub"), None),
+        P("dom", SUB, None),
+        P(("dom",) + SUB, None),
     )
     out_specs = (
-        P("dom", "sub", None),
-        P(("dom", "sub"), None),
+        P("dom", SUB, None),
+        P(("dom",) + SUB, None),
         P("dom", None),
         P("dom", None),
         P("dom", None),
         P("dom", None),
         P(None, "dom"),
     )
-    return jax.shard_map(shards, mesh=mesh, in_specs=in_specs, out_specs=out_specs, check_vma=False)
+    devices = mesh.devices
+    low = 8 if devices.shape[1] % 8 == 0 else 1
+    split = jax.sharding.Mesh(
+        devices.reshape(devices.shape[0], devices.shape[1] // low, low), ("dom",) + SUB
+    )
+    return jax.shard_map(shards, mesh=split, in_specs=in_specs, out_specs=out_specs, check_vma=False)

time: 179 us -> 155 us (0.87)
  the two profiles are of different devices: /device:TPU:154 before, /device:TPU:6 now
where the time goes in v8:
time: 155 us; the launch traced here: 154 us
  starting transfers between devices  76 us (49%)
  waiting for transfers between devices  38 us (25%)
  local copies, waits for them, and re-layouts  17.1 us (11%)
  matrix products  16.1 us (10%)
  other arithmetic  4.7 us (3%)
  between operations  2.03 us (1%)
    ppermute x4, starting transfers between devices, with_halo(): lax.ppermute(lax.slice_in_dim(block, 0, width, axis=dim), axis, backward)  27.1 us
    all_to_all x2, waiting for transfers between devices, sum_sub(): total = jnp.sum(lax.all_to_all(spread, axis, 0, 0, tiled=True), axis=0)  20.1 us
    all_to_all x1, starting transfers between devices, gather_dom(): return lax.all_to_all(spread, 'dom', 0, 0, tiled=True)  13 us
    all_to_all x2, starting transfers between devices, sum_sub(): total = jnp.sum(lax.all_to_all(spread, axis, 0, 0, tiled=True), axis=0)  13 us
    all_to_all x1, starting transfers between devices, reduce_scatter_dom(): return jnp.sum(lax.all_to_all(packed, 'dom', 0, 0, tiled=True), axis=0)  12 us
    ppermute x4, starting transfers between devices, with_halo(): lax.ppermute(lax.slice_in_dim(block, block.shape[dim] - width, None, axis...  10.8 us
    ppermute x4, waiting for transfers between devices, with_halo(): lax.ppermute(lax.slice_in_dim(block, block.shape[dim] - width, None, axis...  10.2 us
    dot_general x2, matrix products, sum_rows(): lax.dot_general(pick.astype(jnp.float32), values, (((0,), (0,)), ((), ())...  8.44 us
  transfers between devices with their start and end apart: 12, of which 5 were waited for; matrix products, arithmetic and copies ran while one was open for 13% of the time, Pallas kernels for 0%

profile of v8, /device:TPU:6, one launch (start us, length us, event | category | flops | bytes accessed | tf_op | source)
XLA Modules:
  0.0 154.0 jit_solution(16079178170809753925)
XLA Ops:
  0.7 0.8 fusion.59
  1.4 14.8 %collective-permute-start.1 = (bf16[1,24,128]{2,1,0:T(8,128)(2,1)S(1)}, bf16[1,24,128]{2,1,0:T(8,128)(2,1)S(1)}, u32[]{:S(2)}, u32[]{:S(2)}) collective-permute-start(bf16[1,24,128]{2,1,0:T(8,128)(2,1)S(1)} %get-tuple-element.104), channel_id=1, source_target_pairs={{48,0},{96,48},{144,96},{192,144},{240,192},{288,240},{336,288},{3... | collective-permute-start | bytes 18440 | tf_op jit(solution)/shard_map/ppermute | solution.py:15
  16.3 1.9 %collective-permute-start = (bf16[1,24,128]{2,1,0:T(8,128)(2,1)S(1)}, bf16[1,24,128]{2,1,0:T(8,128)(2,1)S(1)}, u32[]{:S(2)}, u32[]{:S(2)}) collective-permute-start(bf16[1,24,128]{2,1,0:T(8,128)(2,1)S(1)} %get-tuple-element.105), channel_id=1, source_target_pairs={{0,48},{48,96},{96,144},{144,192},{192,240},{240,288},{288,336},{3... | collective-permute-start | bytes 18440 | tf_op jit(solution)/shard_map/ppermute | solution.py:12
  18.2 0.7 reshape.268
  18.9 0.7 constant_dynamic-update-slice_fusion.7
  19.6 0.7 constant_dynamic-update-slice_fusion.6
  20.3 0.7 constant_dynamic-update-slice_fusion.5
  21.0 0.7 constant_dynamic-update-slice_fusion.4
  21.7 0.8 broadcast_in_dim.17
  22.5 13.0 %all-to-all-start = ((bf16[16,57,128]{2,1,0:T(8,128)(2,1)}), bf16[16,57,128]{2,1,0:T(8,128)(2,1)S(1)}, u32[]{:S(2)}, u32[]{:S(2)}) async-start(bf16[16,57,128]{2,1,0:T(8,128)(2,1)} %broadcast_in_dim.17), calls=%async_computation | async-start | bytes 524288 | tf_op jit(solution)/shard_map/all_to_all | solution.py:83
  35.5 0.7 select_add_fusion
  36.2 2.1 %iota_compare_fusion = (pred[1024,676]{1,0:T(32,128)(4,1)}, pred[1024,676]{1,0:T(32,128)(4,1)}) fusion(s32[1024]{0:T(1024)S(1)} %get-tuple-element.115, s32[1024]{0:T(1024)S(1)} %get-tuple-element.114), kind=kLoop, calls=%fused_computation.4 | loop fusion | flops 1384448 | bytes 1392640 | tf_op jit(solution)/shard_map/eq | solution.py:140
  39.1 3.5 %collective-permute-start.2 = (bf16[26,1,128]{2,1,0:T(2,128)(2,1)S(1)}, bf16[26,1,128]{2,1,0:T(2,128)(2,1)S(1)}, u32[]{:S(2)}, u32[]{:S(2)}) collective-permute-start(bf16[26,1,128]{2,1,0:T(2,128)(2,1)S(1)} %get-tuple-element.102), channel_id=1, source_target_pairs={{0,1},{1,2},{2,3},{3,4},{4,5},{5,6},{6,7},{7,8},{8,9},{9,10},{10,1... | collective-permute-start | bytes 19976 | tf_op jit(solution)/shard_map/ppermute | solution.py:12
  42.6 1.3 collective-permute-start.3
  43.9 0.1 copy.65
  44.0 0.1 copy.69
  44.2 4.0 %collective-permute-done.3 = bf16[26,1,128]{2,1,0:T(2,128)(2,1)S(1)} collective-permute-done((bf16[26,1,128]{2,1,0:T(2,128)(2,1)S(1)}, bf16[26,1,128]{2,1,0:T(2,128)(2,1)S(1)}, u32[]{:S(2)}, u32[]{:S(2)}) %collective-permute-start.3) | collective-permute-done | bytes 6688 | tf_op jit(solution)/shard_map/ppermute | solution.py:15
  48.3 0.8 convolution_convert_fusion
  49.2 0.8 convolution_convert_fusion.1
  50.4 0.2 fusion.28
  50.8 0.4 fusion.26
  51.3 0.3 fusion.62
  51.7 1.7 %fusion.14 = bf16[576,128]{1,0:T(8,128)(2,1)S(1)} fusion(s32[1024]{0:T(1024)S(1)} %copy-done.7, f32[1024,128]{0,1:T(8,128)S(1)} %get-tuple-element.117, f32[1024]{0:T(1024)S(1)} %fusion.44, f32[128]{0:T(128)S(1)} %reshape.285, f32[1024]{0:T(1024)S(1)} %add_rsqrt_fusion.1, f32[1024]{0:T(1024)S(1)} %broadcast_multiply_fusion.6), kind=kOutput, calls=%fused_computation.20 | convolution fusion | flops 907747328 | bytes 688640 | tf_op jit(solution)/shard_map/dot_general | solution.py:152
  53.4 0.2 fusion.36
  53.6 0.3 fusion.63
  54.0 0.3 multiply_reduce_fusion.5
  54.2 0.4 fusion.29
  54.6 0.4 multiply_convert_fusion.1
  55.0 0.2 fusion.13
  55.2 1.0 fusion.35
  56.1 0.2 fusion.64
  56.4 1.9 %multiply_reduce_fusion = (f32[128]{0:T(128)S(1)}, f32[1024]{0:T(1024)S(1)}, f32[1024]{0:T(1024)S(1)}, f32[1024,128]{0,1:T(8,128)S(1)}) fusion(f32[1024,128]{0,1:T(8,128)S(1)} %get-tuple-element.117, f32[1024]{0:T(1024)S(1)} %add_rsqrt_fusion.1, f32[1024]{0:T(1024)S(1)} %broadcast_multiply_fusion.6, f32[128]{0:T(128)S(1)} %reshape.285, ...), kind=kOutput, calls=%fused_computation.31 | convolution fusion | flops 907999104 | bytes 1631232 | tf_op jit(solution)/shard_map/dot_general | solution.py:146
  58.3 0.2 multiply_convert_fusion
  58.5 0.3 fusion.12
  58.7 0.5 copy-done.9
  59.3 0.4 fusion.25
  59.7 0.4 fusion.65
  60.4 0.3 fusion.18
  60.7 0.9 constant_dynamic-update-slice_fusion.8
  61.6 0.2 fusion.17
  61.9 0.8 copy-done.3
  62.7 1.5 dynamic-update-slice.16
  64.2 12.0 %all-to-all-start.1 = ((f32[16,57,128]{2,1,0:T(8,128)}), f32[16,57,128]{2,1,0:T(8,128)S(1)}, u32[]{:S(2)}, u32[]{:S(2)}) async-start(f32[16,57,128]{2,1,0:T(8,128)} %dynamic-update-slice.16), calls=%async_computation.1 | async-start | bytes 1048576 | tf_op jit(solution)/shard_map/all_to_all | solution.py:87
  76.2 1.1 fusion.55
  77.3 0.2 copy.84
  77.5 6.7 %fusion = f32[676,128]{1,0:T(8,128)S(1)} fusion(pred[1024,676]{1,0:T(32,128)(4,1)} %get-tuple-element.121, pred[1024,676]{1,0:T(32,128)(4,1)} %get-tuple-element.122, f32[1024,128]{1,0:T(8,128)} %get-tuple-element.96, f32[1024,128]{1,0:T(8,128)} %get-tuple-element.97), kind=kOutput, calls=%fused_computation | convolution fusion | flops 2128158720 | bytes 2779136 | tf_op jit(solution)/shard_map/dot_general | solution.py:152
  84.4 9.7 %collective-permute-start.5 = (bf16[1,2,24,128]{3,2,1,0:T(8,128)(2,1)S(1)}, bf16[1,2,24,128]{3,2,1,0:T(8,128)(2,1)S(1)}, u32[]{:S(2)}, u32[]{:S(2)}) collective-permute-start(bf16[1,2,24,128]{3,2,1,0:T(8,128)(2,1)S(1)} %maximum_bitcast_fusion.2), channel_id=1, source_target_pairs={{48,0},{96,48},{144,96},{192,144},{240,192},{288,240},{336,288},{3... | collective-permute-start | bytes 36872 | tf_op jit(solution)/shard_map/ppermute | solution.py:15
  94.2 1.9 %collective-permute-start.4 = (bf16[1,2,24,128]{3,2,1,0:T(8,128)(2,1)S(1)}, bf16[1,2,24,128]{3,2,1,0:T(8,128)(2,1)S(1)}, u32[]{:S(2)}, u32[]{:S(2)}) collective-permute-start(bf16[1,2,24,128]{3,2,1,0:T(8,128)(2,1)S(1)} %maximum_bitcast_fusion.1), channel_id=1, source_target_pairs={{0,48},{48,96},{96,144},{144,192},{192,240},{240,288},{288,336},{3... | collective-permute-start | bytes 36872 | tf_op jit(solution)/shard_map/ppermute | solution.py:12
  96.2 10.2 %collective-permute-done.4 = bf16[1,2,24,128]{3,2,1,0:T(8,128)(2,1)S(1)} collective-permute-done((bf16[1,2,24,128]{3,2,1,0:T(8,128)(2,1)S(1)}, bf16[1,2,24,128]{3,2,1,0:T(8,128)(2,1)S(1)}, u32[]{:S(2)}, u32[]{:S(2)}) %collective-permute-start.4) | collective-permute-done | bytes 12320 | tf_op jit(solution)/shard_map/ppermute | solution.py:12
  106.4 3.5 %collective-permute-start.6 = (bf16[4,1,24,128]{3,2,1,0:T(8,128)(2,1)S(1)}, bf16[4,1,24,128]{3,2,1,0:T(8,128)(2,1)S(1)}, u32[]{:S(2)}, u32[]{:S(2)}) collective-permute-start(bf16[4,1,24,128]{3,2,1,0:T(8,128)(2,1)S(1)} %get-tuple-element.108), channel_id=1, source_target_pairs={{0,1},{1,2},{2,3},{3,4},{4,5},{5,6},{6,7},{7,8},{8,9},{9,10},{10,1... | collective-permute-start | bytes 73736 | tf_op jit(solution)/shard_map/ppermute | solution.py:12
  109.9 1.3 collective-permute-start.7
  111.3 0.8 copy.78
  112.2 3.8 %collective-permute-done.7 = bf16[4,1,24,128]{3,2,1,0:T(8,128)(2,1)S(1)} collective-permute-done((bf16[4,1,24,128]{3,2,1,0:T(8,128)(2,1)S(1)}, bf16[4,1,24,128]{3,2,1,0:T(8,128)(2,1)S(1)}, u32[]{:S(2)}, u32[]{:S(2)}) %collective-permute-start.7) | collective-permute-done | bytes 24608 | tf_op jit(solution)/shard_map/ppermute | solution.py:15
  116.2 0.7 broadcast_in_dim.18
  116.9 6.8 %all-to-all-start.2 = ((f32[8,57,128]{2,1,0:T(8,128)}), f32[8,57,128]{2,1,0:T(8,128)S(1)}, u32[]{:S(2)}, u32[]{:S(2)}) async-start(f32[8,57,128]{2,1,0:T(8,128)} %broadcast_in_dim.18), calls=%async_computation.2 | async-start | bytes 524288 | tf_op jit(solution)/shard_map/all_to_all | solution.py:95
  123.8 10.4 %all-to-all-done.2 = f32[8,57,128]{2,1,0:T(8,128)S(1)} async-done(((f32[8,57,128]{2,1,0:T(8,128)}), f32[8,57,128]{2,1,0:T(8,128)S(1)}, u32[]{:S(2)}, u32[]{:S(2)}) %all-to-all-start.2) | async-done | bytes 233504 | tf_op jit(solution)/shard_map/all_to_all | solution.py:95
  134.2 0.7 broadcast_in_dim.19
  134.8 6.2 %all-to-all-start.3 = ((f32[6,57,128]{2,1,0:T(8,128)}), f32[6,57,128]{2,1,0:T(8,128)S(1)}, u32[]{:S(2)}, u32[]{:S(2)}) async-start(f32[6,57,128]{2,1,0:T(8,128)} %broadcast_in_dim.19), calls=%async_computation.3 | async-start | bytes 393216 | tf_op jit(solution)/shard_map/all_to_all | solution.py:95
  141.1 0.7 copy.77
  141.8 9.7 %all-to-all-done.3 = f32[6,57,128]{2,1,0:T(8,128)S(1)} async-done(((f32[6,57,128]{2,1,0:T(8,128)}), f32[6,57,128]{2,1,0:T(8,128)S(1)}, u32[]{:S(2)}, u32[]{:S(2)}) %all-to-all-start.3) | async-done | bytes 175136 | tf_op jit(solution)/shard_map/all_to_all | solution.py:95
  151.6 0.6 slice.256
  152.2 0.6 fusion.61
  152.8 0.6 slice.254
  153.4 0.6 reshape_squeeze.7
  (91 shorter events, 2.1 us)
Async XLA Ops:
  0.6 38.3 %copy-start.4 = (bf16[24,24,128]{2,1,0:T(8,128)(2,1)S(1)}, bf16[24,24,128]{2,1,0:T(8,128)(2,1)}, u32[]{:S(2)}) copy-start(bf16[24,24,128]{2,1,0:T(8,128)(2,1)} %param.20) | copy-start | bytes 442372
  0.6 43.2 %copy-start.5 = (bf16[1024,128]{1,0:T(8,128)(2,1)S(1)}, bf16[1024,128]{1,0:T(8,128)(2,1)}, u32[]{:S(2)}) copy-start(bf16[1024,128]{1,0:T(8,128)(2,1)} %param.21) | copy-start | bytes 786436
  1.4 37.6 %collective-permute-start.1 = (bf16[1,24,128]{2,1,0:T(8,128)(2,1)S(1)}, bf16[1,24,128]{2,1,0:T(8,128)(2,1)S(1)}, u32[]{:S(2)}, u32[]{:S(2)}) collective-permute-start(bf16[1,24,128]{2,1,0:T(8,128)(2,1)S(1)} %get-tuple-element.104), channel_id=1, source_target_pairs={{48,0},{96,48},{144,96},{192,144},{240,192},{288,240},{336,288},{3... | collective-permute-start | bytes 18440 | tf_op jit(solution)/shard_map/ppermute | solution.py:15
  16.3 22.7 %collective-permute-start = (bf16[1,24,128]{2,1,0:T(8,128)(2,1)S(1)}, bf16[1,24,128]{2,1,0:T(8,128)(2,1)S(1)}, u32[]{:S(2)}, u32[]{:S(2)}) collective-permute-start(bf16[1,24,128]{2,1,0:T(8,128)(2,1)S(1)} %get-tuple-element.105), channel_id=1, source_target_pairs={{0,48},{48,96},{96,144},{144,192},{192,240},{240,288},{288,336},{3... | collective-permute-start | bytes 18440 | tf_op jit(solution)/shard_map/ppermute | solution.py:12
  22.5 21.6 %copy-start.6 = (bf16[1024,128]{1,0:T(8,128)(2,1)S(1)}, bf16[1024,128]{1,0:T(8,128)(2,1)}, u32[]{:S(2)}) copy-start(bf16[1024,128]{1,0:T(8,128)(2,1)} %param.31) | copy-start | bytes 786436
  22.5 27.6 %all-to-all-start = ((bf16[16,57,128]{2,1,0:T(8,128)(2,1)}), bf16[16,57,128]{2,1,0:T(8,128)(2,1)S(1)}, u32[]{:S(2)}, u32[]{:S(2)}) async-start(bf16[16,57,128]{2,1,0:T(8,128)(2,1)} %broadcast_in_dim.17), calls=%async_computation | async-start | bytes 524288 | tf_op jit(solution)/shard_map/all_to_all | solution.py:83
  39.1 5.1 %collective-permute-start.2 = (bf16[26,1,128]{2,1,0:T(2,128)(2,1)S(1)}, bf16[26,1,128]{2,1,0:T(2,128)(2,1)S(1)}, u32[]{:S(2)}, u32[]{:S(2)}) collective-permute-start(bf16[26,1,128]{2,1,0:T(2,128)(2,1)S(1)} %get-tuple-element.102), channel_id=1, source_target_pairs={{0,1},{1,2},{2,3},{3,4},{4,5},{5,6},{6,7},{7,8},{8,9},{9,10},{10,1... | collective-permute-start | bytes 19976 | tf_op jit(solution)/shard_map/ppermute | solution.py:12
  42.6 5.6 %collective-permute-start.3 = (bf16[26,1,128]{2,1,0:T(2,128)(2,1)S(1)}, bf16[26,1,128]{2,1,0:T(2,128)(2,1)S(1)}, u32[]{:S(2)}, u32[]{:S(2)}) collective-permute-start(bf16[26,1,128]{2,1,0:T(2,128)(2,1)S(1)} %get-tuple-element.103), channel_id=1, source_target_pairs={{1,0},{2,1},{3,2},{4,3},{5,4},{6,5},{7,6},{8,7},{9,8},{10,9},{11,1... | collective-permute-start | bytes 19976 | tf_op jit(solution)/shard_map/ppermute | solution.py:15
  48.3 2.0 %copy-start = (bf16[24,24,128]{2,1,0:T(8,128)(2,1)S(1)}, bf16[24,24,128]{2,1,0:T(8,128)(2,1)}, u32[]{:S(2)}) copy-start(bf16[24,24,128]{2,1,0:T(8,128)(2,1)} %param.30) | copy-start | bytes 442372
  49.2 1.6 %copy-start.8 = (bf16[1024,128]{0,1:T(8,128)(2,1)}, bf16[1024,128]{0,1:T(8,128)(2,1)S(1)}, u32[]{:S(2)}) copy-start(bf16[1024,128]{0,1:T(8,128)(2,1)S(1)} %convolution_convert_fusion) | copy-start | bytes 786436
  50.0 1.2 copy-start.10
  50.8 0.8 copy-start.7
  56.4 2.1 %copy-start.1 = (f32[576,256]{1,0:T(8,128)}, f32[576,256]{1,0:T(8,128)S(1)}, u32[]{:S(2)}) copy-start(f32[576,256]{1,0:T(8,128)S(1)} %fusion.64) | copy-start | bytes 1769476
  58.3 1.0 copy-start.9
  58.3 1.0 copy-start.11
  61.9 0.8 copy-start.3
  64.2 51.9 %all-to-all-start.1 = ((f32[16,57,128]{2,1,0:T(8,128)}), f32[16,57,128]{2,1,0:T(8,128)S(1)}, u32[]{:S(2)}, u32[]{:S(2)}) async-start(f32[16,57,128]{2,1,0:T(8,128)} %dynamic-update-slice.16), calls=%async_computation.1 | async-start | bytes 1048576 | tf_op jit(solution)/shard_map/all_to_all | solution.py:87
  84.3 27.0 %copy-start.2 = (f32[576,256]{1,0:T(8,128)S(1)}, f32[576,256]{1,0:T(8,128)}, u32[]{:S(2)}) copy-start(f32[576,256]{1,0:T(8,128)} %copy-done.1) | copy-start | bytes 1769476
  84.4 11.7 %collective-permute-start.5 = (bf16[1,2,24,128]{3,2,1,0:T(8,128)(2,1)S(1)}, bf16[1,2,24,128]{3,2,1,0:T(8,128)(2,1)S(1)}, u32[]{:S(2)}, u32[]{:S(2)}) collective-permute-start(bf16[1,2,24,128]{3,2,1,0:T(8,128)(2,1)S(1)} %maximum_bitcast_fusion.2), channel_id=1, source_target_pairs={{48,0},{96,48},{144,96},{192,144},{240,192},{288,240},{336,288},{3... | collective-permute-start | bytes 36872 | tf_op jit(solution)/shard_map/ppermute | solution.py:15
  94.2 12.2 %collective-permute-start.4 = (bf16[1,2,24,128]{3,2,1,0:T(8,128)(2,1)S(1)}, bf16[1,2,24,128]{3,2,1,0:T(8,128)(2,1)S(1)}, u32[]{:S(2)}, u32[]{:S(2)}) collective-permute-start(bf16[1,2,24,128]{3,2,1,0:T(8,128)(2,1)S(1)} %maximum_bitcast_fusion.1), channel_id=1, source_target_pairs={{0,48},{48,96},{96,144},{144,192},{192,240},{240,288},{288,336},{3... | collective-permute-start | bytes 36872 | tf_op jit(solution)/shard_map/ppermute | solution.py:12
  106.4 5.8 %collective-permute-start.6 = (bf16[4,1,24,128]{3,2,1,0:T(8,128)(2,1)S(1)}, bf16[4,1,24,128]{3,2,1,0:T(8,128)(2,1)S(1)}, u32[]{:S(2)}, u32[]{:S(2)}) collective-permute-start(bf16[4,1,24,128]{3,2,1,0:T(8,128)(2,1)S(1)} %get-tuple-element.108), channel_id=1, source_target_pairs={{0,1},{1,2},{2,3},{3,4},{4,5},{5,6},{6,7},{7,8},{8,9},{9,10},{10,1... | collective-permute-start | bytes 73736 | tf_op jit(solution)/shard_map/ppermute | solution.py:12
  109.9 6.1 %collective-permute-start.7 = (bf16[4,1,24,128]{3,2,1,0:T(8,128)(2,1)S(1)}, bf16[4,1,24,128]{3,2,1,0:T(8,128)(2,1)S(1)}, u32[]{:S(2)}, u32[]{:S(2)}) collective-permute-start(bf16[4,1,24,128]{3,2,1,0:T(8,128)(2,1)S(1)} %get-tuple-element.109), channel_id=1, source_target_pairs={{1,0},{2,1},{3,2},{4,3},{5,4},{6,5},{7,6},{8,7},{9,8},{10,9},{11,1... | collective-permute-start | bytes 73736 | tf_op jit(solution)/shard_map/ppermute | solution.py:15
  116.9 17.3 %all-to-all-start.2 = ((f32[8,57,128]{2,1,0:T(8,128)}), f32[8,57,128]{2,1,0:T(8,128)S(1)}, u32[]{:S(2)}, u32[]{:S(2)}) async-start(f32[8,57,128]{2,1,0:T(8,128)} %broadcast_in_dim.18), calls=%async_computation.2 | async-start | bytes 524288 | tf_op jit(solution)/shard_map/all_to_all | solution.py:95
  134.8 16.7 %all-to-all-start.3 = ((f32[6,57,128]{2,1,0:T(8,128)}), f32[6,57,128]{2,1,0:T(8,128)S(1)}, u32[]{:S(2)}, u32[]{:S(2)}) async-start(f32[6,57,128]{2,1,0:T(8,128)} %broadcast_in_dim.19), calls=%async_computation.3 | async-start | bytes 393216 | tf_op jit(solution)/shard_map/all_to_all | solution.py:95

commit v9 on v8

--- a/solution.py
+++ b/solution.py
@@ -136,6 +136,15 @@
     return tuple(outs)
 
 
+def shift_in(value, axis, step):
+    count = axis_count(axis)
+    if step > 0:
+        pairs = [(i, i + 1) for i in range(count - 1)]
+    else:
+        pairs = [(i + 1, i) for i in range(count - 1)]
+    return lax.ppermute(value.astype(jnp.bfloat16), axis, pairs).astype(value.dtype)
+
+
 def one_hot(index, count):
     return (index[:, None] == jnp.arange(count, dtype=index.dtype)[None, :]).astype(jnp.bfloat16)
 
@@ -180,7 +189,13 @@
     block_side = node_feat.shape[0]
     latent = node_feat.shape[2]
     padded_side = block_side + 2
-    padded = with_halo(node_feat, (("dom", 0), (SUB, 1)), 1).reshape(
+    top = shift_in(node_feat[-1], "dom", 1)
+    bottom = shift_in(node_feat[0], "dom", -1)
+    left = shift_in(node_feat[:, -1], SUB, 1)
+    right = shift_in(node_feat[:, 0], SUB, -1)
+    middle = jnp.concatenate([left[:, None], node_feat, right[:, None]], axis=1)
+    edge_rows = jnp.pad(jnp.stack([top, bottom]), ((0, 0), (1, 1), (0, 0)))
+    padded = jnp.concatenate([edge_rows[:1], middle, edge_rows[1:]], axis=0).reshape(
         padded_side * padded_side, latent
     )
     node_row = edge_dst // block_side
@@ -231,18 +246,13 @@
         jnp.concatenate([edge_in_grad[:, latent : 2 * latent], edge_in_grad[:, 2 * latent :]], axis=0),
     )
     spread = spread.reshape(padded_side, padded_side, latent)
-    outgoing = jnp.stack(
-        [
-            jnp.stack([spread[1:-1, 0], spread[0, 1:-1]]),
-            jnp.stack([spread[-1, 1:-1], spread[1:-1, -1]]),
-        ]
-    )
-    incoming = with_halo(outgoing.astype(jnp.bfloat16), (("dom", 0), (SUB, 1)), 1).astype(
-        outgoing.dtype
-    )
     inner = spread[1:-1, 1:-1]
-    inner = inner.at[0].add(incoming[0, 1]).at[-1].add(incoming[3, 2])
-    inner = inner.at[:, 0].add(incoming[2, 0]).at[:, -1].add(incoming[1, 3])
+    from_prev_dom = shift_in(spread[-1, 1:-1], "dom", 1)
+    from_next_dom = shift_in(spread[0, 1:-1], "dom", -1)
+    from_prev_sub = shift_in(spread[1:-1, -1], SUB, 1)
+    from_next_sub = shift_in(spread[1:-1, 0], SUB, -1)
+    inner = inner.at[0].add(from_prev_dom).at[-1].add(from_next_dom)
+    inner = inner.at[:, 0].add(from_prev_sub).at[:, -1].add(from_next_sub)
     node_total = node_upstream + node_in_grad[:, :latent]
     node_grad = (node_total.reshape(block_side, block_side, latent) + inner).astype(jnp.bfloat16)
     nodes_all = block_side * block_side * lax.axis_size("dom") * axis_count(SUB)

time: 155 us -> 150 us (0.968)
  waiting for transfers between devices: 38 us -> 26.3 us
  starting transfers between devices: 76 us -> 80.2 us
    ppermute x8, waiting for transfers between devices: 17.9 us -> 0.02 us  [shift_in(): lax.ppermute(value.astype(jnp.bfloat16), axis, pairs).astype(value.dtype)]
    all_to_all x1, waiting for transfers between devices: 0.01 us -> 6.48 us  [gather_dom(): return lax.all_to_all(spread, 'dom', 0, 0, tiled=True)]
    all_to_all x2, starting transfers between devices: 13 us -> 18.3 us  [sum_sub(): total = jnp.sum(lax.all_to_all(spread, axis, 0, 0, tiled=True), axis=0)]
    all_to_all x1, starting transfers between devices: 12 us -> 8.49 us  [reduce_scatter_dom(): return jnp.sum(lax.all_to_all(packed, 'dom', 0, 0, tiled=True), axis=0)]
    ppermute x8, starting transfers between devices: 37.9 us -> 40.6 us  [shift_in(): lax.ppermute(value.astype(jnp.bfloat16), axis, pairs).astype(value.dtype)]
    unnamed x41 -> x33, local copies, waits for them, and re-layouts: 7.28 us -> 6.99 us
  transfers between devices with their start and end apart: 12 -> 12, of which waited for: 5 -> 3; matrix products, arithmetic and copies ran while one was open for 13% -> 15% of each run, Pallas kernels for 0% -> 0%
where the time goes in v9:
time: 150 us; the launch traced here: 149 us
  starting transfers between devices  80.2 us (53%)
  waiting for transfers between devices  26.3 us (18%)
  local copies, waits for them, and re-layouts  18.2 us (12%)
  matrix products  17.4 us (12%)
  other arithmetic  5.31 us (4%)
  between operations  1.99 us (1%)
    ppermute x8, starting transfers between devices, shift_in(): lax.ppermute(value.astype(jnp.bfloat16), axis, pairs).astype(value.dtype)  40.6 us
    all_to_all x2, waiting for transfers between devices, sum_sub(): total = jnp.sum(lax.all_to_all(spread, axis, 0, 0, tiled=True), axis=0)  19.8 us
    all_to_all x2, starting transfers between devices, sum_sub(): total = jnp.sum(lax.all_to_all(spread, axis, 0, 0, tiled=True), axis=0)  18.3 us
    all_to_all x1, starting transfers between devices, gather_dom(): return lax.all_to_all(spread, 'dom', 0, 0, tiled=True)  12.7 us
    all_to_all x1, starting transfers between devices, reduce_scatter_dom(): return jnp.sum(lax.all_to_all(packed, 'dom', 0, 0, tiled=True), axis=0)  8.49 us
    dot_general x2, matrix products, sum_rows(): lax.dot_general(pick.astype(jnp.float32), values, (((0,), (0,)), ((), ())...  8.44 us
    unnamed x33, local copies, waits for them, and re-layouts  6.99 us
    all_to_all x1, waiting for transfers between devices, gather_dom(): return lax.all_to_all(spread, 'dom', 0, 0, tiled=True)  6.48 us
  transfers between devices with their start and end apart: 12, of which 3 were waited for; matrix products, arithmetic and copies ran while one was open for 15% of the time, Pallas kernels for 0%

profile of v9, /device:TPU:6, one launch (start us, length us, event | category | flops | bytes accessed | tf_op | source)
XLA Modules:
  0.0 149.3 jit_solution(10213609158934892098)
XLA Ops:
  0.7 0.8 slice_bitcast_fusion.9
  1.4 1.9 %collective-permute-start = (bf16[24,128]{1,0:T(8,128)(2,1)S(1)}, bf16[24,128]{1,0:T(8,128)(2,1)S(1)}, u32[]{:S(2)}, u32[]{:S(2)}) collective-permute-start(bf16[24,128]{1,0:T(8,128)(2,1)S(1)} %get-tuple-element.104), channel_id=1, source_target_pairs={{0,48},{48,96},{96,144},{144,192},{192,240},{240,288},{288,336},{3... | collective-permute-start | bytes 18440 | tf_op jit(solution)/shard_map/ppermute | solution.py:145
  3.3 14.8 %collective-permute-start.1 = (bf16[24,128]{1,0:T(8,128)(2,1)S(1)}, bf16[24,128]{1,0:T(8,128)(2,1)S(1)}, u32[]{:S(2)}, u32[]{:S(2)}) collective-permute-start(bf16[24,128]{1,0:T(8,128)(2,1)S(1)} %get-tuple-element.105), channel_id=1, source_target_pairs={{48,0},{96,48},{144,96},{192,144},{240,192},{288,240},{336,288},{3... | collective-permute-start | bytes 18440 | tf_op jit(solution)/shard_map/ppermute | solution.py:145
  18.2 0.8 fusion.58
  19.1 1.3 collective-permute-start.3
  20.4 4.5 %collective-permute-start.2 = (bf16[24,128]{1,0:T(8,128)(2,1)S(1)}, bf16[24,128]{1,0:T(8,128)(2,1)S(1)}, u32[]{:S(2)}, u32[]{:S(2)}) collective-permute-start(bf16[24,128]{1,0:T(8,128)(2,1)S(1)} %bitcast.106), channel_id=1, source_target_pairs={{0,1},{1,2},{2,3},{3,4},{4,5},{5,6},{6,7},{7,8},{8,9},{9,10},{10,1... | collective-permute-start | bytes 18440 | tf_op jit(solution)/shard_map/ppermute | solution.py:145
  24.9 0.7 reshape.276
  25.7 0.7 constant_dynamic-update-slice_fusion.4
  26.4 0.7 constant_dynamic-update-slice_fusion.3
  27.0 0.7 constant_dynamic-update-slice_fusion.2
  27.7 0.7 constant_dynamic-update-slice_fusion.1
  28.4 0.8 broadcast_in_dim.23
  29.2 12.7 %all-to-all-start = ((bf16[16,57,128]{2,1,0:T(8,128)(2,1)}), bf16[16,57,128]{2,1,0:T(8,128)(2,1)S(1)}, u32[]{:S(2)}, u32[]{:S(2)}) async-start(bf16[16,57,128]{2,1,0:T(8,128)(2,1)} %broadcast_in_dim.23), calls=%async_computation | async-start | bytes 524288 | tf_op jit(solution)/shard_map/all_to_all | solution.py:83
  42.5 0.7 select_add_fusion
  43.3 2.1 %iota_compare_fusion = (pred[1024,676]{1,0:T(32,128)(4,1)}, pred[1024,676]{1,0:T(32,128)(4,1)}) fusion(s32[1024]{0:T(1024)S(1)} %get-tuple-element.113, s32[1024]{0:T(1024)S(1)} %get-tuple-element.112), kind=kLoop, calls=%fused_computation.4 | loop fusion | flops 1384448 | bytes 1392640 | tf_op jit(solution)/shard_map/eq | solution.py:149
  45.4 0.1 copy.95
  46.0 0.8 convolution_convert_fusion
  46.8 0.8 convolution_convert_fusion.1
  47.7 6.5 %all-to-all-done = bf16[16,57,128]{2,1,0:T(8,128)(2,1)S(1)} async-done(((bf16[16,57,128]{2,1,0:T(8,128)(2,1)}), bf16[16,57,128]{2,1,0:T(8,128)(2,1)S(1)}, u32[]{:S(2)}, u32[]{:S(2)}) %all-to-all-start) | async-done | bytes 233504 | tf_op jit(solution)/shard_map/all_to_all | solution.py:83
  54.4 0.2 fusion.28
  54.9 0.4 fusion.26
  55.4 0.3 fusion.61
  55.7 1.7 %fusion.14 = bf16[576,128]{1,0:T(8,128)(2,1)S(1)} fusion(s32[1024]{0:T(1024)S(1)} %copy-done.6, f32[1024,128]{0,1:T(8,128)S(1)} %get-tuple-element.115, f32[1024]{0:T(1024)S(1)} %fusion.45, f32[128]{0:T(128)S(1)} %reshape.293, f32[1024]{0:T(1024)S(1)} %add_rsqrt_fusion.1, f32[1024]{0:T(1024)S(1)} %broadcast_multiply_fusion.6), kind=kOutput, calls=%fused_computation.20 | convolution fusion | flops 907747328 | bytes 688640 | tf_op jit(solution)/shard_map/dot_general | solution.py:161
  57.5 0.2 fusion.35
  57.7 0.3 fusion.62
  58.0 0.3 multiply_reduce_fusion.5
  58.3 0.4 fusion.29
  58.7 0.4 multiply_convert_fusion.1
  59.1 0.2 fusion.13
  59.3 1.0 fusion.34
  60.2 0.2 fusion.63
  60.5 1.9 %multiply_reduce_fusion = (f32[128]{0:T(128)S(1)}, f32[1024]{0:T(1024)S(1)}, f32[1024]{0:T(1024)S(1)}, f32[1024,128]{0,1:T(8,128)S(1)}) fusion(f32[1024,128]{0,1:T(8,128)S(1)} %get-tuple-element.115, f32[1024]{0:T(1024)S(1)} %add_rsqrt_fusion.1, f32[1024]{0:T(1024)S(1)} %broadcast_multiply_fusion.6, f32[128]{0:T(128)S(1)} %reshape.293, ...), kind=kOutput, calls=%fused_computation.31 | convolution fusion | flops 907999104 | bytes 1631232 | tf_op jit(solution)/shard_map/dot_general | solution.py:155
  62.4 0.2 multiply_convert_fusion
  62.5 0.3 fusion.12
  62.8 0.5 copy-done.8
  63.3 0.4 fusion.25
  63.7 0.4 fusion.64
  64.4 0.7 constant_dynamic-update-slice_fusion.6
  65.1 0.9 fusion.18
  66.0 1.6 %constant_dynamic-update-slice_fusion.5 = f32[16,57,128]{2,1,0:T(8,128)} fusion(f32[16,57,128]{2,1,0:T(8,128)} %fusion.18, f32[16,16,128]{2,1,0:T(8,128)} %bitcast.95), kind=kLoop, calls=%fused_computation.77 | loop fusion | bytes 262144
  67.6 0.9 fusion.17
  68.4 1.5 %dynamic-update-slice.16 = f32[16,57,128]{2,1,0:T(8,128)} dynamic-update-slice(f32[16,57,128]{2,1,0:T(8,128)} %fusion.17, f32[16,1,128]{2,1,0:T(1,128)S(1)} %pad.22.clone, s32[]{} %constant.178, s32[]{} %constant.182, s32[]{} %constant.178) | dynamic-update-slice | bytes 16388 | tf_op jit(solution)/shard_map/concatenate | solution.py:126
  69.9 8.5 %all-to-all-start.1 = ((f32[16,57,128]{2,1,0:T(8,128)}), f32[16,57,128]{2,1,0:T(8,128)S(1)}, u32[]{:S(2)}, u32[]{:S(2)}) async-start(f32[16,57,128]{2,1,0:T(8,128)} %dynamic-update-slice.16), calls=%async_computation.1 | async-start | bytes 1048576 | tf_op jit(solution)/shard_map/all_to_all | solution.py:87
  78.4 1.1 fusion.56
  79.5 0.2 copy.117
  79.7 6.7 %fusion = f32[676,128]{1,0:T(8,128)S(1)} fusion(pred[1024,676]{1,0:T(32,128)(4,1)} %get-tuple-element.119, pred[1024,676]{1,0:T(32,128)(4,1)} %get-tuple-element.120, f32[1024,128]{1,0:T(8,128)} %get-tuple-element.96, f32[1024,128]{1,0:T(8,128)} %get-tuple-element.97), kind=kOutput, calls=%fused_computation | convolution fusion | flops 2128158720 | bytes 2779136 | tf_op jit(solution)/shard_map/dot_general | solution.py:161
  86.5 0.2 copy.124
  86.8 2.1 %collective-permute-start.4 = (bf16[24,128]{1,0:T(8,128)(2,1)S(1)}, bf16[24,128]{1,0:T(8,128)(2,1)S(1)}, u32[]{:S(2)}, u32[]{:S(2)}) collective-permute-start(bf16[24,128]{1,0:T(8,128)(2,1)S(1)} %bitcast.109), channel_id=1, source_target_pairs={{0,48},{48,96},{96,144},{144,192},{192,240},{240,288},{288,336},{3... | collective-permute-start | bytes 18440 | tf_op jit(solution)/shard_map/ppermute | solution.py:145
  89.0 0.2 copy.100
  89.2 0.8 copy.111
  90.0 1.3 collective-permute-start.7
  91.3 4.5 %collective-permute-start.6 = (bf16[24,128]{1,0:T(8,128)(2,1)S(1)}, bf16[24,128]{1,0:T(8,128)(2,1)S(1)}, u32[]{:S(2)}, u32[]{:S(2)}) collective-permute-start(bf16[24,128]{1,0:T(8,128)(2,1)S(1)} %get-tuple-element.99), channel_id=1, source_target_pairs={{0,1},{1,2},{2,3},{3,4},{4,5},{5,6},{6,7},{7,8},{8,9},{9,10},{10,1... | collective-permute-start | bytes 18440 | tf_op jit(solution)/shard_map/ppermute | solution.py:145
  95.9 10.2 %collective-permute-start.5 = (bf16[24,128]{1,0:T(8,128)(2,1)S(1)}, bf16[24,128]{1,0:T(8,128)(2,1)S(1)}, u32[]{:S(2)}, u32[]{:S(2)}) collective-permute-start(bf16[24,128]{1,0:T(8,128)(2,1)S(1)} %bitcast.108), channel_id=1, source_target_pairs={{48,0},{96,48},{144,96},{192,144},{240,192},{288,240},{336,288},{3... | collective-permute-start | bytes 18440 | tf_op jit(solution)/shard_map/ppermute | solution.py:145
  106.1 0.7 broadcast_in_dim.24
  106.8 7.1 %all-to-all-start.2 = ((f32[8,57,128]{2,1,0:T(8,128)}), f32[8,57,128]{2,1,0:T(8,128)S(1)}, u32[]{:S(2)}, u32[]{:S(2)}) async-start(f32[8,57,128]{2,1,0:T(8,128)} %broadcast_in_dim.24), calls=%async_computation.2 | async-start | bytes 524288 | tf_op jit(solution)/shard_map/all_to_all | solution.py:95
  114.2 10.2 %all-to-all-done.2 = f32[8,57,128]{2,1,0:T(8,128)S(1)} async-done(((f32[8,57,128]{2,1,0:T(8,128)}), f32[8,57,128]{2,1,0:T(8,128)S(1)}, u32[]{:S(2)}, u32[]{:S(2)}) %all-to-all-start.2) | async-done | bytes 233504 | tf_op jit(solution)/shard_map/all_to_all | solution.py:95
  124.5 0.7 broadcast_in_dim.25
  125.2 11.2 %all-to-all-start.3 = ((f32[6,57,128]{2,1,0:T(8,128)}), f32[6,57,128]{2,1,0:T(8,128)S(1)}, u32[]{:S(2)}, u32[]{:S(2)}) async-start(f32[6,57,128]{2,1,0:T(8,128)} %broadcast_in_dim.25), calls=%async_computation.3 | async-start | bytes 393216 | tf_op jit(solution)/shard_map/all_to_all | solution.py:95
  136.6 0.7 add_convert_fusion
  137.3 9.6 %all-to-all-done.3 = f32[6,57,128]{2,1,0:T(8,128)S(1)} async-done(((f32[6,57,128]{2,1,0:T(8,128)}), f32[6,57,128]{2,1,0:T(8,128)S(1)}, u32[]{:S(2)}, u32[]{:S(2)}) %all-to-all-start.3) | async-done | bytes 175136 | tf_op jit(solution)/shard_map/all_to_all | solution.py:95
  146.9 0.6 slice.236
  147.5 0.6 fusion.59
  148.1 0.6 slice.234
  148.7 0.6 reshape_squeeze.7
  (87 shorter events, 2.1 us)
Async XLA Ops:
  0.6 44.7 %copy-start.4 = (bf16[1024,128]{1,0:T(8,128)(2,1)S(1)}, bf16[1024,128]{1,0:T(8,128)(2,1)}, u32[]{:S(2)}) copy-start(bf16[1024,128]{1,0:T(8,128)(2,1)} %param.21) | copy-start | bytes 786436
  0.6 44.9 %copy-start.5 = (bf16[1024,128]{1,0:T(8,128)(2,1)S(1)}, bf16[1024,128]{1,0:T(8,128)(2,1)}, u32[]{:S(2)}) copy-start(bf16[1024,128]{1,0:T(8,128)(2,1)} %param.31) | copy-start | bytes 786436
  1.4 44.3 %collective-permute-start = (bf16[24,128]{1,0:T(8,128)(2,1)S(1)}, bf16[24,128]{1,0:T(8,128)(2,1)S(1)}, u32[]{:S(2)}, u32[]{:S(2)}) collective-permute-start(bf16[24,128]{1,0:T(8,128)(2,1)S(1)} %get-tuple-element.104), channel_id=1, source_target_pairs={{0,48},{48,96},{96,144},{144,192},{192,240},{240,288},{288,336},{3... | collective-permute-start | bytes 18440 | tf_op jit(solution)/shard_map/ppermute | solution.py:145
  3.3 42.3 %collective-permute-start.1 = (bf16[24,128]{1,0:T(8,128)(2,1)S(1)}, bf16[24,128]{1,0:T(8,128)(2,1)S(1)}, u32[]{:S(2)}, u32[]{:S(2)}) collective-permute-start(bf16[24,128]{1,0:T(8,128)(2,1)S(1)} %get-tuple-element.105), channel_id=1, source_target_pairs={{48,0},{96,48},{144,96},{192,144},{240,192},{288,240},{336,288},{3... | collective-permute-start | bytes 18440 | tf_op jit(solution)/shard_map/ppermute | solution.py:145
  19.1 26.7 %collective-permute-start.3 = (bf16[24,128]{1,0:T(8,128)(2,1)S(1)}, bf16[24,128]{1,0:T(8,128)(2,1)S(1)}, u32[]{:S(2)}, u32[]{:S(2)}) collective-permute-start(bf16[24,128]{1,0:T(8,128)(2,1)S(1)} %bitcast.104), channel_id=1, source_target_pairs={{1,0},{2,1},{3,2},{4,3},{5,4},{6,5},{7,6},{8,7},{9,8},{10,9},{11,1... | collective-permute-start | bytes 18440 | tf_op jit(solution)/shard_map/ppermute | solution.py:145
  20.4 25.4 %collective-permute-start.2 = (bf16[24,128]{1,0:T(8,128)(2,1)S(1)}, bf16[24,128]{1,0:T(8,128)(2,1)S(1)}, u32[]{:S(2)}, u32[]{:S(2)}) collective-permute-start(bf16[24,128]{1,0:T(8,128)(2,1)S(1)} %bitcast.106), channel_id=1, source_target_pairs={{0,1},{1,2},{2,3},{3,4},{4,5},{5,6},{6,7},{7,8},{8,9},{9,10},{10,1... | collective-permute-start | bytes 18440 | tf_op jit(solution)/shard_map/ppermute | solution.py:145
  29.2 16.6 %copy-start.3 = (bf16[24,24,128]{2,1,0:T(8,128)(2,1)S(1)}, bf16[24,24,128]{2,1,0:T(8,128)(2,1)}, u32[]{:S(2)}) copy-start(bf16[24,24,128]{2,1,0:T(8,128)(2,1)} %param.20) | copy-start | bytes 442372
  29.2 25.0 %all-to-all-start = ((bf16[16,57,128]{2,1,0:T(8,128)(2,1)}), bf16[16,57,128]{2,1,0:T(8,128)(2,1)S(1)}, u32[]{:S(2)}, u32[]{:S(2)}) async-start(bf16[16,57,128]{2,1,0:T(8,128)(2,1)} %broadcast_in_dim.23), calls=%async_computation | async-start | bytes 524288 | tf_op jit(solution)/shard_map/all_to_all | solution.py:83
  46.0 8.5 %copy-start = (bf16[24,24,128]{2,1,0:T(8,128)(2,1)S(1)}, bf16[24,24,128]{2,1,0:T(8,128)(2,1)}, u32[]{:S(2)}) copy-start(bf16[24,24,128]{2,1,0:T(8,128)(2,1)} %param.30) | copy-start | bytes 442372
  47.7 7.7 %copy-start.7 = (bf16[1024,128]{0,1:T(8,128)(2,1)}, bf16[1024,128]{0,1:T(8,128)(2,1)S(1)}, u32[]{:S(2)}) copy-start(bf16[1024,128]{0,1:T(8,128)(2,1)S(1)} %convolution_convert_fusion.1) | copy-start | bytes 786436
  54.9 0.8 copy-start.6
  60.4 2.1 %copy-start.1 = (f32[576,256]{1,0:T(8,128)}, f32[576,256]{1,0:T(8,128)S(1)}, u32[]{:S(2)}) copy-start(f32[576,256]{1,0:T(8,128)S(1)} %fusion.63) | copy-start | bytes 1769476
  62.3 1.0 copy-start.8
  69.9 36.2 %all-to-all-start.1 = ((f32[16,57,128]{2,1,0:T(8,128)}), f32[16,57,128]{2,1,0:T(8,128)S(1)}, u32[]{:S(2)}, u32[]{:S(2)}) async-start(f32[16,57,128]{2,1,0:T(8,128)} %dynamic-update-slice.16), calls=%async_computation.1 | async-start | bytes 1048576 | tf_op jit(solution)/shard_map/all_to_all | solution.py:87
  86.5 2.4 %copy-start.2 = (f32[576,256]{1,0:T(8,128)S(1)}, f32[576,256]{1,0:T(8,128)}, u32[]{:S(2)}) copy-start(f32[576,256]{1,0:T(8,128)} %copy-done.1) | copy-start | bytes 1769476
  86.8 19.3 %collective-permute-start.4 = (bf16[24,128]{1,0:T(8,128)(2,1)S(1)}, bf16[24,128]{1,0:T(8,128)(2,1)S(1)}, u32[]{:S(2)}, u32[]{:S(2)}) collective-permute-start(bf16[24,128]{1,0:T(8,128)(2,1)S(1)} %bitcast.109), channel_id=1, source_target_pairs={{0,48},{48,96},{96,144},{144,192},{192,240},{240,288},{288,336},{3... | collective-permute-start | bytes 18440 | tf_op jit(solution)/shard_map/ppermute | solution.py:145
  90.0 46.4 %collective-permute-start.7 = (bf16[24,128]{1,0:T(8,128)(2,1)S(1)}, bf16[24,128]{1,0:T(8,128)(2,1)S(1)}, u32[]{:S(2)}, u32[]{:S(2)}) collective-permute-start(bf16[24,128]{1,0:T(8,128)(2,1)S(1)} %get-tuple-element.98), channel_id=1, source_target_pairs={{1,0},{2,1},{3,2},{4,3},{5,4},{6,5},{7,6},{8,7},{9,8},{10,9},{11,1... | collective-permute-start | bytes 18440 | tf_op jit(solution)/shard_map/ppermute | solution.py:145
  91.3 45.0 %collective-permute-start.6 = (bf16[24,128]{1,0:T(8,128)(2,1)S(1)}, bf16[24,128]{1,0:T(8,128)(2,1)S(1)}, u32[]{:S(2)}, u32[]{:S(2)}) collective-permute-start(bf16[24,128]{1,0:T(8,128)(2,1)S(1)} %get-tuple-element.99), channel_id=1, source_target_pairs={{0,1},{1,2},{2,3},{3,4},{4,5},{5,6},{6,7},{7,8},{8,9},{9,10},{10,1... | collective-permute-start | bytes 18440 | tf_op jit(solution)/shard_map/ppermute | solution.py:145
  95.9 18.2 %collective-permute-start.5 = (bf16[24,128]{1,0:T(8,128)(2,1)S(1)}, bf16[24,128]{1,0:T(8,128)(2,1)S(1)}, u32[]{:S(2)}, u32[]{:S(2)}) collective-permute-start(bf16[24,128]{1,0:T(8,128)(2,1)S(1)} %bitcast.108), channel_id=1, source_target_pairs={{48,0},{96,48},{144,96},{192,144},{240,192},{288,240},{336,288},{3... | collective-permute-start | bytes 18440 | tf_op jit(solution)/shard_map/ppermute | solution.py:145
  106.8 17.6 %all-to-all-start.2 = ((f32[8,57,128]{2,1,0:T(8,128)}), f32[8,57,128]{2,1,0:T(8,128)S(1)}, u32[]{:S(2)}, u32[]{:S(2)}) async-start(f32[8,57,128]{2,1,0:T(8,128)} %broadcast_in_dim.24), calls=%async_computation.2 | async-start | bytes 524288 | tf_op jit(solution)/shard_map/all_to_all | solution.py:95
  125.2 21.7 %all-to-all-start.3 = ((f32[6,57,128]{2,1,0:T(8,128)}), f32[6,57,128]{2,1,0:T(8,128)S(1)}, u32[]{:S(2)}, u32[]{:S(2)}) async-start(f32[6,57,128]{2,1,0:T(8,128)} %broadcast_in_dim.25), calls=%async_computation.3 | async-start | bytes 393216 | tf_op jit(solution)/shard_map/all_to_all | solution.py:95

commit v10 on v9

--- a/solution.py
+++ b/solution.py
@@ -84,15 +84,17 @@
 
 
 def reduce_scatter_dom(packed):
-    return jnp.sum(lax.all_to_all(packed, "dom", 0, 0, tiled=True), axis=0)
+    pieces = lax.all_to_all(packed.astype(jnp.bfloat16), "dom", 0, 0, tiled=True)
+    return jnp.sum(pieces.astype(jnp.float32), axis=0)
 
 
 def sum_sub(value):
     total = value
     for axis in reversed(SUB):
         count = lax.axis_size(axis)
-        spread = jnp.broadcast_to(total[None], (count,) + total.shape)
-        total = jnp.sum(lax.all_to_all(spread, axis, 0, 0, tiled=True), axis=0)
+        spread = jnp.broadcast_to(total.astype(jnp.bfloat16)[None], (count,) + total.shape)
+        gathered = lax.all_to_all(spread, axis, 0, 0, tiled=True)
+        total = jnp.sum(gathered.astype(jnp.float32), axis=0)
     return total
 
 

time: 150 us -> 152 us (1.013)
  the two profiles are of different devices: /device:TPU:6 before, /device:TPU:1 now
where the time goes in v10:
time: 152 us; the launch traced here: 151 us
  starting transfers between devices  77.6 us (51%)
  waiting for transfers between devices  31.8 us (21%)
  local copies, waits for them, and re-layouts  17.3 us (11%)
  matrix products  16.5 us (11%)
  other arithmetic  5.32 us (4%)
  between operations  2 us (1%)
    ppermute x8, starting transfers between devices, shift_in(): lax.ppermute(value.astype(jnp.bfloat16), axis, pairs).astype(value.dtype)  40.5 us
    all_to_all x2, starting transfers between devices, sum_sub(): gathered = lax.all_to_all(spread, axis, 0, 0, tiled=True)  17.1 us
    all_to_all x2, waiting for transfers between devices, sum_sub(): gathered = lax.all_to_all(spread, axis, 0, 0, tiled=True)  14.8 us
    all_to_all x1, starting transfers between devices, gather_dom(): return lax.all_to_all(spread, 'dom', 0, 0, tiled=True)  12.9 us
    ppermute x8, waiting for transfers between devices, shift_in(): lax.ppermute(value.astype(jnp.bfloat16), axis, pairs).astype(value.dtype)  9.21 us
    dot_general x2, matrix products, sum_rows(): lax.dot_general(pick.astype(jnp.float32), values, (((0,), (0,)), ((), ())...  8.2 us
    all_to_all x1, waiting for transfers between devices, gather_dom(): return lax.all_to_all(spread, 'dom', 0, 0, tiled=True)  7.8 us
    all_to_all x1, starting transfers between devices, reduce_scatter_dom(): lax.all_to_all(packed.astype(jnp.bfloat16), 'dom', 0, 0, tiled=True)  7.13 us
  transfers between devices with their start and end apart: 12, of which 4 were waited for; matrix products, arithmetic and copies ran while one was open for 14% of the time, Pallas kernels for 0%

profile of v10, /device:TPU:1, one launch (start us, length us, event | category | flops | bytes accessed | tf_op | source)
XLA Modules:
  0.0 150.6 jit_solution(15637306487074015385)
XLA Ops:
  0.7 0.8 slice_bitcast_fusion.9
  1.4 16.2 %collective-permute-start = (bf16[24,128]{1,0:T(8,128)(2,1)S(1)}, bf16[24,128]{1,0:T(8,128)(2,1)S(1)}, u32[]{:S(2)}, u32[]{:S(2)}) collective-permute-start(bf16[24,128]{1,0:T(8,128)(2,1)S(1)} %get-tuple-element.104), channel_id=1, source_target_pairs={{0,48},{48,96},{96,144},{144,192},{192,240},{240,288},{288,336},{3... | collective-permute-start | bytes 18440 | tf_op jit(solution)/shard_map/ppermute | solution.py:147
  17.7 1.9 %collective-permute-start.1 = (bf16[24,128]{1,0:T(8,128)(2,1)S(1)}, bf16[24,128]{1,0:T(8,128)(2,1)S(1)}, u32[]{:S(2)}, u32[]{:S(2)}) collective-permute-start(bf16[24,128]{1,0:T(8,128)(2,1)S(1)} %get-tuple-element.105), channel_id=1, source_target_pairs={{48,0},{96,48},{144,96},{192,144},{240,192},{288,240},{336,288},{3... | collective-permute-start | bytes 18440 | tf_op jit(solution)/shard_map/ppermute | solution.py:147
  19.6 0.8 fusion.58
  20.5 1.3 collective-permute-start.3
  21.8 4.0 %collective-permute-start.2 = (bf16[24,128]{1,0:T(8,128)(2,1)S(1)}, bf16[24,128]{1,0:T(8,128)(2,1)S(1)}, u32[]{:S(2)}, u32[]{:S(2)}) collective-permute-start(bf16[24,128]{1,0:T(8,128)(2,1)S(1)} %bitcast.106), channel_id=1, source_target_pairs={{0,1},{1,2},{2,3},{3,4},{4,5},{5,6},{6,7},{7,8},{8,9},{9,10},{10,1... | collective-permute-start | bytes 18440 | tf_op jit(solution)/shard_map/ppermute | solution.py:147
  25.8 0.7 reshape.283
  26.5 0.7 constant_dynamic-update-slice_fusion.4
  27.2 0.7 constant_dynamic-update-slice_fusion.3
  27.9 0.7 constant_dynamic-update-slice_fusion.2
  28.6 0.7 constant_dynamic-update-slice_fusion.1
  29.3 0.8 broadcast_in_dim.23
  30.0 12.9 %all-to-all-start = ((bf16[16,57,128]{2,1,0:T(8,128)(2,1)}), bf16[16,57,128]{2,1,0:T(8,128)(2,1)S(1)}, u32[]{:S(2)}, u32[]{:S(2)}) async-start(bf16[16,57,128]{2,1,0:T(8,128)(2,1)} %broadcast_in_dim.23), calls=%async_computation | async-start | bytes 524288 | tf_op jit(solution)/shard_map/all_to_all | solution.py:83
  43.6 0.7 select_add_fusion
  44.3 2.1 %iota_compare_fusion = (pred[1024,676]{1,0:T(32,128)(4,1)}, pred[1024,676]{1,0:T(32,128)(4,1)}) fusion(s32[1024]{0:T(1024)S(1)} %get-tuple-element.113, s32[1024]{0:T(1024)S(1)} %get-tuple-element.112), kind=kLoop, calls=%fused_computation.4 | loop fusion | flops 1384448 | bytes 1392640 | tf_op jit(solution)/shard_map/eq | solution.py:151
  47.0 0.8 convolution_convert_fusion
  47.9 0.8 convolution_convert_fusion.1
  48.7 7.8 %all-to-all-done = bf16[16,57,128]{2,1,0:T(8,128)(2,1)S(1)} async-done(((bf16[16,57,128]{2,1,0:T(8,128)(2,1)}), bf16[16,57,128]{2,1,0:T(8,128)(2,1)S(1)}, u32[]{:S(2)}, u32[]{:S(2)}) %all-to-all-start) | async-done | bytes 233504 | tf_op jit(solution)/shard_map/all_to_all | solution.py:83
  57.3 0.4 fusion.27
  57.7 0.3 fusion.61
  58.1 1.7 %fusion.14 = bf16[576,128]{1,0:T(8,128)(2,1)S(1)} fusion(s32[1024]{0:T(1024)S(1)} %copy-done.7, f32[1024,128]{0,1:T(8,128)S(1)} %get-tuple-element.115, f32[1024]{0:T(1024)S(1)} %fusion.45, f32[128]{0:T(128)S(1)} %reshape.300, f32[1024]{0:T(1024)S(1)} %add_rsqrt_fusion.1, f32[1024]{0:T(1024)S(1)} %broadcast_multiply_fusion.6), kind=kOutput, calls=%fused_computation.20 | convolution fusion | flops 907747328 | bytes 688640 | tf_op jit(solution)/shard_map/dot_general | solution.py:163
  59.8 0.2 fusion.35
  60.1 0.3 fusion.62
  60.4 0.3 multiply_reduce_fusion.5
  60.7 0.4 fusion.30
  61.1 0.4 multiply_convert_fusion.1
  61.4 0.2 fusion.13
  61.6 0.3 convolution_convert_fusion.3
  61.9 0.2 fusion.63
  62.2 1.9 %multiply_reduce_fusion = (bf16[128]{0:T(256)(128)(2,1)S(1)}, f32[1024]{0:T(1024)S(1)}, f32[1024]{0:T(1024)S(1)}, f32[1024,128]{0,1:T(8,128)S(1)}) fusion(f32[1024,128]{0,1:T(8,128)S(1)} %get-tuple-element.115, f32[1024]{0:T(1024)S(1)} %add_rsqrt_fusion.1, f32[1024]{0:T(1024)S(1)} %broadcast_multiply_fusion.6, f32[128]{0:T(128)S(1)} %reshape.300, ...), kind=kOutput, calls=%fused_computation.35 | convolution fusion | flops 907999104 | bytes 1630976 | tf_op jit(solution)/shard_map/dot_general | solution.py:157
  64.1 0.2 multiply_convert_fusion
  64.3 0.3 fusion.12
  64.6 0.5 copy-done.6
  65.2 0.4 convolution_convert_fusion.2
  65.6 0.4 fusion.64
  66.3 0.7 constant_dynamic-update-slice_fusion.7
  67.0 0.9 fusion.20
  67.9 0.7 constant_dynamic-update-slice_fusion.6
  68.6 0.9 fusion.18
  69.4 0.6 constant_dynamic-update-slice_fusion.5
  70.0 7.1 %all-to-all-start.1 = ((bf16[16,57,128]{2,1,0:T(8,128)(2,1)}), bf16[16,57,128]{2,1,0:T(8,128)(2,1)S(1)}, u32[]{:S(2)}, u32[]{:S(2)}) async-start(bf16[16,57,128]{2,1,0:T(8,128)(2,1)} %constant_dynamic-update-slice_fusion.5), calls=%async_computation.1 | async-start | bytes 524288 | tf_op jit(solution)/shard_map/all_to_all | solution.py:87
  77.2 1.1 fusion.56
  78.2 0.2 copy.117
  78.5 0.9 copy-done.1
  79.4 6.5 %fusion = f32[676,128]{1,0:T(8,128)S(1)} fusion(pred[1024,676]{1,0:T(32,128)(4,1)S(1)} %copy-done.1, pred[1024,676]{1,0:T(32,128)(4,1)} %get-tuple-element.120, f32[1024,128]{1,0:T(8,128)} %get-tuple-element.96, f32[1024,128]{1,0:T(8,128)} %get-tuple-element.97), kind=kOutput, calls=%fused_computation | convolution fusion | flops 2128158720 | bytes 2779136 | tf_op jit(solution)/shard_map/dot_general | solution.py:163
  85.9 0.2 copy.124
  86.2 9.9 %collective-permute-start.4 = (bf16[24,128]{1,0:T(8,128)(2,1)S(1)}, bf16[24,128]{1,0:T(8,128)(2,1)S(1)}, u32[]{:S(2)}, u32[]{:S(2)}) collective-permute-start(bf16[24,128]{1,0:T(8,128)(2,1)S(1)} %bitcast.108), channel_id=1, source_target_pairs={{0,48},{48,96},{96,144},{144,192},{192,240},{240,288},{288,336},{3... | collective-permute-start | bytes 18440 | tf_op jit(solution)/shard_map/ppermute | solution.py:147
  96.0 0.2 copy.100
  96.3 0.8 copy.111
  97.1 1.3 collective-permute-start.7
  98.4 4.0 %collective-permute-start.6 = (bf16[24,128]{1,0:T(8,128)(2,1)S(1)}, bf16[24,128]{1,0:T(8,128)(2,1)S(1)}, u32[]{:S(2)}, u32[]{:S(2)}) collective-permute-start(bf16[24,128]{1,0:T(8,128)(2,1)S(1)} %get-tuple-element.99), channel_id=1, source_target_pairs={{0,1},{1,2},{2,3},{3,4},{4,5},{5,6},{6,7},{7,8},{8,9},{9,10},{10,1... | collective-permute-start | bytes 18440 | tf_op jit(solution)/shard_map/ppermute | solution.py:147
  102.4 1.9 %collective-permute-start.5 = (bf16[24,128]{1,0:T(8,128)(2,1)S(1)}, bf16[24,128]{1,0:T(8,128)(2,1)S(1)}, u32[]{:S(2)}, u32[]{:S(2)}) collective-permute-start(bf16[24,128]{1,0:T(8,128)(2,1)S(1)} %bitcast.109), channel_id=1, source_target_pairs={{48,0},{96,48},{144,96},{192,144},{240,192},{288,240},{336,288},{3... | collective-permute-start | bytes 18440 | tf_op jit(solution)/shard_map/ppermute | solution.py:147
  104.5 9.2 %collective-permute-done.5 = bf16[24,128]{1,0:T(8,128)(2,1)S(1)} collective-permute-done((bf16[24,128]{1,0:T(8,128)(2,1)S(1)}, bf16[24,128]{1,0:T(8,128)(2,1)S(1)}, u32[]{:S(2)}, u32[]{:S(2)}) %collective-permute-start.5) | collective-permute-done | bytes 6176 | tf_op jit(solution)/shard_map/ppermute | solution.py:147
  113.9 0.7 broadcast_in_dim.24
  114.5 6.1 %all-to-all-start.2 = ((bf16[8,57,128]{2,1,0:T(8,128)(2,1)}), bf16[8,57,128]{2,1,0:T(8,128)(2,1)S(1)}, u32[]{:S(2)}, u32[]{:S(2)}) async-start(bf16[8,57,128]{2,1,0:T(8,128)(2,1)} %broadcast_in_dim.24), calls=%async_computation.2 | async-start | bytes 262144 | tf_op jit(solution)/shard_map/all_to_all | solution.py:96
  120.9 7.7 %all-to-all-done.2 = bf16[8,57,128]{2,1,0:T(8,128)(2,1)S(1)} async-done(((bf16[8,57,128]{2,1,0:T(8,128)(2,1)}), bf16[8,57,128]{2,1,0:T(8,128)(2,1)S(1)}, u32[]{:S(2)}, u32[]{:S(2)}) %all-to-all-start.2) | async-done | bytes 116768 | tf_op jit(solution)/shard_map/all_to_all | solution.py:96
  128.6 0.6 broadcast_in_dim.25
  129.3 11.0 %all-to-all-start.3 = ((bf16[6,57,128]{2,1,0:T(8,128)(2,1)}), bf16[6,57,128]{2,1,0:T(8,128)(2,1)S(1)}, u32[]{:S(2)}, u32[]{:S(2)}) async-start(bf16[6,57,128]{2,1,0:T(8,128)(2,1)} %broadcast_in_dim.25), calls=%async_computation.3 | async-start | bytes 196608 | tf_op jit(solution)/shard_map/all_to_all | solution.py:96
  140.3 0.7 add_convert_fusion
  141.0 7.1 %all-to-all-done.3 = bf16[6,57,128]{2,1,0:T(8,128)(2,1)S(1)} async-done(((bf16[6,57,128]{2,1,0:T(8,128)(2,1)}), bf16[6,57,128]{2,1,0:T(8,128)(2,1)S(1)}, u32[]{:S(2)}, u32[]{:S(2)}) %all-to-all-start.3) | async-done | bytes 87584 | tf_op jit(solution)/shard_map/all_to_all | solution.py:96
  148.1 0.6 slice.236
  148.7 0.6 fusion.59
  149.3 0.6 slice.234
  149.9 0.6 reshape_squeeze.7
  (92 shorter events, 2.6 us)
Async XLA Ops:
  0.6 45.7 %copy-start.3 = (bf16[1024,128]{1,0:T(8,128)(2,1)S(1)}, bf16[1024,128]{1,0:T(8,128)(2,1)}, u32[]{:S(2)}) copy-start(bf16[1024,128]{1,0:T(8,128)(2,1)} %param.21) | copy-start | bytes 786436
  0.6 45.9 %copy-start.4 = (bf16[1024,128]{1,0:T(8,128)(2,1)S(1)}, bf16[1024,128]{1,0:T(8,128)(2,1)}, u32[]{:S(2)}) copy-start(bf16[1024,128]{1,0:T(8,128)(2,1)} %param.31) | copy-start | bytes 786436
  1.4 45.3 %collective-permute-start = (bf16[24,128]{1,0:T(8,128)(2,1)S(1)}, bf16[24,128]{1,0:T(8,128)(2,1)S(1)}, u32[]{:S(2)}, u32[]{:S(2)}) collective-permute-start(bf16[24,128]{1,0:T(8,128)(2,1)S(1)} %get-tuple-element.104), channel_id=1, source_target_pairs={{0,48},{48,96},{96,144},{144,192},{192,240},{240,288},{288,336},{3... | collective-permute-start | bytes 18440 | tf_op jit(solution)/shard_map/ppermute | solution.py:147
  17.7 29.1 %collective-permute-start.1 = (bf16[24,128]{1,0:T(8,128)(2,1)S(1)}, bf16[24,128]{1,0:T(8,128)(2,1)S(1)}, u32[]{:S(2)}, u32[]{:S(2)}) collective-permute-start(bf16[24,128]{1,0:T(8,128)(2,1)S(1)} %get-tuple-element.105), channel_id=1, source_target_pairs={{48,0},{96,48},{144,96},{192,144},{240,192},{288,240},{336,288},{3... | collective-permute-start | bytes 18440 | tf_op jit(solution)/shard_map/ppermute | solution.py:147
  20.5 26.3 %collective-permute-start.3 = (bf16[24,128]{1,0:T(8,128)(2,1)S(1)}, bf16[24,128]{1,0:T(8,128)(2,1)S(1)}, u32[]{:S(2)}, u32[]{:S(2)}) collective-permute-start(bf16[24,128]{1,0:T(8,128)(2,1)S(1)} %bitcast.104), channel_id=1, source_target_pairs={{1,0},{2,1},{3,2},{4,3},{5,4},{6,5},{7,6},{8,7},{9,8},{10,9},{11,1... | collective-permute-start | bytes 18440 | tf_op jit(solution)/shard_map/ppermute | solution.py:147
  21.8 25.0 %collective-permute-start.2 = (bf16[24,128]{1,0:T(8,128)(2,1)S(1)}, bf16[24,128]{1,0:T(8,128)(2,1)S(1)}, u32[]{:S(2)}, u32[]{:S(2)}) collective-permute-start(bf16[24,128]{1,0:T(8,128)(2,1)S(1)} %bitcast.106), channel_id=1, source_target_pairs={{0,1},{1,2},{2,3},{3,4},{4,5},{5,6},{6,7},{7,8},{8,9},{9,10},{10,1... | collective-permute-start | bytes 18440 | tf_op jit(solution)/shard_map/ppermute | solution.py:147
  30.0 16.8 %copy-start.2 = (bf16[24,24,128]{2,1,0:T(8,128)(2,1)S(1)}, bf16[24,24,128]{2,1,0:T(8,128)(2,1)}, u32[]{:S(2)}) copy-start(bf16[24,24,128]{2,1,0:T(8,128)(2,1)} %param.20) | copy-start | bytes 442372
  30.0 26.5 %all-to-all-start = ((bf16[16,57,128]{2,1,0:T(8,128)(2,1)}), bf16[16,57,128]{2,1,0:T(8,128)(2,1)S(1)}, u32[]{:S(2)}, u32[]{:S(2)}) async-start(bf16[16,57,128]{2,1,0:T(8,128)(2,1)} %broadcast_in_dim.23), calls=%async_computation | async-start | bytes 524288 | tf_op jit(solution)/shard_map/all_to_all | solution.py:83
  46.5 10.7 %copy-start.5 = (bf16[1024,128]{0,1:T(8,128)(2,1)}, bf16[1024,128]{0,1:T(8,128)(2,1)S(1)}, u32[]{:S(2)}) copy-start(bf16[1024,128]{0,1:T(8,128)(2,1)S(1)} %copy.95) | copy-start | bytes 786436
  47.0 9.8 %copy-start = (bf16[24,24,128]{2,1,0:T(8,128)(2,1)S(1)}, bf16[24,24,128]{2,1,0:T(8,128)(2,1)}, u32[]{:S(2)}) copy-start(bf16[24,24,128]{2,1,0:T(8,128)(2,1)} %param.30) | copy-start | bytes 442372
  47.8 9.9 %copy-start.8 = (bf16[1024,128]{0,1:T(8,128)(2,1)}, bf16[1024,128]{0,1:T(8,128)(2,1)S(1)}, u32[]{:S(2)}) copy-start(bf16[1024,128]{0,1:T(8,128)(2,1)S(1)} %convolution_convert_fusion) | copy-start | bytes 786436
  48.7 9.0 %copy-start.10 = (bf16[1024,128]{0,1:T(8,128)(2,1)}, bf16[1024,128]{0,1:T(8,128)(2,1)S(1)}, u32[]{:S(2)}) copy-start(bf16[1024,128]{0,1:T(8,128)(2,1)S(1)} %convolution_convert_fusion.1) | copy-start | bytes 786436
  57.3 0.8 copy-start.7
  64.1 1.0 copy-start.6
  64.1 1.0 copy-start.9
  64.1 1.1 copy-start.11
  70.0 43.8 %all-to-all-start.1 = ((bf16[16,57,128]{2,1,0:T(8,128)(2,1)}), bf16[16,57,128]{2,1,0:T(8,128)(2,1)S(1)}, u32[]{:S(2)}, u32[]{:S(2)}) async-start(bf16[16,57,128]{2,1,0:T(8,128)(2,1)} %constant_dynamic-update-slice_fusion.5), calls=%async_computation.1 | async-start | bytes 524288 | tf_op jit(solution)/shard_map/all_to_all | solution.py:87
  78.2 1.1 copy-start.1
  86.2 18.2 %collective-permute-start.4 = (bf16[24,128]{1,0:T(8,128)(2,1)S(1)}, bf16[24,128]{1,0:T(8,128)(2,1)S(1)}, u32[]{:S(2)}, u32[]{:S(2)}) collective-permute-start(bf16[24,128]{1,0:T(8,128)(2,1)S(1)} %bitcast.108), channel_id=1, source_target_pairs={{0,48},{48,96},{96,144},{144,192},{192,240},{240,288},{288,336},{3... | collective-permute-start | bytes 18440 | tf_op jit(solution)/shard_map/ppermute | solution.py:147
  97.1 23.6 %collective-permute-start.7 = (bf16[24,128]{1,0:T(8,128)(2,1)S(1)}, bf16[24,128]{1,0:T(8,128)(2,1)S(1)}, u32[]{:S(2)}, u32[]{:S(2)}) collective-permute-start(bf16[24,128]{1,0:T(8,128)(2,1)S(1)} %get-tuple-element.98), channel_id=1, source_target_pairs={{1,0},{2,1},{3,2},{4,3},{5,4},{6,5},{7,6},{8,7},{9,8},{10,9},{11,1... | collective-permute-start | bytes 18440 | tf_op jit(solution)/shard_map/ppermute | solution.py:147
  98.4 22.2 %collective-permute-start.6 = (bf16[24,128]{1,0:T(8,128)(2,1)S(1)}, bf16[24,128]{1,0:T(8,128)(2,1)S(1)}, u32[]{:S(2)}, u32[]{:S(2)}) collective-permute-start(bf16[24,128]{1,0:T(8,128)(2,1)S(1)} %get-tuple-element.99), channel_id=1, source_target_pairs={{0,1},{1,2},{2,3},{3,4},{4,5},{5,6},{6,7},{7,8},{8,9},{9,10},{10,1... | collective-permute-start | bytes 18440 | tf_op jit(solution)/shard_map/ppermute | solution.py:147
  102.4 11.3 %collective-permute-start.5 = (bf16[24,128]{1,0:T(8,128)(2,1)S(1)}, bf16[24,128]{1,0:T(8,128)(2,1)S(1)}, u32[]{:S(2)}, u32[]{:S(2)}) collective-permute-start(bf16[24,128]{1,0:T(8,128)(2,1)S(1)} %bitcast.109), channel_id=1, source_target_pairs={{48,0},{96,48},{144,96},{192,144},{240,192},{288,240},{336,288},{3... | collective-permute-start | bytes 18440 | tf_op jit(solution)/shard_map/ppermute | solution.py:147
  114.5 14.1 %all-to-all-start.2 = ((bf16[8,57,128]{2,1,0:T(8,128)(2,1)}), bf16[8,57,128]{2,1,0:T(8,128)(2,1)S(1)}, u32[]{:S(2)}, u32[]{:S(2)}) async-start(bf16[8,57,128]{2,1,0:T(8,128)(2,1)} %broadcast_in_dim.24), calls=%async_computation.2 | async-start | bytes 262144 | tf_op jit(solution)/shard_map/all_to_all | solution.py:96
  129.3 18.8 %all-to-all-start.3 = ((bf16[6,57,128]{2,1,0:T(8,128)(2,1)}), bf16[6,57,128]{2,1,0:T(8,128)(2,1)S(1)}, u32[]{:S(2)}, u32[]{:S(2)}) async-start(bf16[6,57,128]{2,1,0:T(8,128)(2,1)} %broadcast_in_dim.25), calls=%async_computation.3 | async-start | bytes 196608 | tf_op jit(solution)/shard_map/all_to_all | solution.py:96

commit v11 on v9

--- a/solution.py
+++ b/solution.py
@@ -96,24 +96,34 @@
     return total
 
 
-def gather_params(weights, gains):
+def gather_params(weights, gains, first_row, last_row):
     latent = weights[0].shape[1]
+    count = lax.axis_size("dom")
+    index = lax.axis_index("dom")
     gain_row = gains.reshape(1, -1)
     gain_row = jnp.pad(gain_row, ((0, 0), (0, latent - gain_row.shape[1])))
     packed = jnp.concatenate(list(weights) + [gain_row], axis=0)
-    full = gather_dom(packed)
-    count = full.shape[0]
+    target = jnp.arange(count)[:, None, None]
+    edge_rows = jnp.where(target == index + 1, last_row[None], jnp.where(target == index - 1, first_row[None], 0))
+    spread = jnp.concatenate(
+        [jnp.broadcast_to(packed[None], (count,) + packed.shape), edge_rows.astype(packed.dtype)], axis=1
+    )
+    received = lax.all_to_all(spread, "dom", 0, 0, tiled=True)
+    rows = packed.shape[0]
+    top = lax.dynamic_index_in_dim(received, (index + count - 1) % count, keepdims=False)[rows:]
+    bottom = lax.dynamic_index_in_dim(received, (index + 1) % count, keepdims=False)[rows:]
+    full = received[:, :rows]
     outs = []
     start = 0
     for w in weights:
-        rows = w.shape[0]
-        outs.append(full[:, start : start + rows].reshape(count * rows, latent))
-        start += rows
+        part = w.shape[0]
+        outs.append(full[:, start : start + part].reshape(count * part, latent))
+        start += part
     width = gains.shape[1]
     gain_full = full[:, start, : 2 * width].reshape(count, 2, width)
     gain_full = jnp.transpose(gain_full, (1, 0, 2)).reshape(2, count * width)
     outs.append(gain_full)
-    return tuple(outs)
+    return tuple(outs), top, bottom
 
 
 def reduce_params(parts, gain_terms, scale):
@@ -181,16 +191,14 @@
     node_cot,
     edge_cot,
 ):
-    full_edge_in, full_edge_out, full_node_in, full_node_out, full_gains = gather_params(
-        (w_edge_in, w_edge_out, w_node_in, w_node_out), gains
+    (full_edge_in, full_edge_out, full_node_in, full_node_out, full_gains), top, bottom = gather_params(
+        (w_edge_in, w_edge_out, w_node_in, w_node_out), gains, node_feat[0], node_feat[-1]
     )
     gain_edge = full_gains[0].astype(jnp.float32)
     gain_node = full_gains[1].astype(jnp.float32)
     block_side = node_feat.shape[0]
     latent = node_feat.shape[2]
     padded_side = block_side + 2
-    top = shift_in(node_feat[-1], "dom", 1)
-    bottom = shift_in(node_feat[0], "dom", -1)
     left = shift_in(node_feat[:, -1], SUB, 1)
     right = shift_in(node_feat[:, 0], SUB, -1)
     middle = jnp.concatenate([left[:, None], node_feat, right[:, None]], axis=1)

time: 150 us -> 135 us (0.900)
  starting transfers between devices: 80.2 us -> 68.2 us
  waiting for transfers between devices: 26.3 us -> 24.4 us
  local copies, waits for them, and re-layouts: 18.2 us -> 16.7 us
    ppermute x8 -> x6, starting transfers between devices: 40.6 us -> 23.9 us  [shift_in(): lax.ppermute(value.astype(jnp.bfloat16), axis, pairs).astype(value.dtype)]
    all_to_all x1, starting transfers between devices: 12.7 us -> 17.6 us  [gather_params(): received = lax.all_to_all(spread, 'dom', 0, 0, tiled=True)]
    all_to_all x1, waiting for transfers between devices: 6.48 us -> 4.35 us  [gather_params(): received = lax.all_to_all(spread, 'dom', 0, 0, tiled=True)]
    unnamed x33 -> x35, local copies, waits for them, and re-layouts: 6.99 us -> 6.99 us
  transfers between devices with their start and end apart: 12 -> 10, of which waited for: 3 -> 3; matrix products, arithmetic and copies ran while one was open for 15% -> 11% of each run, Pallas kernels for 0% -> 0%
where the time goes in v11:
time: 135 us; the launch traced here: 134 us
  starting transfers between devices  68.2 us (51%)
  waiting for transfers between devices  24.4 us (18%)
  matrix products  17.4 us (13%)
  local copies, waits for them, and re-layouts  16.7 us (12%)
  other arithmetic  5.5 us (4%)
  between operations  2.02 us (1%)
    ppermute x6, starting transfers between devices, shift_in(): lax.ppermute(value.astype(jnp.bfloat16), axis, pairs).astype(value.dtype)  23.9 us
    all_to_all x2, waiting for transfers between devices, sum_sub(): total = jnp.sum(lax.all_to_all(spread, axis, 0, 0, tiled=True), axis=0)  20.1 us
    all_to_all x2, starting transfers between devices, sum_sub(): total = jnp.sum(lax.all_to_all(spread, axis, 0, 0, tiled=True), axis=0)  19 us
    all_to_all x1, starting transfers between devices, gather_params(): received = lax.all_to_all(spread, 'dom', 0, 0, tiled=True)  17.6 us
    dot_general x2, matrix products, sum_rows(): lax.dot_general(pick.astype(jnp.float32), values, (((0,), (0,)), ((), ())...  8.44 us
    all_to_all x1, starting transfers between devices, reduce_scatter_dom(): return jnp.sum(lax.all_to_all(packed, 'dom', 0, 0, tiled=True), axis=0)  7.72 us
    unnamed x35, local copies, waits for them, and re-layouts  6.99 us
    all_to_all x1, waiting for transfers between devices, gather_params(): received = lax.all_to_all(spread, 'dom', 0, 0, tiled=True)  4.35 us
  transfers between devices with their start and end apart: 10, of which 3 were waited for; matrix products, arithmetic and copies ran while one was open for 11% of the time, Pallas kernels for 0%

profile of v11, /device:TPU:6, one launch (start us, length us, event | category | flops | bytes accessed | tf_op | source)
XLA Modules:
  0.0 134.2 jit_solution(11362808671349938671)
XLA Ops:
  0.7 0.8 reshape.289
  1.5 0.7 slice_bitcast_fusion.9
  2.2 0.7 constant_dynamic-update-slice_fusion.4
  2.9 0.7 constant_dynamic-update-slice_fusion.3
  3.6 0.7 constant_dynamic-update-slice_fusion.2
  4.3 0.7 constant_dynamic-update-slice_fusion.1
  5.0 0.1 select_select_fusion
  5.1 0.8 pad_maximum_fusion.1
  5.9 17.6 %all-to-all-start = ((bf16[16,81,128]{2,1,0:T(8,128)(2,1)}), bf16[16,81,128]{2,1,0:T(8,128)(2,1)S(1)}, u32[]{:S(2)}, u32[]{:S(2)}) async-start(bf16[16,81,128]{2,1,0:T(8,128)(2,1)} %pad_maximum_fusion.1), calls=%async_computation | async-start | bytes 720896 | tf_op jit(solution)/shard_map/all_to_all | solution.py:111
  23.6 1.3 collective-permute-start.1
  24.9 4.5 %collective-permute-start = (bf16[24,128]{1,0:T(8,128)(2,1)S(1)}, bf16[24,128]{1,0:T(8,128)(2,1)S(1)}, u32[]{:S(2)}, u32[]{:S(2)}) collective-permute-start(bf16[24,128]{1,0:T(8,128)(2,1)S(1)} %bitcast.102), channel_id=1, source_target_pairs={{0,1},{1,2},{2,3},{3,4},{4,5},{5,6},{6,7},{7,8},{8,9},{9,10},{10,1... | collective-permute-start | bytes 18440 | tf_op jit(solution)/shard_map/ppermute | solution.py:155
  30.1 2.1 %iota_compare_fusion = (pred[1024,676]{1,0:T(32,128)(4,1)}, pred[1024,676]{1,0:T(32,128)(4,1)}) fusion(s32[1024]{0:T(1024)S(1)} %get-tuple-element.115, s32[1024]{0:T(1024)S(1)} %get-tuple-element.114), kind=kLoop, calls=%fused_computation.4 | loop fusion | flops 1384448 | bytes 1392640 | tf_op jit(solution)/shard_map/eq | solution.py:159
  32.2 0.1 copy.98
  32.4 0.1 copy.102
  32.6 4.3 %all-to-all-done = bf16[16,81,128]{2,1,0:T(8,128)(2,1)S(1)} async-done(((bf16[16,81,128]{2,1,0:T(8,128)(2,1)}), bf16[16,81,128]{2,1,0:T(8,128)(2,1)S(1)}, u32[]{:S(2)}, u32[]{:S(2)}) %all-to-all-start) | async-done | bytes 331808 | tf_op jit(solution)/shard_map/all_to_all | solution.py:111
  37.0 0.1 pad_maximum_fusion.5
  37.2 0.8 convolution_convert_fusion
  38.0 0.8 convolution_convert_fusion.1
  39.1 0.1 reshape.308
  39.2 0.2 fusion.28
  39.6 0.4 fusion.26
  40.1 0.3 fusion.61
  40.5 1.7 %fusion.14 = bf16[576,128]{1,0:T(8,128)(2,1)S(1)} fusion(s32[1024]{0:T(1024)S(1)} %copy-done.7, f32[1024,128]{0,1:T(8,128)S(1)} %get-tuple-element.117, f32[1024]{0:T(1024)S(1)} %fusion.45, f32[128]{0:T(128)S(1)} %reshape.307, f32[1024]{0:T(1024)S(1)} %add_rsqrt_fusion.1, f32[1024]{0:T(1024)S(1)} %broadcast_multiply_fusion.6), kind=kOutput, calls=%fused_computation.20 | convolution fusion | flops 907747328 | bytes 688640 | tf_op jit(solution)/shard_map/dot_general | solution.py:171
  42.2 0.2 fusion.35
  42.4 0.3 fusion.62
  42.7 0.3 multiply_reduce_fusion.5
  43.0 0.4 fusion.29
  43.4 0.4 multiply_convert_fusion.1
  43.8 0.2 fusion.13
  44.0 1.0 fusion.34
  44.9 0.2 fusion.63
  45.2 1.9 %multiply_reduce_fusion = (f32[128]{0:T(128)S(1)}, f32[1024]{0:T(1024)S(1)}, f32[1024]{0:T(1024)S(1)}, f32[1024,128]{0,1:T(8,128)S(1)}) fusion(f32[1024,128]{0,1:T(8,128)S(1)} %get-tuple-element.117, f32[1024]{0:T(1024)S(1)} %add_rsqrt_fusion.1, f32[1024]{0:T(1024)S(1)} %broadcast_multiply_fusion.6, f32[128]{0:T(128)S(1)} %reshape.307, ...), kind=kOutput, calls=%fused_computation.31 | convolution fusion | flops 907999104 | bytes 1631232 | tf_op jit(solution)/shard_map/dot_general | solution.py:165
  47.1 0.2 multiply_convert_fusion
  47.2 0.3 fusion.12
  47.5 0.5 copy-done.9
  48.0 0.4 fusion.25
  48.4 0.4 fusion.64
  49.1 0.7 constant_dynamic-update-slice_fusion.6
  49.8 0.9 fusion.18
  50.7 1.6 %constant_dynamic-update-slice_fusion.5 = f32[16,57,128]{2,1,0:T(8,128)} fusion(f32[16,57,128]{2,1,0:T(8,128)} %fusion.18, f32[16,16,128]{2,1,0:T(8,128)} %bitcast.93), kind=kLoop, calls=%fused_computation.79 | loop fusion | bytes 262144
  52.3 0.9 fusion.17
  53.1 1.5 %dynamic-update-slice.16 = f32[16,57,128]{2,1,0:T(8,128)} dynamic-update-slice(f32[16,57,128]{2,1,0:T(8,128)} %fusion.17, f32[16,1,128]{2,1,0:T(1,128)S(1)} %pad.22.clone, s32[]{} %constant.208, s32[]{} %constant.212, s32[]{} %constant.208) | dynamic-update-slice | bytes 16388 | tf_op jit(solution)/shard_map/concatenate | solution.py:136
  54.6 7.7 %all-to-all-start.1 = ((f32[16,57,128]{2,1,0:T(8,128)}), f32[16,57,128]{2,1,0:T(8,128)S(1)}, u32[]{:S(2)}, u32[]{:S(2)}) async-start(f32[16,57,128]{2,1,0:T(8,128)} %dynamic-update-slice.16), calls=%async_computation.1 | async-start | bytes 1048576 | tf_op jit(solution)/shard_map/all_to_all | solution.py:87
  62.4 1.1 fusion.56
  63.5 0.2 copy.120
  63.7 6.7 %fusion = f32[676,128]{1,0:T(8,128)S(1)} fusion(pred[1024,676]{1,0:T(32,128)(4,1)} %get-tuple-element.123, pred[1024,676]{1,0:T(32,128)(4,1)} %get-tuple-element.124, f32[1024,128]{1,0:T(8,128)} %get-tuple-element.96, f32[1024,128]{1,0:T(8,128)} %get-tuple-element.97), kind=kOutput, calls=%fused_computation | convolution fusion | flops 2128158720 | bytes 2779136 | tf_op jit(solution)/shard_map/dot_general | solution.py:171
  70.4 0.2 copy.127
  70.7 2.1 %collective-permute-start.2 = (bf16[24,128]{1,0:T(8,128)(2,1)S(1)}, bf16[24,128]{1,0:T(8,128)(2,1)S(1)}, u32[]{:S(2)}, u32[]{:S(2)}) collective-permute-start(bf16[24,128]{1,0:T(8,128)(2,1)S(1)} %bitcast.105), channel_id=1, source_target_pairs={{0,48},{48,96},{96,144},{144,192},{192,240},{240,288},{288,336},{3... | collective-permute-start | bytes 18440 | tf_op jit(solution)/shard_map/ppermute | solution.py:155
  72.9 0.2 copy.103
  73.1 0.8 copy.114
  74.0 1.3 collective-permute-start.5
  75.3 4.5 %collective-permute-start.4 = (bf16[24,128]{1,0:T(8,128)(2,1)S(1)}, bf16[24,128]{1,0:T(8,128)(2,1)S(1)}, u32[]{:S(2)}, u32[]{:S(2)}) collective-permute-start(bf16[24,128]{1,0:T(8,128)(2,1)S(1)} %get-tuple-element.101), channel_id=1, source_target_pairs={{0,1},{1,2},{2,3},{3,4},{4,5},{5,6},{6,7},{7,8},{8,9},{9,10},{10,1... | collective-permute-start | bytes 18440 | tf_op jit(solution)/shard_map/ppermute | solution.py:155
  79.8 10.2 %collective-permute-start.3 = (bf16[24,128]{1,0:T(8,128)(2,1)S(1)}, bf16[24,128]{1,0:T(8,128)(2,1)S(1)}, u32[]{:S(2)}, u32[]{:S(2)}) collective-permute-start(bf16[24,128]{1,0:T(8,128)(2,1)S(1)} %bitcast.104), channel_id=1, source_target_pairs={{48,0},{96,48},{144,96},{192,144},{240,192},{288,240},{336,288},{3... | collective-permute-start | bytes 18440 | tf_op jit(solution)/shard_map/ppermute | solution.py:155
  90.1 0.7 broadcast_in_dim.106
  90.8 10.4 %all-to-all-start.2 = ((f32[8,57,128]{2,1,0:T(8,128)}), f32[8,57,128]{2,1,0:T(8,128)S(1)}, u32[]{:S(2)}, u32[]{:S(2)}) async-start(f32[8,57,128]{2,1,0:T(8,128)} %broadcast_in_dim.106), calls=%async_computation.2 | async-start | bytes 524288 | tf_op jit(solution)/shard_map/all_to_all | solution.py:95
  101.4 10.5 %all-to-all-done.2 = f32[8,57,128]{2,1,0:T(8,128)S(1)} async-done(((f32[8,57,128]{2,1,0:T(8,128)}), f32[8,57,128]{2,1,0:T(8,128)S(1)}, u32[]{:S(2)}, u32[]{:S(2)}) %all-to-all-start.2) | async-done | bytes 233504 | tf_op jit(solution)/shard_map/all_to_all | solution.py:95
  111.9 0.7 broadcast_in_dim.107
  112.6 8.6 %all-to-all-start.3 = ((f32[6,57,128]{2,1,0:T(8,128)}), f32[6,57,128]{2,1,0:T(8,128)S(1)}, u32[]{:S(2)}, u32[]{:S(2)}) async-start(f32[6,57,128]{2,1,0:T(8,128)} %broadcast_in_dim.107), calls=%async_computation.3 | async-start | bytes 393216 | tf_op jit(solution)/shard_map/all_to_all | solution.py:95
  121.4 0.7 add_convert_fusion
  122.1 9.6 %all-to-all-done.3 = f32[6,57,128]{2,1,0:T(8,128)S(1)} async-done(((f32[6,57,128]{2,1,0:T(8,128)}), f32[6,57,128]{2,1,0:T(8,128)S(1)}, u32[]{:S(2)}, u32[]{:S(2)}) %all-to-all-start.3) | async-done | bytes 175136 | tf_op jit(solution)/shard_map/all_to_all | solution.py:95
  131.7 0.6 slice.252
  132.3 0.6 fusion.59
  132.9 0.6 slice.250
  133.5 0.6 reshape_squeeze.7
  (90 shorter events, 1.8 us)
Async XLA Ops:
  0.6 22.9 %copy-start.3 = (bf16[24,24,128]{2,1,0:T(8,128)(2,1)S(1)}, bf16[24,24,128]{2,1,0:T(8,128)(2,1)}, u32[]{:S(2)}) copy-start(bf16[24,24,128]{2,1,0:T(8,128)(2,1)} %param.20) | copy-start | bytes 442372
  0.6 29.4 %copy-start.7 = (s32[1024]{0:T(1024)S(1)}, s32[1024]{0:T(1024)}, u32[]{:S(2)}) copy-start(s32[1024]{0:T(1024)} %param.22) | copy-start | bytes 12292
  0.7 29.4 %copy-start.6 = (s32[1024]{0:T(1024)S(1)}, s32[1024]{0:T(1024)}, u32[]{:S(2)}) copy-start(s32[1024]{0:T(1024)} %param.23) | copy-start | bytes 12292
  5.1 27.1 %copy-start.4 = (bf16[1024,128]{1,0:T(8,128)(2,1)S(1)}, bf16[1024,128]{1,0:T(8,128)(2,1)}, u32[]{:S(2)}) copy-start(bf16[1024,128]{1,0:T(8,128)(2,1)} %param.21) | copy-start | bytes 786436
  5.9 26.4 %copy-start.5 = (bf16[1024,128]{1,0:T(8,128)(2,1)S(1)}, bf16[1024,128]{1,0:T(8,128)(2,1)}, u32[]{:S(2)}) copy-start(bf16[1024,128]{1,0:T(8,128)(2,1)} %param.31) | copy-start | bytes 786436
  5.9 31.0 %all-to-all-start = ((bf16[16,81,128]{2,1,0:T(8,128)(2,1)}), bf16[16,81,128]{2,1,0:T(8,128)(2,1)S(1)}, u32[]{:S(2)}, u32[]{:S(2)}) async-start(bf16[16,81,128]{2,1,0:T(8,128)(2,1)} %pad_maximum_fusion.1), calls=%async_computation | async-start | bytes 720896 | tf_op jit(solution)/shard_map/all_to_all | solution.py:111
  23.6 9.0 %collective-permute-start.1 = (bf16[24,128]{1,0:T(8,128)(2,1)S(1)}, bf16[24,128]{1,0:T(8,128)(2,1)S(1)}, u32[]{:S(2)}, u32[]{:S(2)}) collective-permute-start(bf16[24,128]{1,0:T(8,128)(2,1)S(1)} %bitcast.100), channel_id=1, source_target_pairs={{1,0},{2,1},{3,2},{4,3},{5,4},{6,5},{7,6},{8,7},{9,8},{10,9},{11,1... | collective-permute-start | bytes 18440 | tf_op jit(solution)/shard_map/ppermute | solution.py:155
  24.9 7.7 %collective-permute-start = (bf16[24,128]{1,0:T(8,128)(2,1)S(1)}, bf16[24,128]{1,0:T(8,128)(2,1)S(1)}, u32[]{:S(2)}, u32[]{:S(2)}) collective-permute-start(bf16[24,128]{1,0:T(8,128)(2,1)S(1)} %bitcast.102), channel_id=1, source_target_pairs={{0,1},{1,2},{2,3},{3,4},{4,5},{5,6},{6,7},{7,8},{8,9},{9,10},{10,1... | collective-permute-start | bytes 18440 | tf_op jit(solution)/shard_map/ppermute | solution.py:155
  37.2 2.0 %copy-start = (bf16[24,24,128]{2,1,0:T(8,128)(2,1)S(1)}, bf16[24,24,128]{2,1,0:T(8,128)(2,1)}, u32[]{:S(2)}) copy-start(bf16[24,24,128]{2,1,0:T(8,128)(2,1)} %param.30) | copy-start | bytes 442372
  38.9 1.2 copy-start.8
  45.1 2.1 %copy-start.1 = (f32[576,256]{1,0:T(8,128)}, f32[576,256]{1,0:T(8,128)S(1)}, u32[]{:S(2)}) copy-start(f32[576,256]{1,0:T(8,128)S(1)} %fusion.63) | copy-start | bytes 1769476
  47.0 1.0 copy-start.9
  54.6 35.4 %all-to-all-start.1 = ((f32[16,57,128]{2,1,0:T(8,128)}), f32[16,57,128]{2,1,0:T(8,128)S(1)}, u32[]{:S(2)}, u32[]{:S(2)}) async-start(f32[16,57,128]{2,1,0:T(8,128)} %dynamic-update-slice.16), calls=%async_computation.1 | async-start | bytes 1048576 | tf_op jit(solution)/shard_map/all_to_all | solution.py:87
  70.4 2.4 %copy-start.2 = (f32[576,256]{1,0:T(8,128)S(1)}, f32[576,256]{1,0:T(8,128)}, u32[]{:S(2)}) copy-start(f32[576,256]{1,0:T(8,128)} %copy-done.1) | copy-start | bytes 1769476
  70.7 19.3 %collective-permute-start.2 = (bf16[24,128]{1,0:T(8,128)(2,1)S(1)}, bf16[24,128]{1,0:T(8,128)(2,1)S(1)}, u32[]{:S(2)}, u32[]{:S(2)}) collective-permute-start(bf16[24,128]{1,0:T(8,128)(2,1)S(1)} %bitcast.105), channel_id=1, source_target_pairs={{0,48},{48,96},{96,144},{144,192},{192,240},{240,288},{288,336},{3... | collective-permute-start | bytes 18440 | tf_op jit(solution)/shard_map/ppermute | solution.py:155
  74.0 47.3 %collective-permute-start.5 = (bf16[24,128]{1,0:T(8,128)(2,1)S(1)}, bf16[24,128]{1,0:T(8,128)(2,1)S(1)}, u32[]{:S(2)}, u32[]{:S(2)}) collective-permute-start(bf16[24,128]{1,0:T(8,128)(2,1)S(1)} %get-tuple-element.100), channel_id=1, source_target_pairs={{1,0},{2,1},{3,2},{4,3},{5,4},{6,5},{7,6},{8,7},{9,8},{10,9},{11,1... | collective-permute-start | bytes 18440 | tf_op jit(solution)/shard_map/ppermute | solution.py:155
  75.3 45.9 %collective-permute-start.4 = (bf16[24,128]{1,0:T(8,128)(2,1)S(1)}, bf16[24,128]{1,0:T(8,128)(2,1)S(1)}, u32[]{:S(2)}, u32[]{:S(2)}) collective-permute-start(bf16[24,128]{1,0:T(8,128)(2,1)S(1)} %get-tuple-element.101), channel_id=1, source_target_pairs={{0,1},{1,2},{2,3},{3,4},{4,5},{5,6},{6,7},{7,8},{8,9},{9,10},{10,1... | collective-permute-start | bytes 18440 | tf_op jit(solution)/shard_map/ppermute | solution.py:155
  79.8 21.5 %collective-permute-start.3 = (bf16[24,128]{1,0:T(8,128)(2,1)S(1)}, bf16[24,128]{1,0:T(8,128)(2,1)S(1)}, u32[]{:S(2)}, u32[]{:S(2)}) collective-permute-start(bf16[24,128]{1,0:T(8,128)(2,1)S(1)} %bitcast.104), channel_id=1, source_target_pairs={{48,0},{96,48},{144,96},{192,144},{240,192},{288,240},{336,288},{3... | collective-permute-start | bytes 18440 | tf_op jit(solution)/shard_map/ppermute | solution.py:155
  90.8 21.1 %all-to-all-start.2 = ((f32[8,57,128]{2,1,0:T(8,128)}), f32[8,57,128]{2,1,0:T(8,128)S(1)}, u32[]{:S(2)}, u32[]{:S(2)}) async-start(f32[8,57,128]{2,1,0:T(8,128)} %broadcast_in_dim.106), calls=%async_computation.2 | async-start | bytes 524288 | tf_op jit(solution)/shard_map/all_to_all | solution.py:95
  112.6 19.1 %all-to-all-start.3 = ((f32[6,57,128]{2,1,0:T(8,128)}), f32[6,57,128]{2,1,0:T(8,128)S(1)}, u32[]{:S(2)}, u32[]{:S(2)}) async-start(f32[6,57,128]{2,1,0:T(8,128)} %broadcast_in_dim.107), calls=%async_computation.3 | async-start | bytes 393216 | tf_op jit(solution)/shard_map/all_to_all | solution.py:95

commit v12 on v11

--- a/solution.py
+++ b/solution.py
@@ -89,7 +89,7 @@
 
 def sum_sub(value):
     total = value
-    for axis in reversed(SUB):
+    for axis in SUB:
         count = lax.axis_size(axis)
         spread = jnp.broadcast_to(total[None], (count,) + total.shape)
         total = jnp.sum(lax.all_to_all(spread, axis, 0, 0, tiled=True), axis=0)

time: 135 us -> 135 us (level)
  no operation moved by 1% of the time
where the time goes in v12:
time: 135 us; the launch traced here: 134 us
  starting transfers between devices  67.3 us (50%)
  waiting for transfers between devices  25.3 us (19%)
  matrix products  17.4 us (13%)
  local copies, waits for them, and re-layouts  16.7 us (12%)
  other arithmetic  5.5 us (4%)
  between operations  2.03 us (2%)
    ppermute x6, starting transfers between devices, shift_in(): lax.ppermute(value.astype(jnp.bfloat16), axis, pairs).astype(value.dtype)  23.9 us
    all_to_all x2, waiting for transfers between devices, sum_sub(): total = jnp.sum(lax.all_to_all(spread, axis, 0, 0, tiled=True), axis=0)  20.9 us
    all_to_all x2, starting transfers between devices, sum_sub(): total = jnp.sum(lax.all_to_all(spread, axis, 0, 0, tiled=True), axis=0)  18.1 us
    all_to_all x1, starting transfers between devices, gather_params(): received = lax.all_to_all(spread, 'dom', 0, 0, tiled=True)  17.6 us
    dot_general x2, matrix products, sum_rows(): lax.dot_general(pick.astype(jnp.float32), values, (((0,), (0,)), ((), ())...  8.44 us
    all_to_all x1, starting transfers between devices, reduce_scatter_dom(): return jnp.sum(lax.all_to_all(packed, 'dom', 0, 0, tiled=True), axis=0)  7.72 us
    unnamed x35, local copies, waits for them, and re-layouts  6.99 us
    all_to_all x1, waiting for transfers between devices, gather_params(): received = lax.all_to_all(spread, 'dom', 0, 0, tiled=True)  4.35 us
  transfers between devices with their start and end apart: 10, of which 3 were waited for; matrix products, arithmetic and copies ran while one was open for 11% of the time, Pallas kernels for 0%

profile of v12, /device:TPU:6, one launch (start us, length us, event | category | flops | bytes accessed | tf_op | source)
XLA Modules:
  0.0 134.2 jit_solution(3056186104251286436)
XLA Ops:
  0.7 0.8 reshape.289
  1.5 0.7 slice_bitcast_fusion.9
  2.2 0.7 constant_dynamic-update-slice_fusion.4
  2.9 0.7 constant_dynamic-update-slice_fusion.3
  3.6 0.7 constant_dynamic-update-slice_fusion.2
  4.3 0.7 constant_dynamic-update-slice_fusion.1
  5.0 0.1 select_select_fusion
  5.1 0.8 pad_maximum_fusion.1
  5.9 17.6 %all-to-all-start = ((bf16[16,81,128]{2,1,0:T(8,128)(2,1)}), bf16[16,81,128]{2,1,0:T(8,128)(2,1)S(1)}, u32[]{:S(2)}, u32[]{:S(2)}) async-start(bf16[16,81,128]{2,1,0:T(8,128)(2,1)} %pad_maximum_fusion.1), calls=%async_computation | async-start | bytes 720896 | tf_op jit(solution)/shard_map/all_to_all | solution.py:111
  23.6 1.3 collective-permute-start.1
  24.9 4.5 %collective-permute-start = (bf16[24,128]{1,0:T(8,128)(2,1)S(1)}, bf16[24,128]{1,0:T(8,128)(2,1)S(1)}, u32[]{:S(2)}, u32[]{:S(2)}) collective-permute-start(bf16[24,128]{1,0:T(8,128)(2,1)S(1)} %bitcast.102), channel_id=1, source_target_pairs={{0,1},{1,2},{2,3},{3,4},{4,5},{5,6},{6,7},{7,8},{8,9},{9,10},{10,1... | collective-permute-start | bytes 18440 | tf_op jit(solution)/shard_map/ppermute | solution.py:155
  30.1 2.1 %iota_compare_fusion = (pred[1024,676]{1,0:T(32,128)(4,1)}, pred[1024,676]{1,0:T(32,128)(4,1)}) fusion(s32[1024]{0:T(1024)S(1)} %get-tuple-element.115, s32[1024]{0:T(1024)S(1)} %get-tuple-element.114), kind=kLoop, calls=%fused_computation.4 | loop fusion | flops 1384448 | bytes 1392640 | tf_op jit(solution)/shard_map/eq | solution.py:159
  32.2 0.1 copy.98
  32.4 0.1 copy.102
  32.6 4.3 %all-to-all-done = bf16[16,81,128]{2,1,0:T(8,128)(2,1)S(1)} async-done(((bf16[16,81,128]{2,1,0:T(8,128)(2,1)}), bf16[16,81,128]{2,1,0:T(8,128)(2,1)S(1)}, u32[]{:S(2)}, u32[]{:S(2)}) %all-to-all-start) | async-done | bytes 331808 | tf_op jit(solution)/shard_map/all_to_all | solution.py:111
  37.0 0.1 pad_maximum_fusion.5
  37.2 0.8 convolution_convert_fusion
  38.0 0.8 convolution_convert_fusion.1
  39.1 0.1 reshape.308
  39.2 0.2 fusion.28
  39.6 0.4 fusion.26
  40.1 0.3 fusion.61
  40.5 1.7 %fusion.14 = bf16[576,128]{1,0:T(8,128)(2,1)S(1)} fusion(s32[1024]{0:T(1024)S(1)} %copy-done.7, f32[1024,128]{0,1:T(8,128)S(1)} %get-tuple-element.117, f32[1024]{0:T(1024)S(1)} %fusion.45, f32[128]{0:T(128)S(1)} %reshape.307, f32[1024]{0:T(1024)S(1)} %add_rsqrt_fusion.1, f32[1024]{0:T(1024)S(1)} %broadcast_multiply_fusion.6), kind=kOutput, calls=%fused_computation.20 | convolution fusion | flops 907747328 | bytes 688640 | tf_op jit(solution)/shard_map/dot_general | solution.py:171
  42.2 0.2 fusion.35
  42.4 0.3 fusion.62
  42.7 0.3 multiply_reduce_fusion.5
  43.0 0.4 fusion.29
  43.4 0.4 multiply_convert_fusion.1
  43.8 0.2 fusion.13
  44.0 1.0 fusion.34
  44.9 0.2 fusion.63
  45.2 1.9 %multiply_reduce_fusion = (f32[128]{0:T(128)S(1)}, f32[1024]{0:T(1024)S(1)}, f32[1024]{0:T(1024)S(1)}, f32[1024,128]{0,1:T(8,128)S(1)}) fusion(f32[1024,128]{0,1:T(8,128)S(1)} %get-tuple-element.117, f32[1024]{0:T(1024)S(1)} %add_rsqrt_fusion.1, f32[1024]{0:T(1024)S(1)} %broadcast_multiply_fusion.6, f32[128]{0:T(128)S(1)} %reshape.307, ...), kind=kOutput, calls=%fused_computation.31 | convolution fusion | flops 907999104 | bytes 1631232 | tf_op jit(solution)/shard_map/dot_general | solution.py:165
  47.1 0.2 multiply_convert_fusion
  47.2 0.3 fusion.12
  47.5 0.5 copy-done.9
  48.0 0.4 fusion.25
  48.4 0.4 fusion.64
  49.1 0.7 constant_dynamic-update-slice_fusion.6
  49.8 0.9 fusion.18
  50.7 1.6 %constant_dynamic-update-slice_fusion.5 = f32[16,57,128]{2,1,0:T(8,128)} fusion(f32[16,57,128]{2,1,0:T(8,128)} %fusion.18, f32[16,16,128]{2,1,0:T(8,128)} %bitcast.93), kind=kLoop, calls=%fused_computation.79 | loop fusion | bytes 262144
  52.3 0.9 fusion.17
  53.1 1.5 %dynamic-update-slice.16 = f32[16,57,128]{2,1,0:T(8,128)} dynamic-update-slice(f32[16,57,128]{2,1,0:T(8,128)} %fusion.17, f32[16,1,128]{2,1,0:T(1,128)S(1)} %pad.22.clone, s32[]{} %constant.208, s32[]{} %constant.212, s32[]{} %constant.208) | dynamic-update-slice | bytes 16388 | tf_op jit(solution)/shard_map/concatenate | solution.py:136
  54.6 7.7 %all-to-all-start.1 = ((f32[16,57,128]{2,1,0:T(8,128)}), f32[16,57,128]{2,1,0:T(8,128)S(1)}, u32[]{:S(2)}, u32[]{:S(2)}) async-start(f32[16,57,128]{2,1,0:T(8,128)} %dynamic-update-slice.16), calls=%async_computation.1 | async-start | bytes 1048576 | tf_op jit(solution)/shard_map/all_to_all | solution.py:87
  62.4 1.1 fusion.56
  63.5 0.2 copy.120
  63.7 6.7 %fusion = f32[676,128]{1,0:T(8,128)S(1)} fusion(pred[1024,676]{1,0:T(32,128)(4,1)} %get-tuple-element.123, pred[1024,676]{1,0:T(32,128)(4,1)} %get-tuple-element.124, f32[1024,128]{1,0:T(8,128)} %get-tuple-element.96, f32[1024,128]{1,0:T(8,128)} %get-tuple-element.97), kind=kOutput, calls=%fused_computation | convolution fusion | flops 2128158720 | bytes 2779136 | tf_op jit(solution)/shard_map/dot_general | solution.py:171
  70.4 0.2 copy.127
  70.7 2.1 %collective-permute-start.2 = (bf16[24,128]{1,0:T(8,128)(2,1)S(1)}, bf16[24,128]{1,0:T(8,128)(2,1)S(1)}, u32[]{:S(2)}, u32[]{:S(2)}) collective-permute-start(bf16[24,128]{1,0:T(8,128)(2,1)S(1)} %bitcast.105), channel_id=1, source_target_pairs={{0,48},{48,96},{96,144},{144,192},{192,240},{240,288},{288,336},{3... | collective-permute-start | bytes 18440 | tf_op jit(solution)/shard_map/ppermute | solution.py:155
  72.9 0.2 copy.103
  73.1 0.8 copy.114
  74.0 1.3 collective-permute-start.5
  75.3 4.5 %collective-permute-start.4 = (bf16[24,128]{1,0:T(8,128)(2,1)S(1)}, bf16[24,128]{1,0:T(8,128)(2,1)S(1)}, u32[]{:S(2)}, u32[]{:S(2)}) collective-permute-start(bf16[24,128]{1,0:T(8,128)(2,1)S(1)} %get-tuple-element.101), channel_id=1, source_target_pairs={{0,1},{1,2},{2,3},{3,4},{4,5},{5,6},{6,7},{7,8},{8,9},{9,10},{10,1... | collective-permute-start | bytes 18440 | tf_op jit(solution)/shard_map/ppermute | solution.py:155
  79.8 10.2 %collective-permute-start.3 = (bf16[24,128]{1,0:T(8,128)(2,1)S(1)}, bf16[24,128]{1,0:T(8,128)(2,1)S(1)}, u32[]{:S(2)}, u32[]{:S(2)}) collective-permute-start(bf16[24,128]{1,0:T(8,128)(2,1)S(1)} %bitcast.104), channel_id=1, source_target_pairs={{48,0},{96,48},{144,96},{192,144},{240,192},{288,240},{336,288},{3... | collective-permute-start | bytes 18440 | tf_op jit(solution)/shard_map/ppermute | solution.py:155
  90.1 0.7 broadcast_in_dim.106
  90.8 13.7 %all-to-all-start.2 = ((f32[6,57,128]{2,1,0:T(8,128)}), f32[6,57,128]{2,1,0:T(8,128)S(1)}, u32[]{:S(2)}, u32[]{:S(2)}) async-start(f32[6,57,128]{2,1,0:T(8,128)} %broadcast_in_dim.106), calls=%async_computation.2 | async-start | bytes 393216 | tf_op jit(solution)/shard_map/all_to_all | solution.py:95
  104.7 11.3 %all-to-all-done.2 = f32[6,57,128]{2,1,0:T(8,128)S(1)} async-done(((f32[6,57,128]{2,1,0:T(8,128)}), f32[6,57,128]{2,1,0:T(8,128)S(1)}, u32[]{:S(2)}, u32[]{:S(2)}) %all-to-all-start.2) | async-done | bytes 175136 | tf_op jit(solution)/shard_map/all_to_all | solution.py:95
  116.0 0.7 broadcast_in_dim.107
  116.7 4.4 %all-to-all-start.3 = ((f32[8,57,128]{2,1,0:T(8,128)}), f32[8,57,128]{2,1,0:T(8,128)S(1)}, u32[]{:S(2)}, u32[]{:S(2)}) async-start(f32[8,57,128]{2,1,0:T(8,128)} %broadcast_in_dim.107), calls=%async_computation.3 | async-start | bytes 524288 | tf_op jit(solution)/shard_map/all_to_all | solution.py:95
  121.4 0.7 add_convert_fusion
  122.1 9.6 %all-to-all-done.3 = f32[8,57,128]{2,1,0:T(8,128)S(1)} async-done(((f32[8,57,128]{2,1,0:T(8,128)}), f32[8,57,128]{2,1,0:T(8,128)S(1)}, u32[]{:S(2)}, u32[]{:S(2)}) %all-to-all-start.3) | async-done | bytes 233504 | tf_op jit(solution)/shard_map/all_to_all | solution.py:95
  131.7 0.6 slice.252
  132.3 0.6 fusion.59
  132.9 0.6 slice.250
  133.5 0.6 reshape_squeeze.7
  (90 shorter events, 1.8 us)
Async XLA Ops:
  0.6 22.9 %copy-start.3 = (bf16[24,24,128]{2,1,0:T(8,128)(2,1)S(1)}, bf16[24,24,128]{2,1,0:T(8,128)(2,1)}, u32[]{:S(2)}) copy-start(bf16[24,24,128]{2,1,0:T(8,128)(2,1)} %param.20) | copy-start | bytes 442372
  0.6 29.4 %copy-start.7 = (s32[1024]{0:T(1024)S(1)}, s32[1024]{0:T(1024)}, u32[]{:S(2)}) copy-start(s32[1024]{0:T(1024)} %param.22) | copy-start | bytes 12292
  0.7 29.4 %copy-start.6 = (s32[1024]{0:T(1024)S(1)}, s32[1024]{0:T(1024)}, u32[]{:S(2)}) copy-start(s32[1024]{0:T(1024)} %param.23) | copy-start | bytes 12292
  5.1 27.1 %copy-start.4 = (bf16[1024,128]{1,0:T(8,128)(2,1)S(1)}, bf16[1024,128]{1,0:T(8,128)(2,1)}, u32[]{:S(2)}) copy-start(bf16[1024,128]{1,0:T(8,128)(2,1)} %param.21) | copy-start | bytes 786436
  5.9 26.4 %copy-start.5 = (bf16[1024,128]{1,0:T(8,128)(2,1)S(1)}, bf16[1024,128]{1,0:T(8,128)(2,1)}, u32[]{:S(2)}) copy-start(bf16[1024,128]{1,0:T(8,128)(2,1)} %param.31) | copy-start | bytes 786436
  5.9 31.0 %all-to-all-start = ((bf16[16,81,128]{2,1,0:T(8,128)(2,1)}), bf16[16,81,128]{2,1,0:T(8,128)(2,1)S(1)}, u32[]{:S(2)}, u32[]{:S(2)}) async-start(bf16[16,81,128]{2,1,0:T(8,128)(2,1)} %pad_maximum_fusion.1), calls=%async_computation | async-start | bytes 720896 | tf_op jit(solution)/shard_map/all_to_all | solution.py:111
  23.6 9.0 %collective-permute-start.1 = (bf16[24,128]{1,0:T(8,128)(2,1)S(1)}, bf16[24,128]{1,0:T(8,128)(2,1)S(1)}, u32[]{:S(2)}, u32[]{:S(2)}) collective-permute-start(bf16[24,128]{1,0:T(8,128)(2,1)S(1)} %bitcast.100), channel_id=1, source_target_pairs={{1,0},{2,1},{3,2},{4,3},{5,4},{6,5},{7,6},{8,7},{9,8},{10,9},{11,1... | collective-permute-start | bytes 18440 | tf_op jit(solution)/shard_map/ppermute | solution.py:155
  24.9 7.7 %collective-permute-start = (bf16[24,128]{1,0:T(8,128)(2,1)S(1)}, bf16[24,128]{1,0:T(8,128)(2,1)S(1)}, u32[]{:S(2)}, u32[]{:S(2)}) collective-permute-start(bf16[24,128]{1,0:T(8,128)(2,1)S(1)} %bitcast.102), channel_id=1, source_target_pairs={{0,1},{1,2},{2,3},{3,4},{4,5},{5,6},{6,7},{7,8},{8,9},{9,10},{10,1... | collective-permute-start | bytes 18440 | tf_op jit(solution)/shard_map/ppermute | solution.py:155
  37.2 2.0 %copy-start = (bf16[24,24,128]{2,1,0:T(8,128)(2,1)S(1)}, bf16[24,24,128]{2,1,0:T(8,128)(2,1)}, u32[]{:S(2)}) copy-start(bf16[24,24,128]{2,1,0:T(8,128)(2,1)} %param.30) | copy-start | bytes 442372
  38.9 1.2 copy-start.8
  45.1 2.1 %copy-start.1 = (f32[576,256]{1,0:T(8,128)}, f32[576,256]{1,0:T(8,128)S(1)}, u32[]{:S(2)}) copy-start(f32[576,256]{1,0:T(8,128)S(1)} %fusion.63) | copy-start | bytes 1769476
  47.0 1.0 copy-start.9
  54.6 35.4 %all-to-all-start.1 = ((f32[16,57,128]{2,1,0:T(8,128)}), f32[16,57,128]{2,1,0:T(8,128)S(1)}, u32[]{:S(2)}, u32[]{:S(2)}) async-start(f32[16,57,128]{2,1,0:T(8,128)} %dynamic-update-slice.16), calls=%async_computation.1 | async-start | bytes 1048576 | tf_op jit(solution)/shard_map/all_to_all | solution.py:87
  70.4 2.4 %copy-start.2 = (f32[576,256]{1,0:T(8,128)S(1)}, f32[576,256]{1,0:T(8,128)}, u32[]{:S(2)}) copy-start(f32[576,256]{1,0:T(8,128)} %copy-done.1) | copy-start | bytes 1769476
  70.7 19.3 %collective-permute-start.2 = (bf16[24,128]{1,0:T(8,128)(2,1)S(1)}, bf16[24,128]{1,0:T(8,128)(2,1)S(1)}, u32[]{:S(2)}, u32[]{:S(2)}) collective-permute-start(bf16[24,128]{1,0:T(8,128)(2,1)S(1)} %bitcast.105), channel_id=1, source_target_pairs={{0,48},{48,96},{96,144},{144,192},{192,240},{240,288},{288,336},{3... | collective-permute-start | bytes 18440 | tf_op jit(solution)/shard_map/ppermute | solution.py:155
  74.0 47.3 %collective-permute-start.5 = (bf16[24,128]{1,0:T(8,128)(2,1)S(1)}, bf16[24,128]{1,0:T(8,128)(2,1)S(1)}, u32[]{:S(2)}, u32[]{:S(2)}) collective-permute-start(bf16[24,128]{1,0:T(8,128)(2,1)S(1)} %get-tuple-element.100), channel_id=1, source_target_pairs={{1,0},{2,1},{3,2},{4,3},{5,4},{6,5},{7,6},{8,7},{9,8},{10,9},{11,1... | collective-permute-start | bytes 18440 | tf_op jit(solution)/shard_map/ppermute | solution.py:155
  75.3 45.9 %collective-permute-start.4 = (bf16[24,128]{1,0:T(8,128)(2,1)S(1)}, bf16[24,128]{1,0:T(8,128)(2,1)S(1)}, u32[]{:S(2)}, u32[]{:S(2)}) collective-permute-start(bf16[24,128]{1,0:T(8,128)(2,1)S(1)} %get-tuple-element.101), channel_id=1, source_target_pairs={{0,1},{1,2},{2,3},{3,4},{4,5},{5,6},{6,7},{7,8},{8,9},{9,10},{10,1... | collective-permute-start | bytes 18440 | tf_op jit(solution)/shard_map/ppermute | solution.py:155
  79.8 24.7 %collective-permute-start.3 = (bf16[24,128]{1,0:T(8,128)(2,1)S(1)}, bf16[24,128]{1,0:T(8,128)(2,1)S(1)}, u32[]{:S(2)}, u32[]{:S(2)}) collective-permute-start(bf16[24,128]{1,0:T(8,128)(2,1)S(1)} %bitcast.104), channel_id=1, source_target_pairs={{48,0},{96,48},{144,96},{192,144},{240,192},{288,240},{336,288},{3... | collective-permute-start | bytes 18440 | tf_op jit(solution)/shard_map/ppermute | solution.py:155
  90.8 25.3 %all-to-all-start.2 = ((f32[6,57,128]{2,1,0:T(8,128)}), f32[6,57,128]{2,1,0:T(8,128)S(1)}, u32[]{:S(2)}, u32[]{:S(2)}) async-start(f32[6,57,128]{2,1,0:T(8,128)} %broadcast_in_dim.106), calls=%async_computation.2 | async-start | bytes 393216 | tf_op jit(solution)/shard_map/all_to_all | solution.py:95
  116.7 14.9 %all-to-all-start.3 = ((f32[8,57,128]{2,1,0:T(8,128)}), f32[8,57,128]{2,1,0:T(8,128)S(1)}, u32[]{:S(2)}, u32[]{:S(2)}) async-start(f32[8,57,128]{2,1,0:T(8,128)} %broadcast_in_dim.107), calls=%async_computation.3 | async-start | bytes 524288 | tf_op jit(solution)/shard_map/all_to_all | solution.py:95
